TPU v7x, 512 devices: a whole 4x4x16 slice. The times are simulated.
512 devices in a mesh: lon: 32 (over z, core), lat: 16 (over x, y).
Axes of the slice: x: 4, y: 4, z: 16, core: 2. Of those that a mesh axis runs over, the one named last changes fastest.
Arguments:
- iterate: float32 [127, 16, 4096], P(None, 'lat', 'lon'), may hold values from -200 to 200
- residual: float32 [127, 16, 4096], P(None, 'lat', 'lon'), may hold values from -200 to 200
- direction: float32 [127, 16, 4096], P(None, 'lat', 'lon'), may hold values from -200 to 200
- obs_weight: float32 [127, 16, 4096], P(None, 'lat', 'lon'), may hold values from 0.5 to 5
- vertical: float32 [127, 127], replicated, may hold values from -0.2 to 1.2
- lon_taps: float32 [32, 101], replicated, may hold values from 0 to 1
- lat_taps: float32 [32, 101], replicated, may hold values from 0 to 1
- band_sizes: int32 [32], replicated, may hold values from 1 to 12, 127 in all
Outputs:
- iterate_next: float32 [127, 16, 4096], P(None, 'lat', 'lon')
- residual_next: float32 [127, 16, 4096], P(None, 'lat', 'lon')
- direction_next: float32 [127, 16, 4096], P(None, 'lat', 'lon')
Inputs may be any that keep to these rules, and one draw needn't show every extreme that they name: `band_sizes`: the bands sum to 127 levels and the largest holds exactly 12 levels.
All inputs are finite; a program needn't handle non-finite values.
Results may differ from a plain program's by a relative error of at most 0.000071.
Values sent between devices are 32-bit elements; how exact they have to be, the bound alone decides.
No kernel may reach another device: no remote copies, remote signals or barrier semaphores. Data moves between devices by JAX's collectives and lax.ppermute only.
A program may use at most 64 MiB of HBM per device.

v0:
```python
import jax
import jax.numpy as jnp
from jax import lax
from jax.sharding import PartitionSpec as P

LEV = 127
TAPS = 101
HALF = 50
GROUPS = 32


HIGHEST = lax.Precision.HIGHEST


def with_halo(cells, sides, width):
    for axis, dim in sides:
        count = lax.axis_size(axis)
        head = lax.slice_in_dim(cells, 0, width, axis=dim)
        tail = lax.slice_in_dim(cells, cells.shape[dim] - width, cells.shape[dim], axis=dim)
        cells = jnp.concatenate(
            [
                lax.ppermute(tail, axis, [(i, (i + 1) % count) for i in range(count)]),
                cells,
                lax.ppermute(head, axis, [((i + 1) % count, i) for i in range(count)]),
            ],
            axis=dim,
        )
    return cells


def band_matrices(kernel, width_in, width_out):
    offsets = (
        jnp.arange(width_in, dtype=jnp.int32)[:, None]
        - jnp.arange(width_out, dtype=jnp.int32)[None, :]
        + HALF
    )
    inside = (offsets >= 0) & (offsets < TAPS)
    picked = kernel[:, jnp.clip(offsets, 0, TAPS - 1)]
    return jnp.where(inside[None], picked, jnp.zeros_like(picked))


def group_rows(group_ids, kernel):
    onehot = (group_ids[:, None] == jnp.arange(GROUPS, dtype=jnp.int32)[None, :]).astype(
        jnp.float32
    )
    return jnp.dot(onehot, kernel, precision=HIGHEST)


def slot_plan(groups, devices_count):
    levels = jnp.arange(LEV, dtype=jnp.int32)
    capacity = (LEV + devices_count - 1) // devices_count
    slot_ids = jnp.arange(devices_count * capacity, dtype=jnp.int32)
    matched = levels[None, :] == slot_ids[:, None]
    occupied = jnp.any(matched, axis=1)
    sources = jnp.sum(jnp.where(matched, levels[None, :], 0), axis=1)
    sources = jnp.where(occupied, sources, LEV)
    slot_groups = jnp.sum(jnp.where(matched, groups[None, :], 0), axis=1)
    return (capacity, levels, sources, slot_groups)


def into_slots(grid_field, sources):
    padded = jnp.concatenate(
        [grid_field, jnp.zeros((1,) + grid_field.shape[1:], grid_field.dtype)], axis=0
    )
    return jnp.take(padded, sources, axis=0)


def lon_pass(grid_field, kernel_groups, groups, adjoint):
    kernel = kernel_groups[:, ::-1] if adjoint else kernel_groups
    lon_width = grid_field.shape[2]
    kernels = group_rows(groups, kernel)
    extended = with_halo(grid_field, (("lon", 2),), HALF)
    windows = jnp.stack(
        [extended[:, :, shift_tap : shift_tap + lon_width] for shift_tap in range(TAPS)], axis=2
    )
    return jnp.einsum("lakb,lk->lab", windows, kernels, precision=HIGHEST)


def lat_pass(grid_field, kernel_groups, groups, adjoint):
    kernel = kernel_groups[:, ::-1] if adjoint else kernel_groups
    devices_count = lax.axis_size("lat")
    capacity, position, sources, slot_groups = slot_plan(groups, devices_count)
    slotted = into_slots(grid_field, sources)
    own_groups = lax.dynamic_slice_in_dim(slot_groups, lax.axis_index("lat") * capacity, capacity)
    lat_width = grid_field.shape[1] * devices_count
    matrices = band_matrices(group_rows(own_groups, kernel), lat_width, lat_width)
    filtered = jnp.einsum(
        "sco,scx->sox",
        matrices,
        lax.all_to_all(slotted, "lat", split_axis=0, concat_axis=1, tiled=True),
        precision=HIGHEST,
    )
    returned = lax.all_to_all(filtered, "lat", split_axis=1, concat_axis=0, tiled=True)
    return jnp.take(returned, position, axis=0)


def vertical_mix(matrix, grid_field):
    return jnp.dot(matrix, grid_field.reshape(LEV, -1), precision=HIGHEST).reshape(grid_field.shape)


def local(iterate, residual, direction, obs_weight, vertical, lon_taps, lat_taps, band_sizes):
    bounds = jnp.cumsum(band_sizes)
    levels = jnp.arange(LEV, dtype=jnp.int32)
    groups = jnp.sum((levels[:, None] >= bounds[None, :]).astype(jnp.int32), axis=1)
    lon_part = lon_pass(direction, lon_taps, groups, False)
    lat_part = lat_pass(lon_part, lat_taps, groups, False)
    lifted = vertical_mix(vertical, lat_part)
    weighted = obs_weight * lifted
    back_vert = vertical_mix(vertical.T, weighted)
    back_lat = lat_pass(back_vert, lat_taps, groups, True)
    applied = direction + lon_pass(back_lat, lon_taps, groups, True)
    norm_old, curvature = lax.psum(
        (jnp.sum(residual * residual), jnp.sum(direction * applied)), ("lon", "lat")
    )
    step_length = norm_old / curvature
    residual_next = residual - step_length * applied
    norm_new = lax.psum(jnp.sum(residual_next * residual_next), ("lon", "lat"))
    iterate_next = iterate + step_length * direction
    direction_next = residual_next + norm_new / norm_old * direction
    return (iterate_next, residual_next, direction_next)


def solution(mesh):
    placed = (
        P(None, "lat", "lon"),
        P(None, "lat", "lon"),
        P(None, "lat", "lon"),
        P(None, "lat", "lon"),
        P(),
        P(),
        P(),
        P(),
    )
    return jax.shard_map(
        local,
        mesh=mesh,
        in_specs=placed,
        out_specs=(P(None, "lat", "lon"), P(None, "lat", "lon"), P(None, "lat", "lon")),
        check_vma=False,
    )
```

profile of v0, /device:TPU:1, one launch (start us, length us, event | category | flops | bytes accessed | tf_op | source)
XLA Modules:
  0.0 321.0 jit_solution(8003083662234558421)
XLA Ops:
  0.7 0.9 constant_dynamic-update-slice_fusion.1
  1.6 3.0 collective-permute-start
  4.7 3.9 %collective-permute-start.1 = (f32[127,1,50]{2,0,1:T(8,128)S(1)}, f32[127,1,50]{2,0,1:T(8,128)S(1)}, u32[]{:S(2)}, u32[]{:S(2)}) collective-permute-start(f32[127,1,50]{2,0,1:T(8,128)S(1)} %get-tuple-element.13), channel_id=1, source_target_pairs={{16,0},{32,16},{48,32},{64,48},{80,64},{96,80},{112,96},{128,112},... | collective-permute-start | bytes 76208 | tf_op jit(solution)/shard_map/ppermute | solution.py:24
  8.8 0.7 copy.65
  9.9 1.0 convolution_bitcast_fusion.3
  11.1 1.0 fusion.326
  12.1 0.8 rev.6
  13.0 0.7 gather_fusion.1
  13.9 0.9 copy.77
  24.5 9.6 %fusion.2 = f32[127,1,128]{2,1,0:T(1,128)S(1)} fusion(f32[127,101,1]{1,2,0:T(1,128)S(1)} %copy.85, f32[127,101,128]{2,0,1:T(8,128)S(1)} %bitcast.896), kind=kOutput, calls=%fused_computation.8 | convolution fusion | flops 19702272 | bytes 6683756 | tf_op jit(solution)/shard_map/lakb,lk->lab/dot_general | solution.py:76
  34.2 0.6 gather_fusion.2
  34.8 0.7 bitcast_select_fusion.4
  35.5 3.5 %all-to-all-start = ((f32[128,1,128]{2,1,0:T(1,128)}), f32[128,1,128]{2,1,0:T(1,128)S(1)}, u32[]{:S(2)}, u32[]{:S(2)}) async-start(f32[128,1,128]{2,1,0:T(1,128)} %bitcast.110), calls=%async_computation | async-start | bytes 131072 | tf_op jit(solution)/shard_map/all_to_all | solution.py:90
  39.0 6.4 %all-to-all-done = f32[128,1,128]{2,1,0:T(1,128)S(1)} async-done(((f32[128,1,128]{2,1,0:T(1,128)}), f32[128,1,128]{2,1,0:T(1,128)S(1)}, u32[]{:S(2)}, u32[]{:S(2)}) %all-to-all-start) | async-done | bytes 65568 | tf_op jit(solution)/shard_map/all_to_all | solution.py:90
  46.3 3.5 %all-to-all-start.1 = ((f32[8,16,128]{2,0,1:T(8,128)}), f32[8,16,128]{2,0,1:T(8,128)S(1)}, u32[]{:S(2)}, u32[]{:S(2)}) async-start(f32[8,16,128]{2,0,1:T(8,128)} %copy.76), calls=%async_computation.1 | async-start | bytes 131072 | tf_op jit(solution)/shard_map/all_to_all | solution.py:93
  49.8 6.4 %all-to-all-done.1 = f32[8,16,128]{2,0,1:T(8,128)S(1)} async-done(((f32[8,16,128]{2,0,1:T(8,128)}), f32[8,16,128]{2,0,1:T(8,128)S(1)}, u32[]{:S(2)}, u32[]{:S(2)}) %all-to-all-start.1) | async-done | bytes 65568 | tf_op jit(solution)/shard_map/all_to_all | solution.py:93
  57.6 0.6 gather_fusion.4
  58.2 0.7 bitcast_select_fusion.1
  59.0 3.5 %all-to-all-start.2 = ((f32[128,1,128]{2,1,0:T(1,128)}), f32[128,1,128]{2,1,0:T(1,128)S(1)}, u32[]{:S(2)}, u32[]{:S(2)}) async-start(f32[128,1,128]{2,1,0:T(1,128)} %bitcast.127), calls=%async_computation.2 | async-start | bytes 131072 | tf_op jit(solution)/shard_map/all_to_all | solution.py:90
  62.8 0.7 gather_fusion
  63.7 5.3 %all-to-all-done.2 = f32[128,1,128]{2,1,0:T(1,128)S(1)} async-done(((f32[128,1,128]{2,1,0:T(1,128)}), f32[128,1,128]{2,1,0:T(1,128)S(1)}, u32[]{:S(2)}, u32[]{:S(2)}) %all-to-all-start.2) | async-done | bytes 65568 | tf_op jit(solution)/shard_map/all_to_all | solution.py:90
  69.8 3.5 %all-to-all-start.3 = ((f32[8,16,128]{2,0,1:T(8,128)}), f32[8,16,128]{2,0,1:T(8,128)S(1)}, u32[]{:S(2)}, u32[]{:S(2)}) async-start(f32[8,16,128]{2,0,1:T(8,128)} %copy.81), calls=%async_computation.3 | async-start | bytes 131072 | tf_op jit(solution)/shard_map/all_to_all | solution.py:93
  73.3 0.7 multiply_reduce_fusion.2
  74.0 5.7 %all-to-all-done.3 = f32[8,16,128]{2,0,1:T(8,128)S(1)} async-done(((f32[8,16,128]{2,0,1:T(8,128)}), f32[8,16,128]{2,0,1:T(8,128)S(1)}, u32[]{:S(2)}, u32[]{:S(2)}) %all-to-all-start.3) | async-done | bytes 65568 | tf_op jit(solution)/shard_map/all_to_all | solution.py:93
  80.5 6.1 %collective-permute-start.2 = (f32[127,1,50]{2,0,1:T(8,128)S(1)}, f32[127,1,50]{2,0,1:T(8,128)S(1)}, u32[]{:S(2)}, u32[]{:S(2)}) collective-permute-start(f32[127,1,50]{2,0,1:T(8,128)S(1)} %get-tuple-element.12), channel_id=1, source_target_pairs={{0,16},{16,32},{32,48},{48,64},{64,80},{80,96},{96,112},{112,128},... | collective-permute-start | bytes 76208 | tf_op jit(solution)/shard_map/ppermute | solution.py:22
  87.0 5.8 %collective-permute-start.3 = (f32[127,1,50]{2,0,1:T(8,128)S(1)}, f32[127,1,50]{2,0,1:T(8,128)S(1)}, u32[]{:S(2)}, u32[]{:S(2)}) collective-permute-start(f32[127,1,50]{2,0,1:T(8,128)S(1)} %get-tuple-element.11), channel_id=1, source_target_pairs={{16,0},{32,16},{48,32},{64,48},{80,64},{96,80},{112,96},{128,112},... | collective-permute-start | bytes 76208 | tf_op jit(solution)/shard_map/ppermute | solution.py:24
  103.8 9.7 %fusion = f32[127,1,128]{2,1,0:T(1,128)S(1)} fusion(f32[127,101,1]{1,2,0:T(1,128)S(1)} %copy.88, f32[127,101,128]{2,0,1:T(8,128)S(1)} %bitcast.897), kind=kOutput, calls=%fused_computation.6 | convolution fusion | flops 19702272 | bytes 6683756 | tf_op jit(solution)/shard_map/lakb,lk->lab/dot_general | solution.py:76
  113.5 0.7 multiply_reduce_fusion.1
  114.2 102.2 %all-reduce.2 = (f32[]{:T(128)}, f32[]{:T(128)}) all-reduce(f32[]{:T(128)} %multiply_reduce_fusion.2, f32[]{:T(128)} %multiply_reduce_fusion.1), channel_id=1, replica_groups=mesh['lon'=32,'lat'=16] {'lon','lat'}, use_global_device_ids=true, to_apply=%region_1.2 | all-reduce | flops 2 | bytes 16 | tf_op jit(solution)/shard_map/psum | solution.py:112
  217.8 0.7 multiply_reduce_fusion
  218.5 100.4 %psum.23 = f32[]{:T(128)} all-reduce(f32[]{:T(128)} %get-tuple-element.7), channel_id=1, replica_groups=mesh['lon'=32,'lat'=16] {'lon','lat'}, use_global_device_ids=true, to_apply=%region_10.13 | all-reduce | flops 1 | bytes 8 | tf_op jit(solution)/shard_map/psum | solution.py:117
  320.2 0.8 multiply_add_fusion
  (257 shorter events, 25.2 us)
Async XLA Ops:
  0.6 56.3 %copy-start = (f32[127,127]{1,0:T(8,128)S(1)}, f32[127,127]{1,0:T(8,128)}, u32[]{:S(2)}) copy-start(f32[127,127]{1,0:T(8,128)} %param.16) | copy-start | bytes 193552
  0.6 19.5 %copy-start.1 = (f32[127,1,128]{2,1,0:T(1,128)S(1)}, f32[127,1,128]{2,1,0:T(1,128)}, u32[]{:S(2)}) copy-start(f32[127,1,128]{2,1,0:T(1,128)} %param.14) | copy-start | bytes 195076
  1.6 13.2 %collective-permute-start = (f32[127,1,50]{2,0,1:T(8,128)S(1)}, f32[127,1,50]{2,0,1:T(8,128)S(1)}, u32[]{:S(2)}, u32[]{:S(2)}) collective-permute-start(f32[127,1,50]{2,0,1:T(8,128)S(1)} %get-tuple-element.14), channel_id=1, source_target_pairs={{0,16},{16,32},{32,48},{48,64},{64,80},{80,96},{96,112},{112,128},... | collective-permute-start | bytes 76208 | tf_op jit(solution)/shard_map/ppermute | solution.py:22
  4.7 15.5 %collective-permute-start.1 = (f32[127,1,50]{2,0,1:T(8,128)S(1)}, f32[127,1,50]{2,0,1:T(8,128)S(1)}, u32[]{:S(2)}, u32[]{:S(2)}) collective-permute-start(f32[127,1,50]{2,0,1:T(8,128)S(1)} %get-tuple-element.13), channel_id=1, source_target_pairs={{16,0},{32,16},{48,32},{64,48},{80,64},{96,80},{112,96},{128,112},... | collective-permute-start | bytes 76208 | tf_op jit(solution)/shard_map/ppermute | solution.py:24
  22.8 39.9 %copy-start.4 = (f32[32,101]{1,0:T(8,128)S(1)}, f32[32,101]{1,0:T(8,128)}, u32[]{:S(2)}) copy-start(f32[32,101]{1,0:T(8,128)} %param.17) | copy-start | bytes 38788
  23.7 49.5 %copy-start.3 = (f32[127,1,128]{2,1,0:T(1,128)S(1)}, f32[127,1,128]{2,1,0:T(1,128)}, u32[]{:S(2)}) copy-start(f32[127,1,128]{2,1,0:T(1,128)} %param.13) | copy-start | bytes 195076
  35.5 10.0 %all-to-all-start = ((f32[128,1,128]{2,1,0:T(1,128)}), f32[128,1,128]{2,1,0:T(1,128)S(1)}, u32[]{:S(2)}, u32[]{:S(2)}) async-start(f32[128,1,128]{2,1,0:T(1,128)} %bitcast.110), calls=%async_computation | async-start | bytes 131072 | tf_op jit(solution)/shard_map/all_to_all | solution.py:90
  46.3 10.0 %all-to-all-start.1 = ((f32[8,16,128]{2,0,1:T(8,128)}), f32[8,16,128]{2,0,1:T(8,128)S(1)}, u32[]{:S(2)}, u32[]{:S(2)}) async-start(f32[8,16,128]{2,0,1:T(8,128)} %copy.76), calls=%async_computation.1 | async-start | bytes 131072 | tf_op jit(solution)/shard_map/all_to_all | solution.py:93
  59.0 10.0 %all-to-all-start.2 = ((f32[128,1,128]{2,1,0:T(1,128)}), f32[128,1,128]{2,1,0:T(1,128)S(1)}, u32[]{:S(2)}, u32[]{:S(2)}) async-start(f32[128,1,128]{2,1,0:T(1,128)} %bitcast.127), calls=%async_computation.2 | async-start | bytes 131072 | tf_op jit(solution)/shard_map/all_to_all | solution.py:90
  69.8 10.0 %all-to-all-start.3 = ((f32[8,16,128]{2,0,1:T(8,128)}), f32[8,16,128]{2,0,1:T(8,128)S(1)}, u32[]{:S(2)}, u32[]{:S(2)}) async-start(f32[8,16,128]{2,0,1:T(8,128)} %copy.81), calls=%async_computation.3 | async-start | bytes 131072 | tf_op jit(solution)/shard_map/all_to_all | solution.py:93
  80.5 12.6 %collective-permute-start.2 = (f32[127,1,50]{2,0,1:T(8,128)S(1)}, f32[127,1,50]{2,0,1:T(8,128)S(1)}, u32[]{:S(2)}, u32[]{:S(2)}) collective-permute-start(f32[127,1,50]{2,0,1:T(8,128)S(1)} %get-tuple-element.12), channel_id=1, source_target_pairs={{0,16},{16,32},{32,48},{48,64},{64,80},{80,96},{96,112},{112,128},... | collective-permute-start | bytes 76208 | tf_op jit(solution)/shard_map/ppermute | solution.py:22
  87.0 11.5 %collective-permute-start.3 = (f32[127,1,50]{2,0,1:T(8,128)S(1)}, f32[127,1,50]{2,0,1:T(8,128)S(1)}, u32[]{:S(2)}, u32[]{:S(2)}) collective-permute-start(f32[127,1,50]{2,0,1:T(8,128)S(1)} %get-tuple-element.11), channel_id=1, source_target_pairs={{16,0},{32,16},{48,32},{64,48},{80,64},{96,80},{112,96},{128,112},... | collective-permute-start | bytes 76208 | tf_op jit(solution)/shard_map/ppermute | solution.py:24
  100.6 219.6 %copy-start.5 = (f32[127,1,128]{2,1,0:T(1,128)S(1)}, f32[127,1,128]{2,1,0:T(1,128)}, u32[]{:S(2)}) copy-start(f32[127,1,128]{2,1,0:T(1,128)} %param.12) | copy-start | bytes 195076
  218.5 102.5 %copy-start.2 = (f32[127,1,128]{2,1,0:T(1,128)}, f32[127,1,128]{2,1,0:T(1,128)S(1)}, u32[]{:S(2)}) copy-start(f32[127,1,128]{2,1,0:T(1,128)S(1)} %get-tuple-element.8) | copy-start | bytes 195076
where the time goes:
time: 322 us; the launch traced here: 321 us
  blocking collectives  203 us (63%)
  starting transfers between devices  32.8 us (10%)
  waiting for transfers between devices  24.2 us (8%)
  matrix products  22.8 us (7%)
  other arithmetic  19.9 us (6%)
  local copies, waits for them, and re-layouts  14 us (4%)
  between operations  4.85 us (2%)
    psum x1, blocking collectives, local(): lax.psum((jnp.sum(residual * residual), jnp.sum(direction * applied)), ('...  102 us
    psum x1, blocking collectives, local(): norm_new = lax.psum(jnp.sum(residual_next * residual_next), ('lon', 'lat'))  100 us
    dot_general x2, matrix products, lon_pass(): return jnp.einsum('lakb,lk->lab', windows, kernels, precision=HIGHEST)  19.3 us
    unnamed x150, other arithmetic  14.6 us
    all_to_all x2, waiting for transfers between devices, lat_pass(): lax.all_to_all(filtered, 'lat', split_axis=1, concat_axis=0, tiled=True)  12.2 us
    all_to_all x2, waiting for transfers between devices, lat_pass(): lax.all_to_all(slotted, 'lat', split_axis=0, concat_axis=1, tiled=True)  11.7 us
    ppermute x2, starting transfers between devices, with_halo(): lax.ppermute(head, axis, [((i + 1) % count, i) for i in range(count)])  9.64 us
    ppermute x2, starting transfers between devices, with_halo(): lax.ppermute(tail, axis, [(i, (i + 1) % count) for i in range(count)])  9.14 us
  transfers between devices with their start and end apart: 8, of which 5 were waited for; matrix products, arithmetic and copies ran while one was open for 6% of the time, Pallas kernels for 0%

commit v1 on v0

--- a/solution.py
+++ b/solution.py
@@ -98,6 +98,15 @@
     return jnp.dot(matrix, grid_field.reshape(LEV, -1), precision=HIGHEST).reshape(grid_field.shape)
 
 
+def total(vals):
+    v = jnp.stack(vals)
+    for axis in ("lat", "lon"):
+        n = lax.axis_size(axis)
+        g = lax.all_to_all(jnp.broadcast_to(v[None], (n,) + v.shape), axis, 0, 0, tiled=True)
+        v = jnp.sum(g, axis=0)
+    return tuple(v[i] for i in range(len(vals)))
+
+
 def local(iterate, residual, direction, obs_weight, vertical, lon_taps, lat_taps, band_sizes):
     bounds = jnp.cumsum(band_sizes)
     levels = jnp.arange(LEV, dtype=jnp.int32)
@@ -109,12 +118,10 @@
     back_vert = vertical_mix(vertical.T, weighted)
     back_lat = lat_pass(back_vert, lat_taps, groups, True)
     applied = direction + lon_pass(back_lat, lon_taps, groups, True)
-    norm_old, curvature = lax.psum(
-        (jnp.sum(residual * residual), jnp.sum(direction * applied)), ("lon", "lat")
-    )
+    norm_old, curvature = total((jnp.sum(residual * residual), jnp.sum(direction * applied)))
     step_length = norm_old / curvature
     residual_next = residual - step_length * applied
-    norm_new = lax.psum(jnp.sum(residual_next * residual_next), ("lon", "lat"))
+    (norm_new,) = total((jnp.sum(residual_next * residual_next),))
     iterate_next = iterate + step_length * direction
     direction_next = residual_next + norm_new / norm_old * direction
     return (iterate_next, residual_next, direction_next)

time: 322 us -> 186 us (0.58)
  blocking collectives: 203 us -> 61.7 us
    psum x2 -> x0, blocking collectives: 203 us -> none  [the longest x1 102 us: local(): lax.psum((jnp.sum(residual * residual), jnp.sum(direction * applied)), ('...]
    all_to_all x0 -> x4, blocking collectives: none -> 61.7 us  [total(): lax.all_to_all(jnp.broadcast_to(v[None], (n,) + v.shape), axis, 0, 0, til...]
  transfers between devices with their start and end apart: 8 -> 8, of which waited for: 5 -> 5; matrix products, arithmetic and copies ran while one was open for 6% -> 10% of each run, Pallas kernels for 0% -> 0%
where the time goes in v1:
time: 186 us; the launch traced here: 185 us
  blocking collectives  61.7 us (33%)
  starting transfers between devices  32.8 us (18%)
  waiting for transfers between devices  24.2 us (13%)
  matrix products  22.8 us (12%)
  other arithmetic  22.6 us (12%)
  local copies, waits for them, and re-layouts  15.9 us (9%)
  between operations  4.87 us (3%)
    all_to_all x4, blocking collectives, total(): lax.all_to_all(jnp.broadcast_to(v[None], (n,) + v.shape), axis, 0, 0, til...  61.7 us
    dot_general x2, matrix products, lon_pass(): return jnp.einsum('lakb,lk->lab', windows, kernels, precision=HIGHEST)  19.3 us
    unnamed x150, other arithmetic  14.6 us
    all_to_all x2, waiting for transfers between devices, lat_pass(): lax.all_to_all(filtered, 'lat', split_axis=1, concat_axis=0, tiled=True)  12.2 us
    all_to_all x2, waiting for transfers between devices, lat_pass(): lax.all_to_all(slotted, 'lat', split_axis=0, concat_axis=1, tiled=True)  11.7 us
    ppermute x2, starting transfers between devices, with_halo(): lax.ppermute(head, axis, [((i + 1) % count, i) for i in range(count)])  9.64 us
    ppermute x2, starting transfers between devices, with_halo(): lax.ppermute(tail, axis, [(i, (i + 1) % count) for i in range(count)])  9.14 us
    all_to_all x2, starting transfers between devices, lat_pass(): lax.all_to_all(filtered, 'lat', split_axis=1, concat_axis=0, tiled=True)  6.99 us
  transfers between devices with their start and end apart: 8, of which 5 were waited for; matrix products, arithmetic and copies ran while one was open for 10% of the time, Pallas kernels for 0%

profile of v1, /device:TPU:1, one launch (start us, length us, event | category | flops | bytes accessed | tf_op | source)
XLA Modules:
  0.0 184.7 jit_solution(13500487327718206517)
XLA Ops:
  0.7 0.9 constant_dynamic-update-slice_fusion.1
  1.6 3.0 %collective-permute-start = (f32[127,1,50]{2,0,1:T(8,128)S(1)}, f32[127,1,50]{2,0,1:T(8,128)S(1)}, u32[]{:S(2)}, u32[]{:S(2)}) collective-permute-start(f32[127,1,50]{2,0,1:T(8,128)S(1)} %get-tuple-element.12), channel_id=1, source_target_pairs={{0,16},{16,32},{32,48},{48,64},{64,80},{80,96},{96,112},{112,128},... | collective-permute-start | bytes 76208 | tf_op jit(solution)/shard_map/ppermute | solution.py:22
  4.7 3.9 %collective-permute-start.1 = (f32[127,1,50]{2,0,1:T(8,128)S(1)}, f32[127,1,50]{2,0,1:T(8,128)S(1)}, u32[]{:S(2)}, u32[]{:S(2)}) collective-permute-start(f32[127,1,50]{2,0,1:T(8,128)S(1)} %get-tuple-element.11), channel_id=1, source_target_pairs={{16,0},{32,16},{48,32},{64,48},{80,64},{96,80},{112,96},{128,112},... | collective-permute-start | bytes 76208 | tf_op jit(solution)/shard_map/ppermute | solution.py:24
  8.8 0.7 copy.82
  9.9 1.0 convolution_bitcast_fusion.3
  11.1 1.0 fusion.326
  12.1 0.8 rev.6
  13.0 0.7 gather_fusion.1
  13.9 0.9 copy.94
  24.5 9.6 %fusion.2 = f32[127,1,128]{2,1,0:T(1,128)S(1)} fusion(f32[127,101,1]{1,2,0:T(1,128)S(1)} %copy.106, f32[127,101,128]{2,0,1:T(8,128)S(1)} %bitcast.900), kind=kOutput, calls=%fused_computation.8 | convolution fusion | flops 19702272 | bytes 6683756 | tf_op jit(solution)/shard_map/lakb,lk->lab/dot_general | solution.py:76
  34.8 0.7 bitcast_select_fusion.4
  35.5 3.5 %all-to-all-start = ((f32[128,1,128]{2,1,0:T(1,128)}), f32[128,1,128]{2,1,0:T(1,128)S(1)}, u32[]{:S(2)}, u32[]{:S(2)}) async-start(f32[128,1,128]{2,1,0:T(1,128)} %bitcast.111), calls=%async_computation | async-start | bytes 131072 | tf_op jit(solution)/shard_map/all_to_all | solution.py:90
  39.0 6.4 %all-to-all-done = f32[128,1,128]{2,1,0:T(1,128)S(1)} async-done(((f32[128,1,128]{2,1,0:T(1,128)}), f32[128,1,128]{2,1,0:T(1,128)S(1)}, u32[]{:S(2)}, u32[]{:S(2)}) %all-to-all-start) | async-done | bytes 65568 | tf_op jit(solution)/shard_map/all_to_all | solution.py:90
  46.3 3.5 %all-to-all-start.1 = ((f32[8,16,128]{2,0,1:T(8,128)}), f32[8,16,128]{2,0,1:T(8,128)S(1)}, u32[]{:S(2)}, u32[]{:S(2)}) async-start(f32[8,16,128]{2,0,1:T(8,128)} %copy.93), calls=%async_computation.1 | async-start | bytes 131072 | tf_op jit(solution)/shard_map/all_to_all | solution.py:93
  49.8 6.4 %all-to-all-done.1 = f32[8,16,128]{2,0,1:T(8,128)S(1)} async-done(((f32[8,16,128]{2,0,1:T(8,128)}), f32[8,16,128]{2,0,1:T(8,128)S(1)}, u32[]{:S(2)}, u32[]{:S(2)}) %all-to-all-start.1) | async-done | bytes 65568 | tf_op jit(solution)/shard_map/all_to_all | solution.py:93
  59.0 3.5 %all-to-all-start.2 = ((f32[128,1,128]{2,1,0:T(1,128)}), f32[128,1,128]{2,1,0:T(1,128)S(1)}, u32[]{:S(2)}, u32[]{:S(2)}) async-start(f32[128,1,128]{2,1,0:T(1,128)} %bitcast.128), calls=%async_computation.2 | async-start | bytes 131072 | tf_op jit(solution)/shard_map/all_to_all | solution.py:90
  62.8 0.7 gather_fusion
  63.7 5.3 %all-to-all-done.2 = f32[128,1,128]{2,1,0:T(1,128)S(1)} async-done(((f32[128,1,128]{2,1,0:T(1,128)}), f32[128,1,128]{2,1,0:T(1,128)S(1)}, u32[]{:S(2)}, u32[]{:S(2)}) %all-to-all-start.2) | async-done | bytes 65568 | tf_op jit(solution)/shard_map/all_to_all | solution.py:90
  69.8 3.5 %all-to-all-start.3 = ((f32[8,16,128]{2,0,1:T(8,128)}), f32[8,16,128]{2,0,1:T(8,128)S(1)}, u32[]{:S(2)}, u32[]{:S(2)}) async-start(f32[8,16,128]{2,0,1:T(8,128)} %copy.98), calls=%async_computation.3 | async-start | bytes 131072 | tf_op jit(solution)/shard_map/all_to_all | solution.py:93
  73.3 0.7 multiply_reduce_fusion.2
  74.0 5.7 %all-to-all-done.3 = f32[8,16,128]{2,0,1:T(8,128)S(1)} async-done(((f32[8,16,128]{2,0,1:T(8,128)}), f32[8,16,128]{2,0,1:T(8,128)S(1)}, u32[]{:S(2)}, u32[]{:S(2)}) %all-to-all-start.3) | async-done | bytes 65568 | tf_op jit(solution)/shard_map/all_to_all | solution.py:93
  80.5 6.1 %collective-permute-start.2 = (f32[127,1,50]{2,0,1:T(8,128)S(1)}, f32[127,1,50]{2,0,1:T(8,128)S(1)}, u32[]{:S(2)}, u32[]{:S(2)}) collective-permute-start(f32[127,1,50]{2,0,1:T(8,128)S(1)} %get-tuple-element.10), channel_id=1, source_target_pairs={{0,16},{16,32},{32,48},{48,64},{64,80},{80,96},{96,112},{112,128},... | collective-permute-start | bytes 76208 | tf_op jit(solution)/shard_map/ppermute | solution.py:22
  87.0 5.8 %collective-permute-start.3 = (f32[127,1,50]{2,0,1:T(8,128)S(1)}, f32[127,1,50]{2,0,1:T(8,128)S(1)}, u32[]{:S(2)}, u32[]{:S(2)}) collective-permute-start(f32[127,1,50]{2,0,1:T(8,128)S(1)} %get-tuple-element.9), channel_id=1, source_target_pairs={{16,0},{32,16},{48,32},{64,48},{80,64},{96,80},{112,96},{128,112},... | collective-permute-start | bytes 76208 | tf_op jit(solution)/shard_map/ppermute | solution.py:24
  103.8 9.7 %fusion = f32[127,1,128]{2,1,0:T(1,128)S(1)} fusion(f32[127,101,1]{1,2,0:T(1,128)S(1)} %copy.109, f32[127,101,128]{2,0,1:T(8,128)S(1)} %bitcast.901), kind=kOutput, calls=%fused_computation.6 | convolution fusion | flops 19702272 | bytes 6683756 | tf_op jit(solution)/shard_map/lakb,lk->lab/dot_general | solution.py:76
  113.5 0.7 multiply_reduce_fusion.1
  114.2 1.4 pad_maximum_fusion.3
  115.6 9.3 %all_to_all.96 = f32[16,1,2]{2,1,0:T(1,128)S(1)} all-to-all(f32[16,1,2]{2,1,0:T(1,128)S(1)} %broadcast_in_dim.113), channel_id=1, replica_groups=mesh['lon'=32,'lat'=16] {'lat'}, dimensions={0} | all-to-all | bytes 256 | tf_op jit(solution)/shard_map/all_to_all | solution.py:105
  125.0 26.4 %all_to_all.97 = f32[32,1,2]{2,1,0:T(1,128)S(1)} all-to-all(f32[32,1,2]{2,1,0:T(1,128)S(1)} %broadcast_in_dim.114), channel_id=1, replica_groups=mesh['lon'=32,'lat'=16] {'lon'}, dimensions={0} | all-to-all | bytes 512 | tf_op jit(solution)/shard_map/all_to_all | solution.py:105
  153.3 0.7 multiply_reduce_fusion
  154.7 9.1 %all_to_all.98 = f32[16,1,1]{2,1,0:T(1,128)S(1)} all-to-all(f32[16,1,1]{2,1,0:T(1,128)S(1)} %broadcast_in_dim.115), channel_id=1, replica_groups=mesh['lon'=32,'lat'=16] {'lat'}, dimensions={0} | all-to-all | bytes 128 | tf_op jit(solution)/shard_map/all_to_all | solution.py:105
  165.2 16.8 %all_to_all.99 = f32[32,1,1]{2,1,0:T(1,128)S(1)} all-to-all(f32[32,1,1]{2,1,0:T(1,128)S(1)} %broadcast_in_dim.116), channel_id=1, replica_groups=mesh['lon'=32,'lat'=16] {'lon'}, dimensions={0} | all-to-all | bytes 256 | tf_op jit(solution)/shard_map/all_to_all | solution.py:105
  184.0 0.8 multiply_add_fusion
  (269 shorter events, 30.4 us)
Async XLA Ops:
  0.6 56.3 %copy-start = (f32[127,127]{1,0:T(8,128)S(1)}, f32[127,127]{1,0:T(8,128)}, u32[]{:S(2)}) copy-start(f32[127,127]{1,0:T(8,128)} %param.16) | copy-start | bytes 193552
  0.6 19.5 %copy-start.1 = (f32[127,1,128]{2,1,0:T(1,128)S(1)}, f32[127,1,128]{2,1,0:T(1,128)}, u32[]{:S(2)}) copy-start(f32[127,1,128]{2,1,0:T(1,128)} %param.14) | copy-start | bytes 195076
  1.6 13.2 %collective-permute-start = (f32[127,1,50]{2,0,1:T(8,128)S(1)}, f32[127,1,50]{2,0,1:T(8,128)S(1)}, u32[]{:S(2)}, u32[]{:S(2)}) collective-permute-start(f32[127,1,50]{2,0,1:T(8,128)S(1)} %get-tuple-element.12), channel_id=1, source_target_pairs={{0,16},{16,32},{32,48},{48,64},{64,80},{80,96},{96,112},{112,128},... | collective-permute-start | bytes 76208 | tf_op jit(solution)/shard_map/ppermute | solution.py:22
  4.7 15.5 %collective-permute-start.1 = (f32[127,1,50]{2,0,1:T(8,128)S(1)}, f32[127,1,50]{2,0,1:T(8,128)S(1)}, u32[]{:S(2)}, u32[]{:S(2)}) collective-permute-start(f32[127,1,50]{2,0,1:T(8,128)S(1)} %get-tuple-element.11), channel_id=1, source_target_pairs={{16,0},{32,16},{48,32},{64,48},{80,64},{96,80},{112,96},{128,112},... | collective-permute-start | bytes 76208 | tf_op jit(solution)/shard_map/ppermute | solution.py:24
  22.8 39.9 %copy-start.4 = (f32[32,101]{1,0:T(8,128)S(1)}, f32[32,101]{1,0:T(8,128)}, u32[]{:S(2)}) copy-start(f32[32,101]{1,0:T(8,128)} %param.17) | copy-start | bytes 38788
  23.7 49.5 %copy-start.3 = (f32[127,1,128]{2,1,0:T(1,128)S(1)}, f32[127,1,128]{2,1,0:T(1,128)}, u32[]{:S(2)}) copy-start(f32[127,1,128]{2,1,0:T(1,128)} %param.13) | copy-start | bytes 195076
  35.5 10.0 %all-to-all-start = ((f32[128,1,128]{2,1,0:T(1,128)}), f32[128,1,128]{2,1,0:T(1,128)S(1)}, u32[]{:S(2)}, u32[]{:S(2)}) async-start(f32[128,1,128]{2,1,0:T(1,128)} %bitcast.111), calls=%async_computation | async-start | bytes 131072 | tf_op jit(solution)/shard_map/all_to_all | solution.py:90
  46.3 10.0 %all-to-all-start.1 = ((f32[8,16,128]{2,0,1:T(8,128)}), f32[8,16,128]{2,0,1:T(8,128)S(1)}, u32[]{:S(2)}, u32[]{:S(2)}) async-start(f32[8,16,128]{2,0,1:T(8,128)} %copy.93), calls=%async_computation.1 | async-start | bytes 131072 | tf_op jit(solution)/shard_map/all_to_all | solution.py:93
  59.0 10.0 %all-to-all-start.2 = ((f32[128,1,128]{2,1,0:T(1,128)}), f32[128,1,128]{2,1,0:T(1,128)S(1)}, u32[]{:S(2)}, u32[]{:S(2)}) async-start(f32[128,1,128]{2,1,0:T(1,128)} %bitcast.128), calls=%async_computation.2 | async-start | bytes 131072 | tf_op jit(solution)/shard_map/all_to_all | solution.py:90
  69.8 10.0 %all-to-all-start.3 = ((f32[8,16,128]{2,0,1:T(8,128)}), f32[8,16,128]{2,0,1:T(8,128)S(1)}, u32[]{:S(2)}, u32[]{:S(2)}) async-start(f32[8,16,128]{2,0,1:T(8,128)} %copy.98), calls=%async_computation.3 | async-start | bytes 131072 | tf_op jit(solution)/shard_map/all_to_all | solution.py:93
  80.5 12.6 %collective-permute-start.2 = (f32[127,1,50]{2,0,1:T(8,128)S(1)}, f32[127,1,50]{2,0,1:T(8,128)S(1)}, u32[]{:S(2)}, u32[]{:S(2)}) collective-permute-start(f32[127,1,50]{2,0,1:T(8,128)S(1)} %get-tuple-element.10), channel_id=1, source_target_pairs={{0,16},{16,32},{32,48},{48,64},{64,80},{80,96},{96,112},{112,128},... | collective-permute-start | bytes 76208 | tf_op jit(solution)/shard_map/ppermute | solution.py:22
  87.0 11.5 %collective-permute-start.3 = (f32[127,1,50]{2,0,1:T(8,128)S(1)}, f32[127,1,50]{2,0,1:T(8,128)S(1)}, u32[]{:S(2)}, u32[]{:S(2)}) collective-permute-start(f32[127,1,50]{2,0,1:T(8,128)S(1)} %get-tuple-element.9), channel_id=1, source_target_pairs={{16,0},{32,16},{48,32},{64,48},{80,64},{96,80},{112,96},{128,112},... | collective-permute-start | bytes 76208 | tf_op jit(solution)/shard_map/ppermute | solution.py:24
  100.8 83.1 %copy-start.5 = (f32[127,1,128]{2,1,0:T(1,128)S(1)}, f32[127,1,128]{2,1,0:T(1,128)}, u32[]{:S(2)}) copy-start(f32[127,1,128]{2,1,0:T(1,128)} %param.12) | copy-start | bytes 195076
  154.1 30.7 %copy-start.2 = (f32[127,1,128]{2,1,0:T(1,128)}, f32[127,1,128]{2,1,0:T(1,128)S(1)}, u32[]{:S(2)}) copy-start(f32[127,1,128]{2,1,0:T(1,128)S(1)} %get-tuple-element.6) | copy-start | bytes 195076

commit v2 on v1

--- a/solution.py
+++ b/solution.py
@@ -70,28 +70,25 @@
     lon_width = grid_field.shape[2]
     kernels = group_rows(groups, kernel)
     extended = with_halo(grid_field, (("lon", 2),), HALF)
-    windows = jnp.stack(
-        [extended[:, :, shift_tap : shift_tap + lon_width] for shift_tap in range(TAPS)], axis=2
-    )
-    return jnp.einsum("lakb,lk->lab", windows, kernels, precision=HIGHEST)
+    total_sum = kernels[:, None, 0:1] * extended[:, :, 0:lon_width]
+    for shift_tap in range(1, TAPS):
+        total_sum = total_sum + kernels[:, None, shift_tap : shift_tap + 1] * extended[
+            :, :, shift_tap : shift_tap + lon_width
+        ]
+    return total_sum
 
 
 def lat_pass(grid_field, kernel_groups, groups, adjoint):
     kernel = kernel_groups[:, ::-1] if adjoint else kernel_groups
-    devices_count = lax.axis_size("lat")
-    capacity, position, sources, slot_groups = slot_plan(groups, devices_count)
-    slotted = into_slots(grid_field, sources)
-    own_groups = lax.dynamic_slice_in_dim(slot_groups, lax.axis_index("lat") * capacity, capacity)
-    lat_width = grid_field.shape[1] * devices_count
-    matrices = band_matrices(group_rows(own_groups, kernel), lat_width, lat_width)
-    filtered = jnp.einsum(
-        "sco,scx->sox",
-        matrices,
-        lax.all_to_all(slotted, "lat", split_axis=0, concat_axis=1, tiled=True),
-        precision=HIGHEST,
-    )
-    returned = lax.all_to_all(filtered, "lat", split_axis=1, concat_axis=0, tiled=True)
-    return jnp.take(returned, position, axis=0)
+    rows = grid_field.shape[1]
+    full = lax.all_gather(grid_field, "lat", axis=1, tiled=True)
+    lat_width = full.shape[1]
+    own = lax.axis_index("lat") * rows + jnp.arange(rows, dtype=jnp.int32)
+    offsets = jnp.arange(lat_width, dtype=jnp.int32)[:, None] - own[None, :] + HALF
+    inside = (offsets >= 0) & (offsets < TAPS)
+    picked = group_rows(groups, kernel)[:, jnp.clip(offsets, 0, TAPS - 1)]
+    matrices = jnp.where(inside[None], picked, jnp.zeros_like(picked))
+    return jnp.sum(matrices[:, :, :, None] * full[:, :, None, :], axis=1)
 
 
 def vertical_mix(matrix, grid_field):

time: 186 us -> 147 us (0.79)
  matrix products: 22.8 us -> 1.61 us
  other arithmetic: 22.6 us -> 11.4 us
  starting transfers between devices: 32.8 us -> 40.2 us
  local copies, waits for them, and re-layouts: 15.9 us -> 10.2 us
  blocking collectives: 61.7 us -> 56.7 us
    all_to_all x4 -> x2, blocking collectives: 61.7 us -> 19.5 us  [total(): lax.all_to_all(jnp.broadcast_to(v[None], (n,) + v.shape), axis, 0, 0, til...]
    all_gather x0 -> x2, blocking collectives: none -> 37.2 us  [lat_pass(): full = lax.all_gather(grid_field, 'lat', axis=1, tiled=True)]
    dot_general x4 -> x0, matrix products: 19.7 us -> none  [the longest x2 19.3 us: lon_pass(): return jnp.einsum('lakb,lk->lab', windows, kernels, precision=HIGHEST)]
    unnamed x150 -> x0, other arithmetic: 14.6 us -> none
    add x0 -> x1, other arithmetic: none -> 4.75 us  [lon_pass(): total_sum + kernels[:, None, shift_tap:shift_tap + 1] * extended[:, :, sh...]
    ppermute x2, starting transfers between devices: 9.64 us -> 13.9 us  [with_halo(): lax.ppermute(head, axis, [((i + 1) % count, i) for i in range(count)])]
    all_to_all x4 -> x2, starting transfers between devices: 14 us -> 17.8 us  [total(): lax.all_to_all(jnp.broadcast_to(v[None], (n,) + v.shape), axis, 0, 0, til...]
    gather x8 -> x2, local copies, waits for them, and re-layouts: 4.29 us -> 1.12 us  [lat_pass(): picked = group_rows(groups, kernel)[:, jnp.clip(offsets, 0, TAPS - 1)]]
  transfers between devices with their start and end apart: 8 -> 6, of which waited for: 5 -> 2; matrix products, arithmetic and copies ran while one was open for 10% -> 3% of each run, Pallas kernels for 0% -> 0%
where the time goes in v2:
time: 147 us; the launch traced here: 146 us
  blocking collectives  56.7 us (39%)
  starting transfers between devices  40.2 us (27%)
  waiting for transfers between devices  22.6 us (15%)
  other arithmetic  11.4 us (8%)
  local copies, waits for them, and re-layouts  10.2 us (7%)
  between operations  3.67 us (2%)
  matrix products  1.61 us (1%)
    all_gather x2, blocking collectives, lat_pass(): full = lax.all_gather(grid_field, 'lat', axis=1, tiled=True)  37.2 us
    all_to_all x2, waiting for transfers between devices, total(): lax.all_to_all(jnp.broadcast_to(v[None], (n,) + v.shape), axis, 0, 0, til...  22.6 us
    all_to_all x2, blocking collectives, total(): lax.all_to_all(jnp.broadcast_to(v[None], (n,) + v.shape), axis, 0, 0, til...  19.5 us
    all_to_all x2, starting transfers between devices, total(): lax.all_to_all(jnp.broadcast_to(v[None], (n,) + v.shape), axis, 0, 0, til...  17.8 us
    ppermute x2, starting transfers between devices, with_halo(): lax.ppermute(head, axis, [((i + 1) % count, i) for i in range(count)])  13.9 us
    ppermute x2, starting transfers between devices, with_halo(): lax.ppermute(tail, axis, [(i, (i + 1) % count) for i in range(count)])  8.51 us
    unnamed x24, local copies, waits for them, and re-layouts  5.49 us
    add x1, other arithmetic, lon_pass(): total_sum + kernels[:, None, shift_tap:shift_tap + 1] * extended[:, :, sh...  4.75 us
  transfers between devices with their start and end apart: 6, of which 2 were waited for; matrix products, arithmetic and copies ran while one was open for 3% of the time, Pallas kernels for 0%

profile of v2, /device:TPU:1, one launch (start us, length us, event | category | flops | bytes accessed | tf_op | source)
XLA Modules:
  0.0 146.4 jit_solution(199378811069680016)
XLA Ops:
  0.6 0.9 fusion.512
  1.6 6.9 %collective-permute-start.1 = (f32[127,1,50]{2,0,1:T(8,128)S(1)}, f32[127,1,50]{2,0,1:T(8,128)S(1)}, u32[]{:S(2)}, u32[]{:S(2)}) collective-permute-start(f32[127,1,50]{2,0,1:T(8,128)S(1)} %get-tuple-element.21), channel_id=1, source_target_pairs={{16,0},{32,16},{48,32},{64,48},{80,64},{96,80},{112,96},{128,112},... | collective-permute-start | bytes 76208 | tf_op jit(solution)/shard_map/ppermute | solution.py:24
  8.5 0.7 copy-done.7
  9.5 0.5 copy-done.4
  10.4 0.7 copy-done.3
  12.3 0.6 gather_fusion
  12.8 0.6 gather_fusion.1
  13.8 4.7 %fusion.467 = f32[127,1,128]{2,0,1:T(8,128)S(1)} fusion(f32[127,1,178]{2,0,1:T(8,128)S(1)} %constant_dynamic-update-slice_fusion, f32[127,1,128]{2,0,1:T(8,128)S(1)} %get-tuple-element.22, f32[127,1,50]{2,0,1:T(8,128)S(1)} %collective-permute-done, f32[127]{0:T(128)S(1)} %get-tuple-element.126, f32[127]{0:T(128)S(1)} %get-tuple-element.127, ...), kind=kLoop, calls=%fused_computation.770 | loop fusion | flops 4080256 | bytes 3457956 | tf_op jit(solution)/shard_map/add | solution.py:75
  18.6 18.7 %all_gather.6 = f32[127,16,128]{2,0,1:T(8,128)S(1)} all-gather(f32[127,1,128]{2,0,1:T(8,128)S(1)} %fusion.467), channel_id=1, replica_groups=mesh['lon'=32,'lat'=16] {'lat'}, dimensions={1}, use_global_device_ids=true | all-gather | bytes 1105408 | tf_op jit(solution)/shard_map/all_gather | solution.py:84
  37.3 0.3 multiply_reduce_fusion.1
  38.1 18.5 %all-gather = f32[127,2048]{0,1:T(8,128)S(1)} all-gather(f32[127,128]{0,1:T(8,128)S(1)} %convolution_bitcast_fusion), channel_id=2, replica_groups=mesh['lon'=32,'lat'=16] {'lat'}, dimensions={1}, use_global_device_ids=true | all-gather | bytes 1105408 | tf_op jit(solution)/shard_map/all_gather | solution.py:84
  56.7 8.5 %collective-permute-start.2 = (f32[127,1,50]{0,2,1:T(8,128)S(1)}, f32[127,1,50]{0,2,1:T(8,128)S(1)}, u32[]{:S(2)}, u32[]{:S(2)}) collective-permute-start(f32[127,1,50]{0,2,1:T(8,128)S(1)} %get-tuple-element.18), channel_id=1, source_target_pairs={{0,16},{16,32},{32,48},{48,64},{64,80},{80,96},{96,112},{112,128},... | collective-permute-start | bytes 76208 | tf_op jit(solution)/shard_map/ppermute | solution.py:22
  65.3 7.0 %collective-permute-start.3 = (f32[127,1,50]{0,2,1:T(8,128)S(1)}, f32[127,1,50]{0,2,1:T(8,128)S(1)}, u32[]{:S(2)}, u32[]{:S(2)}) collective-permute-start(f32[127,1,50]{0,2,1:T(8,128)S(1)} %get-tuple-element.19), channel_id=1, source_target_pairs={{16,0},{32,16},{48,32},{64,48},{80,64},{96,80},{112,96},{128,112},... | collective-permute-start | bytes 76208 | tf_op jit(solution)/shard_map/ppermute | solution.py:24
  72.2 0.7 multiply_reduce_fusion.4
  73.1 1.8 %multiply_reduce_fusion.3 = (f32[]{:T(128)}, f32[127,1,128]{0,2,1:T(8,128)S(1)}) fusion(f32[127,1,128]{0,2,1:T(8,128)S(1)} %copy.57, f32[127,1,50]{0,2,1:T(8,128)S(1)} %collective-permute-done.3, f32[127,1,128]{0,2,1:T(8,128)S(1)} %bitcast.439, f32[127]{0:T(128)S(1)} %get-tuple-element.25, f32[127]{0:T(128)S(1)} %get-tuple-element.26, ...), kind=kLoop, calls=%fused_computation.857 | loop fusion | flops 4941823 | bytes 297184 | tf_op jit(solution)/shard_map/reduce_sum | solution.py:118
  74.9 1.4 pad_maximum_fusion.3
  76.3 10.4 %all_to_all.24 = f32[16,1,2]{2,1,0:T(1,128)S(1)} all-to-all(f32[16,1,2]{2,1,0:T(1,128)S(1)} %broadcast_in_dim.17), channel_id=1, replica_groups=mesh['lon'=32,'lat'=16] {'lat'}, dimensions={0} | all-to-all | bytes 256 | tf_op jit(solution)/shard_map/all_to_all | solution.py:102
  86.7 0.6 broadcast_in_dim.18
  87.3 12.0 %all-to-all-start.1 = ((f32[32,1,2]{2,1,0:T(1,128)}), f32[32,1,2]{2,1,0:T(1,128)S(1)}, u32[]{:S(2)}, u32[]{:S(2)}) async-start(f32[32,1,2]{2,1,0:T(1,128)} %broadcast_in_dim.18), calls=%async_computation.1 | async-start | bytes 32768 | tf_op jit(solution)/shard_map/all_to_all | solution.py:102
  99.4 11.6 %all-to-all-done.1 = f32[32,1,2]{2,1,0:T(1,128)S(1)} async-done(((f32[32,1,2]{2,1,0:T(1,128)}), f32[32,1,2]{2,1,0:T(1,128)S(1)}, u32[]{:S(2)}, u32[]{:S(2)}) %all-to-all-start.1) | async-done | bytes 288 | tf_op jit(solution)/shard_map/all_to_all | solution.py:102
  111.1 0.6 fusion.513
  113.0 0.6 multiply_reduce_fusion.2
  113.6 0.7 broadcast_in_dim.19
  114.3 9.1 %all_to_all.25 = f32[16,1,1]{2,1,0:T(1,128)S(1)} all-to-all(f32[16,1,1]{2,1,0:T(1,128)S(1)} %broadcast_in_dim.19), channel_id=1, replica_groups=mesh['lon'=32,'lat'=16] {'lat'}, dimensions={0} | all-to-all | bytes 128 | tf_op jit(solution)/shard_map/all_to_all | solution.py:102
  123.4 0.6 reduce_sum.101
  124.0 1.3 broadcast_in_dim.20
  125.3 5.8 %all-to-all-start.3 = ((f32[32,1,1]{2,1,0:T(1,128)}), f32[32,1,1]{2,1,0:T(1,128)S(1)}, u32[]{:S(2)}, u32[]{:S(2)}) async-start(f32[32,1,1]{2,1,0:T(1,128)} %broadcast_in_dim.20), calls=%async_computation.3 | async-start | bytes 32768 | tf_op jit(solution)/shard_map/all_to_all | solution.py:102
  131.2 0.7 copy.67
  131.9 11.0 %all-to-all-done.3 = f32[32,1,1]{2,1,0:T(1,128)S(1)} async-done(((f32[32,1,1]{2,1,0:T(1,128)}), f32[32,1,1]{2,1,0:T(1,128)S(1)}, u32[]{:S(2)}, u32[]{:S(2)}) %all-to-all-start.3) | async-done | bytes 160 | tf_op jit(solution)/shard_map/all_to_all | solution.py:102
  142.9 0.6 reduce_sum.102
  144.9 0.7 copy.66
  145.6 0.7 copy.68
  (58 shorter events, 3.3 us)
Async XLA Ops:
  0.6 37.0 %copy-start = (f32[127,127]{1,0:T(8,128)S(1)}, f32[127,127]{1,0:T(8,128)}, u32[]{:S(2)}) copy-start(f32[127,127]{1,0:T(8,128)} %param.12) | copy-start | bytes 193552
  1.6 12.2 %collective-permute-start.1 = (f32[127,1,50]{2,0,1:T(8,128)S(1)}, f32[127,1,50]{2,0,1:T(8,128)S(1)}, u32[]{:S(2)}, u32[]{:S(2)}) collective-permute-start(f32[127,1,50]{2,0,1:T(8,128)S(1)} %get-tuple-element.21), channel_id=1, source_target_pairs={{16,0},{32,16},{48,32},{64,48},{80,64},{96,80},{112,96},{128,112},... | collective-permute-start | bytes 76208 | tf_op jit(solution)/shard_map/ppermute | solution.py:24
  8.5 0.7 copy-start.7
  8.5 5.3 %collective-permute-start = (f32[127,1,50]{2,0,1:T(8,128)S(1)}, f32[127,1,50]{2,0,1:T(8,128)S(1)}, u32[]{:S(2)}, u32[]{:S(2)}) collective-permute-start(f32[127,1,50]{2,0,1:T(8,128)S(1)} %get-tuple-element.20), channel_id=1, source_target_pairs={{0,16},{16,32},{32,48},{48,64},{64,80},{80,96},{96,112},{112,128},... | collective-permute-start | bytes 76208 | tf_op jit(solution)/shard_map/ppermute | solution.py:22
  9.3 0.7 copy-start.4
  10.4 0.7 copy-start.3
  12.8 0.8 copy-start.5
  56.7 15.5 %copy-start.2 = (f32[127,1,128]{2,1,0:T(1,128)S(1)}, f32[127,1,128]{2,1,0:T(1,128)}, u32[]{:S(2)}) copy-start(f32[127,1,128]{2,1,0:T(1,128)} %param.9) | copy-start | bytes 195076
  56.7 16.3 %copy-start.1 = (f32[127,1,128]{2,1,0:T(1,128)S(1)}, f32[127,1,128]{2,1,0:T(1,128)}, u32[]{:S(2)}) copy-start(f32[127,1,128]{2,1,0:T(1,128)} %param.10) | copy-start | bytes 195076
  56.7 16.3 %collective-permute-start.2 = (f32[127,1,50]{0,2,1:T(8,128)S(1)}, f32[127,1,50]{0,2,1:T(8,128)S(1)}, u32[]{:S(2)}, u32[]{:S(2)}) collective-permute-start(f32[127,1,50]{0,2,1:T(8,128)S(1)} %get-tuple-element.18), channel_id=1, source_target_pairs={{0,16},{16,32},{32,48},{48,64},{64,80},{80,96},{96,112},{112,128},... | collective-permute-start | bytes 76208 | tf_op jit(solution)/shard_map/ppermute | solution.py:22
  65.3 7.8 %collective-permute-start.3 = (f32[127,1,50]{0,2,1:T(8,128)S(1)}, f32[127,1,50]{0,2,1:T(8,128)S(1)}, u32[]{:S(2)}, u32[]{:S(2)}) collective-permute-start(f32[127,1,50]{0,2,1:T(8,128)S(1)} %get-tuple-element.19), channel_id=1, source_target_pairs={{16,0},{32,16},{48,32},{64,48},{80,64},{96,80},{112,96},{128,112},... | collective-permute-start | bytes 76208 | tf_op jit(solution)/shard_map/ppermute | solution.py:24
  87.3 23.7 %all-to-all-start.1 = ((f32[32,1,2]{2,1,0:T(1,128)}), f32[32,1,2]{2,1,0:T(1,128)S(1)}, u32[]{:S(2)}, u32[]{:S(2)}) async-start(f32[32,1,2]{2,1,0:T(1,128)} %broadcast_in_dim.18), calls=%async_computation.1 | async-start | bytes 32768 | tf_op jit(solution)/shard_map/all_to_all | solution.py:102
  113.6 17.5 %copy-start.6 = (f32[127,1,128]{2,1,0:T(1,128)S(1)}, f32[127,1,128]{2,1,0:T(1,128)}, u32[]{:S(2)}) copy-start(f32[127,1,128]{2,1,0:T(1,128)} %param.8) | copy-start | bytes 195076
  125.3 17.6 %all-to-all-start.3 = ((f32[32,1,1]{2,1,0:T(1,128)}), f32[32,1,1]{2,1,0:T(1,128)S(1)}, u32[]{:S(2)}, u32[]{:S(2)}) async-start(f32[32,1,1]{2,1,0:T(1,128)} %broadcast_in_dim.20), calls=%async_computation.3 | async-start | bytes 32768 | tf_op jit(solution)/shard_map/all_to_all | solution.py:102

commit v3 on v2

--- a/solution.py
+++ b/solution.py
@@ -112,10 +112,12 @@
     lat_part = lat_pass(lon_part, lat_taps, groups, False)
     lifted = vertical_mix(vertical, lat_part)
     weighted = obs_weight * lifted
+    norm_old, curvature = total(
+        (jnp.sum(residual * residual), jnp.sum(direction * direction) + jnp.sum(weighted * lifted))
+    )
     back_vert = vertical_mix(vertical.T, weighted)
     back_lat = lat_pass(back_vert, lat_taps, groups, True)
-    applied = direction + lon_pass(back_lat, lon_taps, groups, True)
-    norm_old, curvature = total((jnp.sum(residual * residual), jnp.sum(direction * applied)))
+    applied = lax.optimization_barrier(direction + lon_pass(back_lat, lon_taps, groups, True))
     step_length = norm_old / curvature
     residual_next = residual - step_length * applied
     (norm_new,) = total((jnp.sum(residual_next * residual_next),))

time: 147 us -> 142 us (0.966)
  blocking collectives: 56.7 us -> 47.7 us
  starting transfers between devices: 40.2 us -> 43.2 us
  waiting for transfers between devices: 22.6 us -> 21.1 us
    all_to_all x2 -> x3, starting transfers between devices: 17.8 us -> 34.7 us  [total(): lax.all_to_all(jnp.broadcast_to(v[None], (n,) + v.shape), axis, 0, 0, til...]
    all_to_all x2 -> x1, blocking collectives: 19.5 us -> 10.9 us  [total(): lax.all_to_all(jnp.broadcast_to(v[None], (n,) + v.shape), axis, 0, 0, til...]
    ppermute x2, starting transfers between devices: 13.9 us -> 6.89 us  [with_halo(): lax.ppermute(head, axis, [((i + 1) % count, i) for i in range(count)])]
    ppermute x2, starting transfers between devices: 8.51 us -> 1.65 us  [with_halo(): lax.ppermute(tail, axis, [(i, (i + 1) % count) for i in range(count)])]
    all_to_all x2 -> x3, waiting for transfers between devices: 22.6 us -> 21.1 us  [total(): lax.all_to_all(jnp.broadcast_to(v[None], (n,) + v.shape), axis, 0, 0, til...]
  transfers between devices with their start and end apart: 6 -> 7, of which waited for: 2 -> 2; matrix products, arithmetic and copies ran while one was open for 3% -> 5% of each run, Pallas kernels for 0% -> 0%
where the time goes in v3:
time: 142 us
  blocking collectives  47.7 us (34%)
  starting transfers between devices  43.2 us (30%)
  waiting for transfers between devices  21.1 us (15%)
  local copies, waits for them, and re-layouts  11.5 us (8%)
  other arithmetic  10.9 us (8%)
  between operations  4.99 us (4%)
  matrix products  2.22 us (2%)
    all_gather x2, blocking collectives, lat_pass(): full = lax.all_gather(grid_field, 'lat', axis=1, tiled=True)  36.8 us
    all_to_all x3, starting transfers between devices, total(): lax.all_to_all(jnp.broadcast_to(v[None], (n,) + v.shape), axis, 0, 0, til...  34.7 us
    all_to_all x3, waiting for transfers between devices, total(): lax.all_to_all(jnp.broadcast_to(v[None], (n,) + v.shape), axis, 0, 0, til...  21.1 us
    all_to_all x1, blocking collectives, total(): lax.all_to_all(jnp.broadcast_to(v[None], (n,) + v.shape), axis, 0, 0, til...  10.9 us
    ppermute x2, starting transfers between devices, with_halo(): lax.ppermute(head, axis, [((i + 1) % count, i) for i in range(count)])  6.89 us
    unnamed x24, local copies, waits for them, and re-layouts  6.19 us
    add x1, other arithmetic, lon_pass(): total_sum + kernels[:, None, shift_tap:shift_tap + 1] * extended[:, :, sh...  4.75 us
    broadcast_in_dim x4, local copies, waits for them, and re-layouts, total(): jnp.broadcast_to(v[None], (n,) + v.shape)  3.14 us
  transfers between devices with their start and end apart: 7, of which 2 were waited for; matrix products, arithmetic and copies ran while one was open for 5% of the time, Pallas kernels for 0%

profile of v3, /device:TPU:1, one launch (start us, length us, event | category | flops | bytes accessed | tf_op | source)
XLA Modules:
  0.0 141.6 jit_solution(13945324349366110084)
XLA Ops:
  0.6 0.9 fusion.511
  1.6 6.9 %collective-permute-start.1 = (f32[127,1,50]{2,0,1:T(8,128)S(1)}, f32[127,1,50]{2,0,1:T(8,128)S(1)}, u32[]{:S(2)}, u32[]{:S(2)}) collective-permute-start(f32[127,1,50]{2,0,1:T(8,128)S(1)} %get-tuple-element.19), channel_id=1, source_target_pairs={{16,0},{32,16},{48,32},{64,48},{80,64},{96,80},{112,96},{128,112},... | collective-permute-start | bytes 76208 | tf_op jit(solution)/shard_map/ppermute | solution.py:24
  8.5 0.7 copy-done.7
  10.4 0.6 copy-done.3
  11.5 0.7 multiply_reduce_fusion.4
  13.6 0.6 gather_fusion
  14.4 0.7 multiply_reduce_fusion.5
  15.4 0.7 copy-done.5
  16.2 4.7 %fusion.465 = f32[127,1,128]{2,0,1:T(8,128)S(1)} fusion(f32[127,1,178]{2,0,1:T(8,128)S(1)} %constant_dynamic-update-slice_fusion, f32[127,1,128]{2,0,1:T(8,128)S(1)} %get-tuple-element.20, f32[127,1,50]{2,0,1:T(8,128)S(1)} %collective-permute-done, f32[127]{0:T(128)S(1)} %get-tuple-element.124, f32[127]{0:T(128)S(1)} %get-tuple-element.125, ...), kind=kLoop, calls=%fused_computation.768 | loop fusion | flops 4080256 | bytes 3457956 | tf_op jit(solution)/shard_map/add | solution.py:75
  21.0 16.6 %all_gather.6 = f32[127,16,128]{2,0,1:T(8,128)S(1)} all-gather(f32[127,1,128]{2,0,1:T(8,128)S(1)} %fusion.465), channel_id=1, replica_groups=mesh['lon'=32,'lat'=16] {'lat'}, dimensions={1}, use_global_device_ids=true | all-gather | bytes 1105408 | tf_op jit(solution)/shard_map/all_gather | solution.py:84
  37.9 0.9 multiply_reduce_fusion.3
  40.1 0.7 pad_maximum_fusion.3
  40.8 0.6 broadcast_in_dim.17
  41.4 5.3 %all-to-all-start = ((f32[16,1,2]{2,1,0:T(1,128)}), f32[16,1,2]{2,1,0:T(1,128)S(1)}, u32[]{:S(2)}, u32[]{:S(2)}) async-start(f32[16,1,2]{2,1,0:T(1,128)} %broadcast_in_dim.17), calls=%async_computation | async-start | bytes 16384 | tf_op jit(solution)/shard_map/all_to_all | solution.py:102
  47.0 20.2 %all-gather = f32[127,2048]{0,1:T(8,128)S(1)} all-gather(f32[127,128]{0,1:T(8,128)S(1)} %convolution_bitcast_fusion), channel_id=2, replica_groups=mesh['lon'=32,'lat'=16] {'lat'}, dimensions={1}, use_global_device_ids=true | all-gather | bytes 1105408 | tf_op jit(solution)/shard_map/all_gather | solution.py:84
  67.3 0.6 broadcast_in_dim.18
  68.0 23.5 %all-to-all-start.1 = ((f32[32,1,2]{2,1,0:T(1,128)}), f32[32,1,2]{2,1,0:T(1,128)S(1)}, u32[]{:S(2)}, u32[]{:S(2)}) async-start(f32[32,1,2]{2,1,0:T(1,128)} %broadcast_in_dim.18), calls=%async_computation.1 | async-start | bytes 32768 | tf_op jit(solution)/shard_map/all_to_all | solution.py:102
  91.5 1.6 %collective-permute-start.2 = (f32[127,1,50]{0,2,1:T(8,128)S(1)}, f32[127,1,50]{0,2,1:T(8,128)S(1)}, u32[]{:S(2)}, u32[]{:S(2)}) collective-permute-start(f32[127,1,50]{0,2,1:T(8,128)S(1)} %get-tuple-element.16), channel_id=1, source_target_pairs={{0,16},{16,32},{32,48},{48,64},{64,80},{80,96},{96,112},{112,128},... | collective-permute-start | bytes 76208 | tf_op jit(solution)/shard_map/ppermute | solution.py:22
  93.2 10.2 %all-to-all-done.1 = f32[32,1,2]{2,1,0:T(1,128)S(1)} async-done(((f32[32,1,2]{2,1,0:T(1,128)}), f32[32,1,2]{2,1,0:T(1,128)S(1)}, u32[]{:S(2)}, u32[]{:S(2)}) %all-to-all-start.1) | async-done | bytes 288 | tf_op jit(solution)/shard_map/all_to_all | solution.py:102
  103.4 0.6 fusion.512
  105.3 1.2 fusion.4
  106.5 0.6 multiply_reduce_fusion.2
  107.1 0.7 broadcast_in_dim.19
  107.8 10.9 %all_to_all.24 = f32[16,1,1]{2,1,0:T(1,128)S(1)} all-to-all(f32[16,1,1]{2,1,0:T(1,128)S(1)} %broadcast_in_dim.19), channel_id=1, replica_groups=mesh['lon'=32,'lat'=16] {'lat'}, dimensions={0} | all-to-all | bytes 128 | tf_op jit(solution)/shard_map/all_to_all | solution.py:102
  118.6 0.6 reduce_sum.111
  119.3 1.3 broadcast_in_dim.20
  120.5 5.8 %all-to-all-start.3 = ((f32[32,1,1]{2,1,0:T(1,128)}), f32[32,1,1]{2,1,0:T(1,128)S(1)}, u32[]{:S(2)}, u32[]{:S(2)}) async-start(f32[32,1,1]{2,1,0:T(1,128)} %broadcast_in_dim.20), calls=%async_computation.3 | async-start | bytes 32768 | tf_op jit(solution)/shard_map/all_to_all | solution.py:102
  126.5 0.7 copy.64
  127.2 11.0 %all-to-all-done.3 = f32[32,1,1]{2,1,0:T(1,128)S(1)} async-done(((f32[32,1,1]{2,1,0:T(1,128)}), f32[32,1,1]{2,1,0:T(1,128)S(1)}, u32[]{:S(2)}, u32[]{:S(2)}) %all-to-all-start.3) | async-done | bytes 160 | tf_op jit(solution)/shard_map/all_to_all | solution.py:102
  138.2 0.6 reduce_sum.112
  140.1 0.7 copy.63
  140.9 0.7 copy.65
  (60 shorter events, 4.4 us)
Async XLA Ops:
  0.6 37.3 %copy-start = (f32[127,127]{1,0:T(8,128)S(1)}, f32[127,127]{1,0:T(8,128)}, u32[]{:S(2)}) copy-start(f32[127,127]{1,0:T(8,128)} %param.12) | copy-start | bytes 193552
  1.6 14.6 %collective-permute-start.1 = (f32[127,1,50]{2,0,1:T(8,128)S(1)}, f32[127,1,50]{2,0,1:T(8,128)S(1)}, u32[]{:S(2)}, u32[]{:S(2)}) collective-permute-start(f32[127,1,50]{2,0,1:T(8,128)S(1)} %get-tuple-element.19), channel_id=1, source_target_pairs={{16,0},{32,16},{48,32},{64,48},{80,64},{96,80},{112,96},{128,112},... | collective-permute-start | bytes 76208 | tf_op jit(solution)/shard_map/ppermute | solution.py:24
  8.5 0.7 copy-start.7
  8.5 7.7 %collective-permute-start = (f32[127,1,50]{2,0,1:T(8,128)S(1)}, f32[127,1,50]{2,0,1:T(8,128)S(1)}, u32[]{:S(2)}, u32[]{:S(2)}) collective-permute-start(f32[127,1,50]{2,0,1:T(8,128)S(1)} %get-tuple-element.18), channel_id=1, source_target_pairs={{0,16},{16,32},{32,48},{48,64},{64,80},{80,96},{96,112},{112,128},... | collective-permute-start | bytes 76208 | tf_op jit(solution)/shard_map/ppermute | solution.py:22
  9.3 0.7 copy-start.4
  10.4 0.7 copy-start.3
  10.4 1.1 copy-start.1
  13.6 0.8 copy-start.2
  15.2 0.8 copy-start.5
  41.4 25.9 %all-to-all-start = ((f32[16,1,2]{2,1,0:T(1,128)}), f32[16,1,2]{2,1,0:T(1,128)S(1)}, u32[]{:S(2)}, u32[]{:S(2)}) async-start(f32[16,1,2]{2,1,0:T(1,128)} %broadcast_in_dim.17), calls=%async_computation | async-start | bytes 16384 | tf_op jit(solution)/shard_map/all_to_all | solution.py:102
  68.0 35.3 %all-to-all-start.1 = ((f32[32,1,2]{2,1,0:T(1,128)}), f32[32,1,2]{2,1,0:T(1,128)S(1)}, u32[]{:S(2)}, u32[]{:S(2)}) async-start(f32[32,1,2]{2,1,0:T(1,128)} %broadcast_in_dim.18), calls=%async_computation.1 | async-start | bytes 32768 | tf_op jit(solution)/shard_map/all_to_all | solution.py:102
  91.5 13.8 %collective-permute-start.2 = (f32[127,1,50]{0,2,1:T(8,128)S(1)}, f32[127,1,50]{0,2,1:T(8,128)S(1)}, u32[]{:S(2)}, u32[]{:S(2)}) collective-permute-start(f32[127,1,50]{0,2,1:T(8,128)S(1)} %get-tuple-element.16), channel_id=1, source_target_pairs={{0,16},{16,32},{32,48},{48,64},{64,80},{80,96},{96,112},{112,128},... | collective-permute-start | bytes 76208 | tf_op jit(solution)/shard_map/ppermute | solution.py:22
  93.2 12.1 %collective-permute-start.3 = (f32[127,1,50]{0,2,1:T(8,128)S(1)}, f32[127,1,50]{0,2,1:T(8,128)S(1)}, u32[]{:S(2)}, u32[]{:S(2)}) collective-permute-start(f32[127,1,50]{0,2,1:T(8,128)S(1)} %get-tuple-element.17), channel_id=1, source_target_pairs={{16,0},{32,16},{48,32},{64,48},{80,64},{96,80},{112,96},{128,112},... | collective-permute-start | bytes 76208 | tf_op jit(solution)/shard_map/ppermute | solution.py:24
  107.1 19.2 %copy-start.6 = (f32[127,1,128]{2,1,0:T(1,128)S(1)}, f32[127,1,128]{2,1,0:T(1,128)}, u32[]{:S(2)}) copy-start(f32[127,1,128]{2,1,0:T(1,128)} %param.8) | copy-start | bytes 195076
  120.5 17.6 %all-to-all-start.3 = ((f32[32,1,1]{2,1,0:T(1,128)}), f32[32,1,1]{2,1,0:T(1,128)S(1)}, u32[]{:S(2)}, u32[]{:S(2)}) async-start(f32[32,1,1]{2,1,0:T(1,128)} %broadcast_in_dim.20), calls=%async_computation.3 | async-start | bytes 32768 | tf_op jit(solution)/shard_map/all_to_all | solution.py:102

commit v4 on v3

--- a/solution.py
+++ b/solution.py
@@ -1,6 +1,7 @@
 import jax
 import jax.numpy as jnp
 from jax import lax
+from jax.experimental import pallas as pl
 from jax.sharding import PartitionSpec as P
 
 LEV = 127
@@ -65,39 +66,49 @@
     return jnp.take(padded, sources, axis=0)
 
 
+def lon_kernel(taps_ref, extended_ref, out_ref):
+    width = out_ref.shape[1]
+    total_sum = taps_ref[:, 0:1] * extended_ref[:, 0:width]
+    for shift_tap in range(1, TAPS):
+        total_sum = total_sum + taps_ref[:, shift_tap : shift_tap + 1] * extended_ref[
+            :, shift_tap : shift_tap + width
+        ]
+    out_ref[...] = total_sum
+
+
 def lon_pass(grid_field, kernel_groups, groups, adjoint):
     kernel = kernel_groups[:, ::-1] if adjoint else kernel_groups
-    lon_width = grid_field.shape[2]
-    kernels = group_rows(groups, kernel)
+    levels, rows, lon_width = grid_field.shape
+    kernels = jnp.repeat(group_rows(groups, kernel), rows, axis=0)
     extended = with_halo(grid_field, (("lon", 2),), HALF)
-    total_sum = kernels[:, None, 0:1] * extended[:, :, 0:lon_width]
-    for shift_tap in range(1, TAPS):
-        total_sum = total_sum + kernels[:, None, shift_tap : shift_tap + 1] * extended[
-            :, :, shift_tap : shift_tap + lon_width
-        ]
-    return total_sum
+    filtered = pl.pallas_call(
+        lon_kernel, out_shape=jax.ShapeDtypeStruct((levels * rows, lon_width), grid_field.dtype)
+    )(kernels, extended.reshape(levels * rows, -1))
+    return filtered.reshape(levels, rows, lon_width)
+
+
+def to_columns(grid_field):
+    return lax.all_to_all(grid_field, "lat", 2, 1, tiled=True)
+
+
+def to_rows(grid_field):
+    return lax.all_to_all(grid_field, "lat", 1, 2, tiled=True)
 
 
 def lat_pass(grid_field, kernel_groups, groups, adjoint):
     kernel = kernel_groups[:, ::-1] if adjoint else kernel_groups
-    rows = grid_field.shape[1]
-    full = lax.all_gather(grid_field, "lat", axis=1, tiled=True)
-    lat_width = full.shape[1]
-    own = lax.axis_index("lat") * rows + jnp.arange(rows, dtype=jnp.int32)
-    offsets = jnp.arange(lat_width, dtype=jnp.int32)[:, None] - own[None, :] + HALF
-    inside = (offsets >= 0) & (offsets < TAPS)
-    picked = group_rows(groups, kernel)[:, jnp.clip(offsets, 0, TAPS - 1)]
-    matrices = jnp.where(inside[None], picked, jnp.zeros_like(picked))
-    return jnp.sum(matrices[:, :, :, None] * full[:, :, None, :], axis=1)
+    lat_width = grid_field.shape[1]
+    matrices = band_matrices(group_rows(groups, kernel), lat_width, lat_width)
+    return jnp.sum(matrices[:, :, :, None] * grid_field[:, :, None, :], axis=1)
 
 
 def vertical_mix(matrix, grid_field):
     return jnp.dot(matrix, grid_field.reshape(LEV, -1), precision=HIGHEST).reshape(grid_field.shape)
 
 
-def total(vals):
+def total(vals, axes=("lat", "lon")):
     v = jnp.stack(vals)
-    for axis in ("lat", "lon"):
+    for axis in axes:
         n = lax.axis_size(axis)
         g = lax.all_to_all(jnp.broadcast_to(v[None], (n,) + v.shape), axis, 0, 0, tiled=True)
         v = jnp.sum(g, axis=0)
@@ -109,14 +120,21 @@
     levels = jnp.arange(LEV, dtype=jnp.int32)
     groups = jnp.sum((levels[:, None] >= bounds[None, :]).astype(jnp.int32), axis=1)
     lon_part = lon_pass(direction, lon_taps, groups, False)
-    lat_part = lat_pass(lon_part, lat_taps, groups, False)
+    both = to_columns(jnp.concatenate([lon_part, obs_weight], axis=0))
+    lat_part = lat_pass(both[:LEV], lat_taps, groups, False)
     lifted = vertical_mix(vertical, lat_part)
-    weighted = obs_weight * lifted
-    norm_old, curvature = total(
-        (jnp.sum(residual * residual), jnp.sum(direction * direction) + jnp.sum(weighted * lifted))
+    weighted = both[LEV:] * lifted
+    partial = jnp.stack(
+        [jnp.sum(residual * residual), jnp.sum(direction * direction) + jnp.sum(weighted * lifted)]
     )
     back_vert = vertical_mix(vertical.T, weighted)
-    back_lat = lat_pass(back_vert, lat_taps, groups, True)
+    back_cols = lat_pass(back_vert, lat_taps, groups, True)
+    chunk = back_cols.shape[2]
+    extra = jnp.zeros((1,) + back_cols.shape[1:], back_cols.dtype).at[0, :, :2].set(partial)
+    returned = to_rows(jnp.concatenate([back_cols, extra], axis=0))
+    back_lat = returned[:LEV]
+    lat_sums = jnp.sum(returned[LEV, 0].reshape(-1, chunk)[:, :2], axis=0)
+    norm_old, curvature = total((lat_sums[0], lat_sums[1]), ("lon",))
     applied = lax.optimization_barrier(direction + lon_pass(back_lat, lon_taps, groups, True))
     step_length = norm_old / curvature
     residual_next = residual - step_length * applied

time: 142 us -> 134 us (0.944)
  blocking collectives: 47.7 us -> 9.35 us
  Pallas kernels: 0 us -> 23.9 us
  waiting for transfers between devices: 21.1 us -> 31.6 us
  starting transfers between devices: 43.2 us -> 40.4 us
  other arithmetic: 10.9 us -> 8.79 us
    all_gather x2 -> x0, blocking collectives: 36.8 us -> none  [lat_pass(): full = lax.all_gather(grid_field, 'lat', axis=1, tiled=True)]
    pallas_call x0 -> x2, Pallas kernels: none -> 23.9 us  [lon_pass(): pl.pallas_call(lon_kernel, out_shape=jax.ShapeDtypeStruct((levels * rows,...]
    all_to_all x0 -> x2, waiting for transfers between devices: none -> 10.6 us  [the longest x1 5.6 us: to_rows(): return lax.all_to_all(grid_field, 'lat', 1, 2, tiled=True)]
    all_to_all x3 -> x2, starting transfers between devices: 34.7 us -> 24.7 us  [total(): lax.all_to_all(jnp.broadcast_to(v[None], (n,) + v.shape), axis, 0, 0, til...]
    all_to_all x0 -> x2, starting transfers between devices: none -> 7.14 us  [the longest x1 3.64 us: to_columns(): return lax.all_to_all(grid_field, 'lat', 2, 1, tiled=True)]
    add x1 -> x0, other arithmetic: 4.75 us -> none  [lon_pass(): total_sum + kernels[:, None, shift_tap:shift_tap + 1] * extended[:, :, sh...]
    ppermute x2, starting transfers between devices: 1.65 us -> 4.68 us  [with_halo(): lax.ppermute(tail, axis, [(i, (i + 1) % count) for i in range(count)])]
    ppermute x2, starting transfers between devices: 6.89 us -> 3.87 us  [with_halo(): lax.ppermute(head, axis, [((i + 1) % count, i) for i in range(count)])]
  transfers between devices with their start and end apart: 7 -> 8, of which waited for: 2 -> 4; matrix products, arithmetic and copies ran while one was open for 5% -> 6% of each run, Pallas kernels for 0% -> 0%
where the time goes in v4:
time: 134 us; the launch traced here: 133 us
  starting transfers between devices  40.4 us (30%)
  waiting for transfers between devices  31.6 us (24%)
  Pallas kernels  23.9 us (18%)
  local copies, waits for them, and re-layouts  11.2 us (8%)
  blocking collectives  9.35 us (7%)
  other arithmetic  8.79 us (7%)
  between operations  4.83 us (4%)
  matrix products  3.34 us (2%)
    all_to_all x2, starting transfers between devices, total(): lax.all_to_all(jnp.broadcast_to(v[None], (n,) + v.shape), axis, 0, 0, til...  24.7 us
    pallas_call x2, Pallas kernels, lon_pass(): pl.pallas_call(lon_kernel, out_shape=jax.ShapeDtypeStruct((levels * rows,...  23.9 us
    all_to_all x2, waiting for transfers between devices, total(): lax.all_to_all(jnp.broadcast_to(v[None], (n,) + v.shape), axis, 0, 0, til...  21 us
    all_to_all x1, blocking collectives, total(): lax.all_to_all(jnp.broadcast_to(v[None], (n,) + v.shape), axis, 0, 0, til...  9.35 us
    all_to_all x1, waiting for transfers between devices, to_rows(): return lax.all_to_all(grid_field, 'lat', 1, 2, tiled=True)  5.6 us
    all_to_all x1, waiting for transfers between devices, to_columns(): return lax.all_to_all(grid_field, 'lat', 2, 1, tiled=True)  5.05 us
    unnamed x22, local copies, waits for them, and re-layouts  4.9 us
    ppermute x2, starting transfers between devices, with_halo(): lax.ppermute(tail, axis, [(i, (i + 1) % count) for i in range(count)])  4.68 us
  transfers between devices with their start and end apart: 8, of which 4 were waited for; matrix products, arithmetic and copies ran while one was open for 6% of the time, Pallas kernels for 0%

profile of v4, /device:TPU:1, one launch (start us, length us, event | category | flops | bytes accessed | tf_op | source)
XLA Modules:
  0.0 133.4 jit_solution(10399213764760928489)
XLA Ops:
  0.6 0.9 copy.105
  1.6 3.0 %collective-permute-start = (f32[127,1,50]{2,0,1:T(8,128)S(1)}, f32[127,1,50]{2,0,1:T(8,128)S(1)}, u32[]{:S(2)}, u32[]{:S(2)}) collective-permute-start(f32[127,1,50]{2,0,1:T(8,128)S(1)} %get-tuple-element.36), channel_id=1, source_target_pairs={{0,16},{16,32},{32,48},{48,64},{64,80},{80,96},{96,112},{112,128},... | collective-permute-start | bytes 76208 | tf_op jit(solution)/shard_map/ppermute | solution.py:23
  4.6 3.9 %collective-permute-start.1 = (f32[127,1,50]{2,0,1:T(8,128)S(1)}, f32[127,1,50]{2,0,1:T(8,128)S(1)}, u32[]{:S(2)}, u32[]{:S(2)}) collective-permute-start(f32[127,1,50]{2,0,1:T(8,128)S(1)} %get-tuple-element.37), channel_id=1, source_target_pairs={{16,0},{32,16},{48,32},{64,48},{80,64},{96,80},{112,96},{128,112},... | collective-permute-start | bytes 76208 | tf_op jit(solution)/shard_map/ppermute | solution.py:25
  10.8 0.7 gather_fusion
  11.5 0.7 gather_fusion.1
  13.0 0.8 fusion.3.taps_ref
  13.9 0.8 maximum_bitcast_fusion.extended_ref
  14.6 12.0 %shard_map.103 = f32[127,128]{1,0:T(8,128)} custom-call(f32[127,101]{1,0:T(8,128)} %fusion.3.taps_ref, f32[127,228]{1,0:T(8,128)} %maximum_bitcast_fusion.extended_ref), custom_call_target="tpu_custom_call" | custom-call | tf_op jit(solution)/shard_map/pallas_call | solution.py:84
  26.6 0.8 pad_maximum_fusion
  27.4 0.7 copy.110
  28.2 3.6 %all-to-all-start = ((f32[254,1,128]{0,1,2:T(1,128)}), f32[254,1,128]{0,1,2:T(1,128)S(1)}, u32[]{:S(2)}, u32[]{:S(2)}) async-start(f32[254,1,128]{0,1,2:T(1,128)} %copy.110), calls=%async_computation | async-start | bytes 262144 | tf_op jit(solution)/shard_map/all_to_all | solution.py:91
  31.8 0.7 multiply_reduce_fusion.4
  32.7 0.7 multiply_reduce_fusion.5
  33.4 5.0 %all-to-all-done = f32[254,1,128]{0,1,2:T(1,128)S(1)} async-done(((f32[254,1,128]{0,1,2:T(1,128)}), f32[254,1,128]{0,1,2:T(1,128)S(1)}, u32[]{:S(2)}, u32[]{:S(2)}) %all-to-all-start) | async-done | bytes 130080 | tf_op jit(solution)/shard_map/all_to_all | solution.py:91
  38.8 0.9 multiply_reduce_fusion.3
  41.3 0.7 fusion.13
  42.1 0.7 pad_maximum_fusion.1
  42.8 3.5 %all-to-all-start.1 = ((f32[128,16,8]{0,2,1:T(8,128)}), f32[128,16,8]{0,2,1:T(8,128)S(1)}, u32[]{:S(2)}, u32[]{:S(2)}) async-start(f32[128,16,8]{0,2,1:T(8,128)} %pad_maximum_fusion.1), calls=%async_computation.1 | async-start | bytes 131072 | tf_op jit(solution)/shard_map/all_to_all | solution.py:95
  46.3 0.8 fusion.1.taps_ref
  47.1 5.6 %all-to-all-done.1 = f32[128,16,8]{0,2,1:T(8,128)S(1)} async-done(((f32[128,16,8]{0,2,1:T(8,128)}), f32[128,16,8]{0,2,1:T(8,128)S(1)}, u32[]{:S(2)}, u32[]{:S(2)}) %all-to-all-start.1) | async-done | bytes 65568 | tf_op jit(solution)/shard_map/all_to_all | solution.py:95
  53.7 18.9 %all-to-all-start.2 = ((f32[32,1,2]{2,1,0:T(1,128)}), f32[32,1,2]{2,1,0:T(1,128)S(1)}, u32[]{:S(2)}, u32[]{:S(2)}) async-start(f32[32,1,2]{2,1,0:T(1,128)} %broadcast_in_dim.20), calls=%async_computation.2 | async-start | bytes 32768 | tf_op jit(solution)/shard_map/all_to_all | solution.py:113
  72.8 1.6 %collective-permute-start.2 = (f32[127,1,50]{2,0,1:T(8,128)S(1)}, f32[127,1,50]{2,0,1:T(8,128)S(1)}, u32[]{:S(2)}, u32[]{:S(2)}) collective-permute-start(f32[127,1,50]{2,0,1:T(8,128)S(1)} %get-tuple-element.34), channel_id=1, source_target_pairs={{0,16},{16,32},{32,48},{48,64},{64,80},{80,96},{96,112},{112,128},... | collective-permute-start | bytes 76208 | tf_op jit(solution)/shard_map/ppermute | solution.py:23
  74.4 9.9 %all-to-all-done.2 = f32[32,1,2]{2,1,0:T(1,128)S(1)} async-done(((f32[32,1,2]{2,1,0:T(1,128)}), f32[32,1,2]{2,1,0:T(1,128)S(1)}, u32[]{:S(2)}, u32[]{:S(2)}) %all-to-all-start.2) | async-done | bytes 288 | tf_op jit(solution)/shard_map/all_to_all | solution.py:113
  86.3 0.8 maximum_bitcast_fusion.1.extended_ref
  87.0 12.0 %shard_map.104 = f32[127,128]{1,0:T(8,128)} custom-call(f32[127,101]{1,0:T(8,128)} %fusion.1.taps_ref, f32[127,228]{1,0:T(8,128)} %maximum_bitcast_fusion.1.extended_ref), custom_call_target="tpu_custom_call" | custom-call | tf_op jit(solution)/shard_map/pallas_call | solution.py:84
  99.0 0.8 bitcast_add_fusion
  101.1 9.4 %all_to_all.36 = f32[16,1,1]{2,1,0:T(1,128)S(1)} all-to-all(f32[16,1,1]{2,1,0:T(1,128)S(1)} %broadcast_in_dim.21), channel_id=1, replica_groups=mesh['lon'=32,'lat'=16] {'lat'}, dimensions={0} | all-to-all | bytes 128 | tf_op jit(solution)/shard_map/all_to_all | solution.py:113
  111.1 1.3 broadcast_in_dim.22
  112.3 5.9 %all-to-all-start.4 = ((f32[32,1,1]{2,1,0:T(1,128)}), f32[32,1,1]{2,1,0:T(1,128)S(1)}, u32[]{:S(2)}, u32[]{:S(2)}) async-start(f32[32,1,1]{2,1,0:T(1,128)} %broadcast_in_dim.22), calls=%async_computation.4 | async-start | bytes 32768 | tf_op jit(solution)/shard_map/all_to_all | solution.py:113
  118.2 0.7 copy.127
  118.9 11.1 %all-to-all-done.4 = f32[32,1,1]{2,1,0:T(1,128)S(1)} async-done(((f32[32,1,1]{2,1,0:T(1,128)}), f32[32,1,1]{2,1,0:T(1,128)S(1)}, u32[]{:S(2)}, u32[]{:S(2)}) %all-to-all-start.4) | async-done | bytes 160 | tf_op jit(solution)/shard_map/all_to_all | solution.py:113
  132.0 0.7 copy.126
  (56 shorter events, 8.9 us)
Async XLA Ops:
  0.6 38.1 %copy-start = (f32[127,127]{1,0:T(8,128)S(1)}, f32[127,127]{1,0:T(8,128)}, u32[]{:S(2)}) copy-start(f32[127,127]{1,0:T(8,128)} %param.14) | copy-start | bytes 193552
  1.6 12.2 %collective-permute-start = (f32[127,1,50]{2,0,1:T(8,128)S(1)}, f32[127,1,50]{2,0,1:T(8,128)S(1)}, u32[]{:S(2)}, u32[]{:S(2)}) collective-permute-start(f32[127,1,50]{2,0,1:T(8,128)S(1)} %get-tuple-element.36), channel_id=1, source_target_pairs={{0,16},{16,32},{32,48},{48,64},{64,80},{80,96},{96,112},{112,128},... | collective-permute-start | bytes 76208 | tf_op jit(solution)/shard_map/ppermute | solution.py:23
  4.6 9.2 %collective-permute-start.1 = (f32[127,1,50]{2,0,1:T(8,128)S(1)}, f32[127,1,50]{2,0,1:T(8,128)S(1)}, u32[]{:S(2)}, u32[]{:S(2)}) collective-permute-start(f32[127,1,50]{2,0,1:T(8,128)S(1)} %get-tuple-element.37), channel_id=1, source_target_pairs={{16,0},{32,16},{48,32},{64,48},{80,64},{96,80},{112,96},{128,112},... | collective-permute-start | bytes 76208 | tf_op jit(solution)/shard_map/ppermute | solution.py:25
  8.5 0.7 copy-start.7
  9.3 0.7 copy-start.3
  12.3 0.7 copy-start.4
  13.0 0.9 copy-start.6
  28.2 3.7 %copy-start.1 = (f32[127,1,128]{2,1,0:T(1,128)S(1)}, f32[127,1,128]{2,1,0:T(1,128)}, u32[]{:S(2)}) copy-start(f32[127,1,128]{2,1,0:T(1,128)} %param.12) | copy-start | bytes 195076
  28.2 10.3 %all-to-all-start = ((f32[254,1,128]{0,1,2:T(1,128)}), f32[254,1,128]{0,1,2:T(1,128)S(1)}, u32[]{:S(2)}, u32[]{:S(2)}) async-start(f32[254,1,128]{0,1,2:T(1,128)} %copy.110), calls=%async_computation | async-start | bytes 262144 | tf_op jit(solution)/shard_map/all_to_all | solution.py:91
  31.8 0.8 copy-start.2
  42.8 10.0 %all-to-all-start.1 = ((f32[128,16,8]{0,2,1:T(8,128)}), f32[128,16,8]{0,2,1:T(8,128)S(1)}, u32[]{:S(2)}, u32[]{:S(2)}) async-start(f32[128,16,8]{0,2,1:T(8,128)} %pad_maximum_fusion.1), calls=%async_computation.1 | async-start | bytes 131072 | tf_op jit(solution)/shard_map/all_to_all | solution.py:95
  53.7 30.6 %all-to-all-start.2 = ((f32[32,1,2]{2,1,0:T(1,128)}), f32[32,1,2]{2,1,0:T(1,128)S(1)}, u32[]{:S(2)}, u32[]{:S(2)}) async-start(f32[32,1,2]{2,1,0:T(1,128)} %broadcast_in_dim.20), calls=%async_computation.2 | async-start | bytes 32768 | tf_op jit(solution)/shard_map/all_to_all | solution.py:113
  72.8 13.5 %collective-permute-start.2 = (f32[127,1,50]{2,0,1:T(8,128)S(1)}, f32[127,1,50]{2,0,1:T(8,128)S(1)}, u32[]{:S(2)}, u32[]{:S(2)}) collective-permute-start(f32[127,1,50]{2,0,1:T(8,128)S(1)} %get-tuple-element.34), channel_id=1, source_target_pairs={{0,16},{16,32},{32,48},{48,64},{64,80},{80,96},{96,112},{112,128},... | collective-permute-start | bytes 76208 | tf_op jit(solution)/shard_map/ppermute | solution.py:23
  74.4 11.9 %collective-permute-start.3 = (f32[127,1,50]{2,0,1:T(8,128)S(1)}, f32[127,1,50]{2,0,1:T(8,128)S(1)}, u32[]{:S(2)}, u32[]{:S(2)}) collective-permute-start(f32[127,1,50]{2,0,1:T(8,128)S(1)} %get-tuple-element.35), channel_id=1, source_target_pairs={{16,0},{32,16},{48,32},{64,48},{80,64},{96,80},{112,96},{128,112},... | collective-permute-start | bytes 76208 | tf_op jit(solution)/shard_map/ppermute | solution.py:25
  112.3 17.7 %all-to-all-start.4 = ((f32[32,1,1]{2,1,0:T(1,128)}), f32[32,1,1]{2,1,0:T(1,128)S(1)}, u32[]{:S(2)}, u32[]{:S(2)}) async-start(f32[32,1,1]{2,1,0:T(1,128)} %broadcast_in_dim.22), calls=%async_computation.4 | async-start | bytes 32768 | tf_op jit(solution)/shard_map/all_to_all | solution.py:113
  118.2 13.8 %copy-start.5 = (f32[127,1,128]{2,1,0:T(1,128)S(1)}, f32[127,1,128]{2,1,0:T(1,128)}, u32[]{:S(2)}) copy-start(f32[127,1,128]{2,1,0:T(1,128)} %param.10) | copy-start | bytes 195076

commit v5 on v4

--- a/solution.py
+++ b/solution.py
@@ -67,11 +67,11 @@
 
 
 def lon_kernel(taps_ref, extended_ref, out_ref):
-    width = out_ref.shape[1]
-    total_sum = taps_ref[:, 0:1] * extended_ref[:, 0:width]
+    width = out_ref.shape[0]
+    total_sum = taps_ref[0:1, :] * extended_ref[0:width, :]
     for shift_tap in range(1, TAPS):
-        total_sum = total_sum + taps_ref[:, shift_tap : shift_tap + 1] * extended_ref[
-            :, shift_tap : shift_tap + width
+        total_sum = total_sum + taps_ref[shift_tap : shift_tap + 1, :] * extended_ref[
+            shift_tap : shift_tap + width, :
         ]
     out_ref[...] = total_sum
 
@@ -82,9 +82,9 @@
     kernels = jnp.repeat(group_rows(groups, kernel), rows, axis=0)
     extended = with_halo(grid_field, (("lon", 2),), HALF)
     filtered = pl.pallas_call(
-        lon_kernel, out_shape=jax.ShapeDtypeStruct((levels * rows, lon_width), grid_field.dtype)
-    )(kernels, extended.reshape(levels * rows, -1))
-    return filtered.reshape(levels, rows, lon_width)
+        lon_kernel, out_shape=jax.ShapeDtypeStruct((lon_width, levels * rows), grid_field.dtype)
+    )(kernels.T, extended.reshape(levels * rows, -1).T)
+    return filtered.T.reshape(levels, rows, lon_width)
 
 
 def to_columns(grid_field):

time: 134 us -> 115 us (0.86)
  Pallas kernels: 23.9 us -> 4.16 us
    pallas_call x2, Pallas kernels: 23.9 us -> 4.16 us  [lon_pass(): pl.pallas_call(lon_kernel, out_shape=jax.ShapeDtypeStruct((lon_width, lev...]
    reshape x2 -> x0, other arithmetic: 1.52 us -> none  [lon_pass(): extended.reshape(levels * rows, -1)]
    unnamed x22 -> x24, local copies, waits for them, and re-layouts: 4.9 us -> 5.37 us
  transfers between devices with their start and end apart: 8 -> 8, of which waited for: 4 -> 4; matrix products, arithmetic and copies ran while one was open for 6% -> 7% of each run, Pallas kernels for 0% -> 0%
where the time goes in v5:
time: 115 us; the launch traced here: 114 us
  starting transfers between devices  40.4 us (35%)
  waiting for transfers between devices  31.6 us (27%)
  local copies, waits for them, and re-layouts  11.4 us (10%)
  blocking collectives  9.35 us (8%)
  other arithmetic  8.66 us (8%)
  between operations  4.87 us (4%)
  Pallas kernels  4.16 us (4%)
  matrix products  3.45 us (3%)
    all_to_all x2, starting transfers between devices, total(): lax.all_to_all(jnp.broadcast_to(v[None], (n,) + v.shape), axis, 0, 0, til...  24.7 us
    all_to_all x2, waiting for transfers between devices, total(): lax.all_to_all(jnp.broadcast_to(v[None], (n,) + v.shape), axis, 0, 0, til...  21.1 us
    all_to_all x1, blocking collectives, total(): lax.all_to_all(jnp.broadcast_to(v[None], (n,) + v.shape), axis, 0, 0, til...  9.35 us
    all_to_all x1, waiting for transfers between devices, to_rows(): return lax.all_to_all(grid_field, 'lat', 1, 2, tiled=True)  5.45 us
    unnamed x24, local copies, waits for them, and re-layouts  5.37 us
    all_to_all x1, waiting for transfers between devices, to_columns(): return lax.all_to_all(grid_field, 'lat', 2, 1, tiled=True)  5.05 us
    ppermute x2, starting transfers between devices, with_halo(): lax.ppermute(tail, axis, [(i, (i + 1) % count) for i in range(count)])  4.68 us
    pallas_call x2, Pallas kernels, lon_pass(): pl.pallas_call(lon_kernel, out_shape=jax.ShapeDtypeStruct((lon_width, lev...  4.16 us
  transfers between devices with their start and end apart: 8, of which 4 were waited for; matrix products, arithmetic and copies ran while one was open for 7% of the time, Pallas kernels for 0%

profile of v5, /device:TPU:1, one launch (start us, length us, event | category | flops | bytes accessed | tf_op | source)
XLA Modules:
  0.0 113.9 jit_solution(8073836094957732652)
XLA Ops:
  0.6 1.0 copy.84
  1.6 3.0 %collective-permute-start = (f32[127,1,50]{0,2,1:T(8,128)S(1)}, f32[127,1,50]{0,2,1:T(8,128)S(1)}, u32[]{:S(2)}, u32[]{:S(2)}) collective-permute-start(f32[127,1,50]{0,2,1:T(8,128)S(1)} %get-tuple-element.38), channel_id=1, source_target_pairs={{0,16},{16,32},{32,48},{48,64},{64,80},{80,96},{96,112},{112,128},... | collective-permute-start | bytes 76208 | tf_op jit(solution)/shard_map/ppermute | solution.py:23
  4.7 3.9 %collective-permute-start.1 = (f32[127,1,50]{0,2,1:T(8,128)S(1)}, f32[127,1,50]{0,2,1:T(8,128)S(1)}, u32[]{:S(2)}, u32[]{:S(2)}) collective-permute-start(f32[127,1,50]{0,2,1:T(8,128)S(1)} %get-tuple-element.39), channel_id=1, source_target_pairs={{16,0},{32,16},{48,32},{64,48},{80,64},{96,80},{112,96},{128,112},... | collective-permute-start | bytes 76208 | tf_op jit(solution)/shard_map/ppermute | solution.py:25
  10.8 0.7 gather_fusion
  11.6 0.7 gather_fusion.1
  13.0 0.9 convolution_bitcast_fusion.3.taps_ref
  14.7 2.1 %shard_map.103 = f32[128,127]{1,0:T(8,128)} custom-call(f32[101,127]{1,0:T(8,128)} %convolution_bitcast_fusion.3.taps_ref, f32[228,127]{1,0:T(8,128)} %maximum_bitcast_fusion.extended_ref), custom_call_target="tpu_custom_call" | custom-call | tf_op jit(solution)/shard_map/pallas_call | solution.py:84
  16.8 0.9 pad_maximum_fusion
  17.7 0.8 copy.88
  18.5 3.6 %all-to-all-start = ((f32[254,1,128]{0,1,2:T(1,128)}), f32[254,1,128]{0,1,2:T(1,128)S(1)}, u32[]{:S(2)}, u32[]{:S(2)}) async-start(f32[254,1,128]{0,1,2:T(1,128)} %copy.88), calls=%async_computation | async-start | bytes 262144 | tf_op jit(solution)/shard_map/all_to_all | solution.py:91
  22.2 0.7 multiply_reduce_fusion.4
  23.0 0.7 multiply_reduce_fusion.5
  23.7 5.0 %all-to-all-done = f32[254,1,128]{0,1,2:T(1,128)S(1)} async-done(((f32[254,1,128]{0,1,2:T(1,128)}), f32[254,1,128]{0,1,2:T(1,128)S(1)}, u32[]{:S(2)}, u32[]{:S(2)}) %all-to-all-start) | async-done | bytes 130080 | tf_op jit(solution)/shard_map/all_to_all | solution.py:91
  29.1 0.9 multiply_reduce_fusion.3
  31.6 0.7 fusion.11
  32.4 0.7 pad_maximum_fusion.1
  33.1 3.5 %all-to-all-start.1 = ((f32[128,16,8]{0,2,1:T(8,128)}), f32[128,16,8]{0,2,1:T(8,128)S(1)}, u32[]{:S(2)}, u32[]{:S(2)}) async-start(f32[128,16,8]{0,2,1:T(8,128)} %pad_maximum_fusion.1), calls=%async_computation.1 | async-start | bytes 131072 | tf_op jit(solution)/shard_map/all_to_all | solution.py:95
  36.6 0.9 convolution_bitcast_fusion.2.taps_ref
  37.6 5.4 %all-to-all-done.1 = f32[128,16,8]{0,2,1:T(8,128)S(1)} async-done(((f32[128,16,8]{0,2,1:T(8,128)}), f32[128,16,8]{0,2,1:T(8,128)S(1)}, u32[]{:S(2)}, u32[]{:S(2)}) %all-to-all-start.1) | async-done | bytes 65568 | tf_op jit(solution)/shard_map/all_to_all | solution.py:95
  44.0 18.9 %all-to-all-start.2 = ((f32[32,1,2]{2,1,0:T(1,128)}), f32[32,1,2]{2,1,0:T(1,128)S(1)}, u32[]{:S(2)}, u32[]{:S(2)}) async-start(f32[32,1,2]{2,1,0:T(1,128)} %broadcast_in_dim.20), calls=%async_computation.2 | async-start | bytes 32768 | tf_op jit(solution)/shard_map/all_to_all | solution.py:113
  62.9 1.6 %collective-permute-start.2 = (f32[127,1,50]{0,2,1:T(8,128)S(1)}, f32[127,1,50]{0,2,1:T(8,128)S(1)}, u32[]{:S(2)}, u32[]{:S(2)}) collective-permute-start(f32[127,1,50]{0,2,1:T(8,128)S(1)} %get-tuple-element.36), channel_id=1, source_target_pairs={{0,16},{16,32},{32,48},{48,64},{64,80},{80,96},{96,112},{112,128},... | collective-permute-start | bytes 76208 | tf_op jit(solution)/shard_map/ppermute | solution.py:23
  64.6 10.1 %all-to-all-done.2 = f32[32,1,2]{2,1,0:T(1,128)S(1)} async-done(((f32[32,1,2]{2,1,0:T(1,128)}), f32[32,1,2]{2,1,0:T(1,128)S(1)}, u32[]{:S(2)}, u32[]{:S(2)}) %all-to-all-start.2) | async-done | bytes 288 | tf_op jit(solution)/shard_map/all_to_all | solution.py:113
  77.3 2.1 %shard_map.104 = f32[128,127]{1,0:T(8,128)} custom-call(f32[101,127]{1,0:T(8,128)} %convolution_bitcast_fusion.2.taps_ref, f32[228,127]{1,0:T(8,128)} %maximum_bitcast_fusion.1.extended_ref), custom_call_target="tpu_custom_call" | custom-call | tf_op jit(solution)/shard_map/pallas_call | solution.py:84
  79.4 0.8 bitcast_add_fusion
  80.9 0.7 broadcast_in_dim.21
  81.6 9.4 %all_to_all.36 = f32[16,1,1]{2,1,0:T(1,128)S(1)} all-to-all(f32[16,1,1]{2,1,0:T(1,128)S(1)} %broadcast_in_dim.21), channel_id=1, replica_groups=mesh['lon'=32,'lat'=16] {'lat'}, dimensions={0} | all-to-all | bytes 128 | tf_op jit(solution)/shard_map/all_to_all | solution.py:113
  91.5 1.3 %broadcast_in_dim.22 = f32[32,1,1]{2,1,0:T(1,128)} broadcast(f32[]{:T(128)} %reduce_sum.108), dimensions={} | broadcast | bytes 132 | tf_op jit(solution)/shard_map/broadcast_in_dim | solution.py:113
  92.8 5.8 %all-to-all-start.4 = ((f32[32,1,1]{2,1,0:T(1,128)}), f32[32,1,1]{2,1,0:T(1,128)S(1)}, u32[]{:S(2)}, u32[]{:S(2)}) async-start(f32[32,1,1]{2,1,0:T(1,128)} %broadcast_in_dim.22), calls=%async_computation.4 | async-start | bytes 32768 | tf_op jit(solution)/shard_map/all_to_all | solution.py:113
  98.7 0.7 copy.100
  99.5 11.0 %all-to-all-done.4 = f32[32,1,1]{2,1,0:T(1,128)S(1)} async-done(((f32[32,1,1]{2,1,0:T(1,128)}), f32[32,1,1]{2,1,0:T(1,128)S(1)}, u32[]{:S(2)}, u32[]{:S(2)}) %all-to-all-start.4) | async-done | bytes 160 | tf_op jit(solution)/shard_map/all_to_all | solution.py:113
  112.4 0.7 copy.101
  113.1 0.7 copy.99
  (57 shorter events, 8.9 us)
Async XLA Ops:
  0.6 28.5 %copy-start = (f32[127,127]{1,0:T(8,128)S(1)}, f32[127,127]{1,0:T(8,128)}, u32[]{:S(2)}) copy-start(f32[127,127]{1,0:T(8,128)} %param.14) | copy-start | bytes 193552
  1.6 12.4 %collective-permute-start = (f32[127,1,50]{0,2,1:T(8,128)S(1)}, f32[127,1,50]{0,2,1:T(8,128)S(1)}, u32[]{:S(2)}, u32[]{:S(2)}) collective-permute-start(f32[127,1,50]{0,2,1:T(8,128)S(1)} %get-tuple-element.38), channel_id=1, source_target_pairs={{0,16},{16,32},{32,48},{48,64},{64,80},{80,96},{96,112},{112,128},... | collective-permute-start | bytes 76208 | tf_op jit(solution)/shard_map/ppermute | solution.py:23
  4.7 9.4 %collective-permute-start.1 = (f32[127,1,50]{0,2,1:T(8,128)S(1)}, f32[127,1,50]{0,2,1:T(8,128)S(1)}, u32[]{:S(2)}, u32[]{:S(2)}) collective-permute-start(f32[127,1,50]{0,2,1:T(8,128)S(1)} %get-tuple-element.39), channel_id=1, source_target_pairs={{16,0},{32,16},{48,32},{64,48},{80,64},{96,80},{112,96},{128,112},... | collective-permute-start | bytes 76208 | tf_op jit(solution)/shard_map/ppermute | solution.py:25
  8.6 0.7 copy-start.7
  9.4 0.7 copy-start.3
  12.3 0.7 copy-start.4
  13.0 0.9 copy-start.5
  18.5 3.7 %copy-start.1 = (f32[127,1,128]{2,1,0:T(1,128)S(1)}, f32[127,1,128]{2,1,0:T(1,128)}, u32[]{:S(2)}) copy-start(f32[127,1,128]{2,1,0:T(1,128)} %param.12) | copy-start | bytes 195076
  18.5 10.3 %all-to-all-start = ((f32[254,1,128]{0,1,2:T(1,128)}), f32[254,1,128]{0,1,2:T(1,128)S(1)}, u32[]{:S(2)}, u32[]{:S(2)}) async-start(f32[254,1,128]{0,1,2:T(1,128)} %copy.88), calls=%async_computation | async-start | bytes 262144 | tf_op jit(solution)/shard_map/all_to_all | solution.py:91
  22.2 0.8 copy-start.2
  33.1 10.0 %all-to-all-start.1 = ((f32[128,16,8]{0,2,1:T(8,128)}), f32[128,16,8]{0,2,1:T(8,128)S(1)}, u32[]{:S(2)}, u32[]{:S(2)}) async-start(f32[128,16,8]{0,2,1:T(8,128)} %pad_maximum_fusion.1), calls=%async_computation.1 | async-start | bytes 131072 | tf_op jit(solution)/shard_map/all_to_all | solution.py:95
  44.0 30.7 %all-to-all-start.2 = ((f32[32,1,2]{2,1,0:T(1,128)}), f32[32,1,2]{2,1,0:T(1,128)S(1)}, u32[]{:S(2)}, u32[]{:S(2)}) async-start(f32[32,1,2]{2,1,0:T(1,128)} %broadcast_in_dim.20), calls=%async_computation.2 | async-start | bytes 32768 | tf_op jit(solution)/shard_map/all_to_all | solution.py:113
  62.9 13.8 %collective-permute-start.2 = (f32[127,1,50]{0,2,1:T(8,128)S(1)}, f32[127,1,50]{0,2,1:T(8,128)S(1)}, u32[]{:S(2)}, u32[]{:S(2)}) collective-permute-start(f32[127,1,50]{0,2,1:T(8,128)S(1)} %get-tuple-element.36), channel_id=1, source_target_pairs={{0,16},{16,32},{32,48},{48,64},{64,80},{80,96},{96,112},{112,128},... | collective-permute-start | bytes 76208 | tf_op jit(solution)/shard_map/ppermute | solution.py:23
  64.6 12.1 %collective-permute-start.3 = (f32[127,1,50]{0,2,1:T(8,128)S(1)}, f32[127,1,50]{0,2,1:T(8,128)S(1)}, u32[]{:S(2)}, u32[]{:S(2)}) collective-permute-start(f32[127,1,50]{0,2,1:T(8,128)S(1)} %get-tuple-element.37), channel_id=1, source_target_pairs={{16,0},{32,16},{48,32},{64,48},{80,64},{96,80},{112,96},{128,112},... | collective-permute-start | bytes 76208 | tf_op jit(solution)/shard_map/ppermute | solution.py:25
  80.9 17.7 %copy-start.6 = (f32[127,1,128]{2,1,0:T(1,128)S(1)}, f32[127,1,128]{2,1,0:T(1,128)}, u32[]{:S(2)}) copy-start(f32[127,1,128]{2,1,0:T(1,128)} %param.10) | copy-start | bytes 195076
  92.8 17.6 %all-to-all-start.4 = ((f32[32,1,1]{2,1,0:T(1,128)}), f32[32,1,1]{2,1,0:T(1,128)S(1)}, u32[]{:S(2)}, u32[]{:S(2)}) async-start(f32[32,1,1]{2,1,0:T(1,128)} %broadcast_in_dim.22), calls=%async_computation.4 | async-start | bytes 32768 | tf_op jit(solution)/shard_map/all_to_all | solution.py:113

commit v6 on v5

--- a/solution.py
+++ b/solution.py
@@ -95,10 +95,9 @@
     return lax.all_to_all(grid_field, "lat", 1, 2, tiled=True)
 
 
-def lat_pass(grid_field, kernel_groups, groups, adjoint):
-    kernel = kernel_groups[:, ::-1] if adjoint else kernel_groups
-    lat_width = grid_field.shape[1]
-    matrices = band_matrices(group_rows(groups, kernel), lat_width, lat_width)
+def lat_pass(grid_field, matrices, adjoint):
+    if adjoint:
+        return jnp.sum(matrices[:, :, :, None] * grid_field[:, None, :, :], axis=2)
     return jnp.sum(matrices[:, :, :, None] * grid_field[:, :, None, :], axis=1)
 
 
@@ -121,14 +120,16 @@
     groups = jnp.sum((levels[:, None] >= bounds[None, :]).astype(jnp.int32), axis=1)
     lon_part = lon_pass(direction, lon_taps, groups, False)
     both = to_columns(jnp.concatenate([lon_part, obs_weight], axis=0))
-    lat_part = lat_pass(both[:LEV], lat_taps, groups, False)
+    lat_width = both.shape[1]
+    matrices = band_matrices(group_rows(groups, lat_taps), lat_width, lat_width)
+    lat_part = lat_pass(both[:LEV], matrices, False)
     lifted = vertical_mix(vertical, lat_part)
     weighted = both[LEV:] * lifted
     partial = jnp.stack(
         [jnp.sum(residual * residual), jnp.sum(direction * direction) + jnp.sum(weighted * lifted)]
     )
     back_vert = vertical_mix(vertical.T, weighted)
-    back_cols = lat_pass(back_vert, lat_taps, groups, True)
+    back_cols = lat_pass(back_vert, matrices, True)
     chunk = back_cols.shape[2]
     extra = jnp.zeros((1,) + back_cols.shape[1:], back_cols.dtype).at[0, :, :2].set(partial)
     returned = to_rows(jnp.concatenate([back_cols, extra], axis=0))

time: 115 us -> 114 us (level)
    dot_general x4 -> x3, matrix products: 2.37 us -> 2.09 us  [group_rows(): return jnp.dot(onehot, kernel, precision=HIGHEST)]
  transfers between devices with their start and end apart: 8 -> 8, of which waited for: 4 -> 4; matrix products, arithmetic and copies ran while one was open for 7% -> 6% of each run, Pallas kernels for 0% -> 0%
where the time goes in v6:
time: 114 us; the launch traced here: 113 us
  starting transfers between devices  40.4 us (35%)
  waiting for transfers between devices  31.6 us (28%)
  local copies, waits for them, and re-layouts  10.5 us (9%)
  blocking collectives  9.35 us (8%)
  other arithmetic  8.65 us (8%)
  between operations  4.86 us (4%)
  Pallas kernels  4.16 us (4%)
  matrix products  3.17 us (3%)
    all_to_all x2, starting transfers between devices, total(): lax.all_to_all(jnp.broadcast_to(v[None], (n,) + v.shape), axis, 0, 0, til...  24.7 us
    all_to_all x2, waiting for transfers between devices, total(): lax.all_to_all(jnp.broadcast_to(v[None], (n,) + v.shape), axis, 0, 0, til...  21.1 us
    all_to_all x1, blocking collectives, total(): lax.all_to_all(jnp.broadcast_to(v[None], (n,) + v.shape), axis, 0, 0, til...  9.35 us
    all_to_all x1, waiting for transfers between devices, to_rows(): return lax.all_to_all(grid_field, 'lat', 1, 2, tiled=True)  5.45 us
    unnamed x24, local copies, waits for them, and re-layouts  5.28 us
    all_to_all x1, waiting for transfers between devices, to_columns(): return lax.all_to_all(grid_field, 'lat', 2, 1, tiled=True)  5.05 us
    ppermute x2, starting transfers between devices, with_halo(): lax.ppermute(tail, axis, [(i, (i + 1) % count) for i in range(count)])  4.68 us
    pallas_call x2, Pallas kernels, lon_pass(): pl.pallas_call(lon_kernel, out_shape=jax.ShapeDtypeStruct((lon_width, lev...  4.16 us
  transfers between devices with their start and end apart: 8, of which 4 were waited for; matrix products, arithmetic and copies ran while one was open for 6% of the time, Pallas kernels for 0%

profile of v6, /device:TPU:1, one launch (start us, length us, event | category | flops | bytes accessed | tf_op | source)
XLA Modules:
  0.0 112.7 jit_solution(15760574803840841496)
XLA Ops:
  0.6 1.0 copy.81
  1.6 3.0 %collective-permute-start = (f32[127,1,50]{0,2,1:T(8,128)S(1)}, f32[127,1,50]{0,2,1:T(8,128)S(1)}, u32[]{:S(2)}, u32[]{:S(2)}) collective-permute-start(f32[127,1,50]{0,2,1:T(8,128)S(1)} %get-tuple-element.38), channel_id=1, source_target_pairs={{0,16},{16,32},{32,48},{48,64},{64,80},{80,96},{96,112},{112,128},... | collective-permute-start | bytes 76208 | tf_op jit(solution)/shard_map/ppermute | solution.py:23
  4.7 3.9 %collective-permute-start.1 = (f32[127,1,50]{0,2,1:T(8,128)S(1)}, f32[127,1,50]{0,2,1:T(8,128)S(1)}, u32[]{:S(2)}, u32[]{:S(2)}) collective-permute-start(f32[127,1,50]{0,2,1:T(8,128)S(1)} %get-tuple-element.39), channel_id=1, source_target_pairs={{16,0},{32,16},{48,32},{64,48},{80,64},{96,80},{112,96},{128,112},... | collective-permute-start | bytes 76208 | tf_op jit(solution)/shard_map/ppermute | solution.py:25
  10.4 0.7 gather_fusion
  11.8 0.9 convolution_bitcast_fusion.3.taps_ref
  12.9 0.7 maximum_bitcast_fusion.extended_ref
  13.5 2.1 %shard_map.103 = f32[128,127]{1,0:T(8,128)} custom-call(f32[101,127]{1,0:T(8,128)} %convolution_bitcast_fusion.3.taps_ref, f32[228,127]{1,0:T(8,128)} %maximum_bitcast_fusion.extended_ref), custom_call_target="tpu_custom_call" | custom-call | tf_op jit(solution)/shard_map/pallas_call | solution.py:84
  15.6 0.9 pad_maximum_fusion
  16.5 0.8 copy.85
  17.3 3.6 %all-to-all-start = ((f32[254,1,128]{0,1,2:T(1,128)}), f32[254,1,128]{0,1,2:T(1,128)S(1)}, u32[]{:S(2)}, u32[]{:S(2)}) async-start(f32[254,1,128]{0,1,2:T(1,128)} %copy.85), calls=%async_computation | async-start | bytes 262144 | tf_op jit(solution)/shard_map/all_to_all | solution.py:91
  21.0 0.7 multiply_reduce_fusion.4
  21.8 0.7 multiply_reduce_fusion.5
  22.5 5.0 %all-to-all-done = f32[254,1,128]{0,1,2:T(1,128)S(1)} async-done(((f32[254,1,128]{0,1,2:T(1,128)}), f32[254,1,128]{0,1,2:T(1,128)S(1)}, u32[]{:S(2)}, u32[]{:S(2)}) %all-to-all-start) | async-done | bytes 130080 | tf_op jit(solution)/shard_map/all_to_all | solution.py:91
  27.9 0.9 multiply_reduce_fusion.3
  30.4 0.7 fusion.9
  31.2 0.7 pad_maximum_fusion.1
  31.9 3.5 %all-to-all-start.1 = ((f32[128,16,8]{0,2,1:T(8,128)}), f32[128,16,8]{0,2,1:T(8,128)S(1)}, u32[]{:S(2)}, u32[]{:S(2)}) async-start(f32[128,16,8]{0,2,1:T(8,128)} %pad_maximum_fusion.1), calls=%async_computation.1 | async-start | bytes 131072 | tf_op jit(solution)/shard_map/all_to_all | solution.py:95
  35.4 0.9 convolution_bitcast_fusion.2.taps_ref
  36.4 5.5 %all-to-all-done.1 = f32[128,16,8]{0,2,1:T(8,128)S(1)} async-done(((f32[128,16,8]{0,2,1:T(8,128)}), f32[128,16,8]{0,2,1:T(8,128)S(1)}, u32[]{:S(2)}, u32[]{:S(2)}) %all-to-all-start.1) | async-done | bytes 65568 | tf_op jit(solution)/shard_map/all_to_all | solution.py:95
  42.8 18.9 %all-to-all-start.2 = ((f32[32,1,2]{2,1,0:T(1,128)}), f32[32,1,2]{2,1,0:T(1,128)S(1)}, u32[]{:S(2)}, u32[]{:S(2)}) async-start(f32[32,1,2]{2,1,0:T(1,128)} %broadcast_in_dim.18), calls=%async_computation.2 | async-start | bytes 32768 | tf_op jit(solution)/shard_map/all_to_all | solution.py:112
  61.7 1.6 %collective-permute-start.2 = (f32[127,1,50]{0,2,1:T(8,128)S(1)}, f32[127,1,50]{0,2,1:T(8,128)S(1)}, u32[]{:S(2)}, u32[]{:S(2)}) collective-permute-start(f32[127,1,50]{0,2,1:T(8,128)S(1)} %get-tuple-element.36), channel_id=1, source_target_pairs={{0,16},{16,32},{32,48},{48,64},{64,80},{80,96},{96,112},{112,128},... | collective-permute-start | bytes 76208 | tf_op jit(solution)/shard_map/ppermute | solution.py:23
  63.4 10.1 %all-to-all-done.2 = f32[32,1,2]{2,1,0:T(1,128)S(1)} async-done(((f32[32,1,2]{2,1,0:T(1,128)}), f32[32,1,2]{2,1,0:T(1,128)S(1)}, u32[]{:S(2)}, u32[]{:S(2)}) %all-to-all-start.2) | async-done | bytes 288 | tf_op jit(solution)/shard_map/all_to_all | solution.py:112
  76.2 2.1 %shard_map.104 = f32[128,127]{1,0:T(8,128)} custom-call(f32[101,127]{1,0:T(8,128)} %convolution_bitcast_fusion.2.taps_ref, f32[228,127]{1,0:T(8,128)} %maximum_bitcast_fusion.1.extended_ref), custom_call_target="tpu_custom_call" | custom-call | tf_op jit(solution)/shard_map/pallas_call | solution.py:84
  78.2 0.8 bitcast_add_fusion
  79.7 0.7 broadcast_in_dim.19
  80.4 9.4 %all_to_all.36 = f32[16,1,1]{2,1,0:T(1,128)S(1)} all-to-all(f32[16,1,1]{2,1,0:T(1,128)S(1)} %broadcast_in_dim.19), channel_id=1, replica_groups=mesh['lon'=32,'lat'=16] {'lat'}, dimensions={0} | all-to-all | bytes 128 | tf_op jit(solution)/shard_map/all_to_all | solution.py:112
  90.3 1.3 %broadcast_in_dim.20 = f32[32,1,1]{2,1,0:T(1,128)} broadcast(f32[]{:T(128)} %reduce_sum.108), dimensions={} | broadcast | bytes 132 | tf_op jit(solution)/shard_map/broadcast_in_dim | solution.py:112
  91.6 5.8 %all-to-all-start.4 = ((f32[32,1,1]{2,1,0:T(1,128)}), f32[32,1,1]{2,1,0:T(1,128)S(1)}, u32[]{:S(2)}, u32[]{:S(2)}) async-start(f32[32,1,1]{2,1,0:T(1,128)} %broadcast_in_dim.20), calls=%async_computation.4 | async-start | bytes 32768 | tf_op jit(solution)/shard_map/all_to_all | solution.py:112
  97.5 0.7 copy.97
  98.3 11.0 %all-to-all-done.4 = f32[32,1,1]{2,1,0:T(1,128)S(1)} async-done(((f32[32,1,1]{2,1,0:T(1,128)}), f32[32,1,1]{2,1,0:T(1,128)S(1)}, u32[]{:S(2)}, u32[]{:S(2)}) %all-to-all-start.4) | async-done | bytes 160 | tf_op jit(solution)/shard_map/all_to_all | solution.py:112
  111.2 0.7 copy.96
  112.0 0.7 copy.98
  (54 shorter events, 7.8 us)
Async XLA Ops:
  0.6 27.3 %copy-start = (f32[127,127]{1,0:T(8,128)S(1)}, f32[127,127]{1,0:T(8,128)}, u32[]{:S(2)}) copy-start(f32[127,127]{1,0:T(8,128)} %param.14) | copy-start | bytes 193552
  1.6 11.2 %collective-permute-start = (f32[127,1,50]{0,2,1:T(8,128)S(1)}, f32[127,1,50]{0,2,1:T(8,128)S(1)}, u32[]{:S(2)}, u32[]{:S(2)}) collective-permute-start(f32[127,1,50]{0,2,1:T(8,128)S(1)} %get-tuple-element.38), channel_id=1, source_target_pairs={{0,16},{16,32},{32,48},{48,64},{64,80},{80,96},{96,112},{112,128},... | collective-permute-start | bytes 76208 | tf_op jit(solution)/shard_map/ppermute | solution.py:23
  4.7 8.2 %collective-permute-start.1 = (f32[127,1,50]{0,2,1:T(8,128)S(1)}, f32[127,1,50]{0,2,1:T(8,128)S(1)}, u32[]{:S(2)}, u32[]{:S(2)}) collective-permute-start(f32[127,1,50]{0,2,1:T(8,128)S(1)} %get-tuple-element.39), channel_id=1, source_target_pairs={{16,0},{32,16},{48,32},{64,48},{80,64},{96,80},{112,96},{128,112},... | collective-permute-start | bytes 76208 | tf_op jit(solution)/shard_map/ppermute | solution.py:25
  8.6 0.7 copy-start.7
  9.4 0.7 copy-start.6
  11.1 0.7 copy-start.3
  11.8 0.9 copy-start.4
  17.3 3.7 %copy-start.1 = (f32[127,1,128]{2,1,0:T(1,128)S(1)}, f32[127,1,128]{2,1,0:T(1,128)}, u32[]{:S(2)}) copy-start(f32[127,1,128]{2,1,0:T(1,128)} %param.12) | copy-start | bytes 195076
  17.3 10.3 %all-to-all-start = ((f32[254,1,128]{0,1,2:T(1,128)}), f32[254,1,128]{0,1,2:T(1,128)S(1)}, u32[]{:S(2)}, u32[]{:S(2)}) async-start(f32[254,1,128]{0,1,2:T(1,128)} %copy.85), calls=%async_computation | async-start | bytes 262144 | tf_op jit(solution)/shard_map/all_to_all | solution.py:91
  21.0 0.8 copy-start.2
  31.9 10.0 %all-to-all-start.1 = ((f32[128,16,8]{0,2,1:T(8,128)}), f32[128,16,8]{0,2,1:T(8,128)S(1)}, u32[]{:S(2)}, u32[]{:S(2)}) async-start(f32[128,16,8]{0,2,1:T(8,128)} %pad_maximum_fusion.1), calls=%async_computation.1 | async-start | bytes 131072 | tf_op jit(solution)/shard_map/all_to_all | solution.py:95
  42.8 30.7 %all-to-all-start.2 = ((f32[32,1,2]{2,1,0:T(1,128)}), f32[32,1,2]{2,1,0:T(1,128)S(1)}, u32[]{:S(2)}, u32[]{:S(2)}) async-start(f32[32,1,2]{2,1,0:T(1,128)} %broadcast_in_dim.18), calls=%async_computation.2 | async-start | bytes 32768 | tf_op jit(solution)/shard_map/all_to_all | solution.py:112
  61.7 13.8 %collective-permute-start.2 = (f32[127,1,50]{0,2,1:T(8,128)S(1)}, f32[127,1,50]{0,2,1:T(8,128)S(1)}, u32[]{:S(2)}, u32[]{:S(2)}) collective-permute-start(f32[127,1,50]{0,2,1:T(8,128)S(1)} %get-tuple-element.36), channel_id=1, source_target_pairs={{0,16},{16,32},{32,48},{48,64},{64,80},{80,96},{96,112},{112,128},... | collective-permute-start | bytes 76208 | tf_op jit(solution)/shard_map/ppermute | solution.py:23
  63.4 12.1 %collective-permute-start.3 = (f32[127,1,50]{0,2,1:T(8,128)S(1)}, f32[127,1,50]{0,2,1:T(8,128)S(1)}, u32[]{:S(2)}, u32[]{:S(2)}) collective-permute-start(f32[127,1,50]{0,2,1:T(8,128)S(1)} %get-tuple-element.37), channel_id=1, source_target_pairs={{16,0},{32,16},{48,32},{64,48},{80,64},{96,80},{112,96},{128,112},... | collective-permute-start | bytes 76208 | tf_op jit(solution)/shard_map/ppermute | solution.py:25
  79.7 17.7 %copy-start.5 = (f32[127,1,128]{2,1,0:T(1,128)S(1)}, f32[127,1,128]{2,1,0:T(1,128)}, u32[]{:S(2)}) copy-start(f32[127,1,128]{2,1,0:T(1,128)} %param.10) | copy-start | bytes 195076
  91.6 17.6 %all-to-all-start.4 = ((f32[32,1,1]{2,1,0:T(1,128)}), f32[32,1,1]{2,1,0:T(1,128)S(1)}, u32[]{:S(2)}, u32[]{:S(2)}) async-start(f32[32,1,1]{2,1,0:T(1,128)} %broadcast_in_dim.20), calls=%async_computation.4 | async-start | bytes 32768 | tf_op jit(solution)/shard_map/all_to_all | solution.py:112

commit v7 on v6

--- a/solution.py
+++ b/solution.py
@@ -139,7 +139,7 @@
     applied = lax.optimization_barrier(direction + lon_pass(back_lat, lon_taps, groups, True))
     step_length = norm_old / curvature
     residual_next = residual - step_length * applied
-    (norm_new,) = total((jnp.sum(residual_next * residual_next),))
+    (norm_new,) = total((jnp.sum(residual_next * residual_next),), ("lon", "lat"))
     iterate_next = iterate + step_length * direction
     direction_next = residual_next + norm_new / norm_old * direction
     return (iterate_next, residual_next, direction_next)

time: 114 us -> 113 us (level)
  blocking collectives: 9.35 us -> 0 us
  waiting for transfers between devices: 31.6 us -> 37.9 us
  starting transfers between devices: 40.4 us -> 42.4 us
    all_to_all x1 -> x0, blocking collectives: 9.35 us -> none  [total(): lax.all_to_all(jnp.broadcast_to(v[None], (n,) + v.shape), axis, 0, 0, til...]
    all_to_all x2 -> x3, waiting for transfers between devices: 21.1 us -> 27.4 us  [total(): lax.all_to_all(jnp.broadcast_to(v[None], (n,) + v.shape), axis, 0, 0, til...]
    all_to_all x2 -> x3, starting transfers between devices: 24.7 us -> 26.7 us  [total(): lax.all_to_all(jnp.broadcast_to(v[None], (n,) + v.shape), axis, 0, 0, til...]
  transfers between devices with their start and end apart: 8 -> 9, of which waited for: 4 -> 5; matrix products, arithmetic and copies ran while one was open for 6% -> 6% of each run, Pallas kernels for 0% -> 0%
where the time goes in v7:
time: 113 us; the launch traced here: 112 us
  starting transfers between devices  42.4 us (38%)
  waiting for transfers between devices  37.9 us (34%)
  local copies, waits for them, and re-layouts  11.1 us (10%)
  other arithmetic  8.66 us (8%)
  between operations  4.87 us (4%)
  Pallas kernels  4.16 us (4%)
  matrix products  3.17 us (3%)
    all_to_all x3, waiting for transfers between devices, total(): lax.all_to_all(jnp.broadcast_to(v[None], (n,) + v.shape), axis, 0, 0, til...  27.4 us
    all_to_all x3, starting transfers between devices, total(): lax.all_to_all(jnp.broadcast_to(v[None], (n,) + v.shape), axis, 0, 0, til...  26.7 us
    all_to_all x1, waiting for transfers between devices, to_rows(): return lax.all_to_all(grid_field, 'lat', 1, 2, tiled=True)  5.45 us
    unnamed x24, local copies, waits for them, and re-layouts  5.28 us
    all_to_all x1, waiting for transfers between devices, to_columns(): return lax.all_to_all(grid_field, 'lat', 2, 1, tiled=True)  5.05 us
    ppermute x2, starting transfers between devices, with_halo(): lax.ppermute(tail, axis, [(i, (i + 1) % count) for i in range(count)])  4.68 us
    pallas_call x2, Pallas kernels, lon_pass(): pl.pallas_call(lon_kernel, out_shape=jax.ShapeDtypeStruct((lon_width, lev...  4.16 us
    ppermute x2, starting transfers between devices, with_halo(): lax.ppermute(head, axis, [((i + 1) % count, i) for i in range(count)])  3.88 us
  transfers between devices with their start and end apart: 9, of which 5 were waited for; matrix products, arithmetic and copies ran while one was open for 6% of the time, Pallas kernels for 0%

profile of v7, /device:TPU:1, one launch (start us, length us, event | category | flops | bytes accessed | tf_op | source)
XLA Modules:
  0.0 112.2 jit_solution(8485742722152506965)
XLA Ops:
  0.6 1.0 copy.81
  1.6 3.0 %collective-permute-start = (f32[127,1,50]{0,2,1:T(8,128)S(1)}, f32[127,1,50]{0,2,1:T(8,128)S(1)}, u32[]{:S(2)}, u32[]{:S(2)}) collective-permute-start(f32[127,1,50]{0,2,1:T(8,128)S(1)} %get-tuple-element.38), channel_id=1, source_target_pairs={{0,16},{16,32},{32,48},{48,64},{64,80},{80,96},{96,112},{112,128},... | collective-permute-start | bytes 76208 | tf_op jit(solution)/shard_map/ppermute | solution.py:23
  4.7 3.9 %collective-permute-start.1 = (f32[127,1,50]{0,2,1:T(8,128)S(1)}, f32[127,1,50]{0,2,1:T(8,128)S(1)}, u32[]{:S(2)}, u32[]{:S(2)}) collective-permute-start(f32[127,1,50]{0,2,1:T(8,128)S(1)} %get-tuple-element.39), channel_id=1, source_target_pairs={{16,0},{32,16},{48,32},{64,48},{80,64},{96,80},{112,96},{128,112},... | collective-permute-start | bytes 76208 | tf_op jit(solution)/shard_map/ppermute | solution.py:25
  10.4 0.7 gather_fusion
  11.8 0.9 convolution_bitcast_fusion.3.taps_ref
  13.5 2.1 %shard_map.103 = f32[128,127]{1,0:T(8,128)} custom-call(f32[101,127]{1,0:T(8,128)} %convolution_bitcast_fusion.3.taps_ref, f32[228,127]{1,0:T(8,128)} %maximum_bitcast_fusion.extended_ref), custom_call_target="tpu_custom_call" | custom-call | tf_op jit(solution)/shard_map/pallas_call | solution.py:84
  15.6 0.9 pad_maximum_fusion
  16.5 0.8 copy.85
  17.3 3.6 %all-to-all-start = ((f32[254,1,128]{0,1,2:T(1,128)}), f32[254,1,128]{0,1,2:T(1,128)S(1)}, u32[]{:S(2)}, u32[]{:S(2)}) async-start(f32[254,1,128]{0,1,2:T(1,128)} %copy.85), calls=%async_computation | async-start | bytes 262144 | tf_op jit(solution)/shard_map/all_to_all | solution.py:91
  21.0 0.7 multiply_reduce_fusion.4
  21.8 0.7 multiply_reduce_fusion.5
  22.5 5.0 %all-to-all-done = f32[254,1,128]{0,1,2:T(1,128)S(1)} async-done(((f32[254,1,128]{0,1,2:T(1,128)}), f32[254,1,128]{0,1,2:T(1,128)S(1)}, u32[]{:S(2)}, u32[]{:S(2)}) %all-to-all-start) | async-done | bytes 130080 | tf_op jit(solution)/shard_map/all_to_all | solution.py:91
  27.9 0.9 multiply_reduce_fusion.3
  30.4 0.7 fusion.9
  31.2 0.7 pad_maximum_fusion.1
  31.9 3.5 %all-to-all-start.1 = ((f32[128,16,8]{0,2,1:T(8,128)}), f32[128,16,8]{0,2,1:T(8,128)S(1)}, u32[]{:S(2)}, u32[]{:S(2)}) async-start(f32[128,16,8]{0,2,1:T(8,128)} %pad_maximum_fusion.1), calls=%async_computation.1 | async-start | bytes 131072 | tf_op jit(solution)/shard_map/all_to_all | solution.py:95
  35.4 0.9 convolution_bitcast_fusion.2.taps_ref
  36.4 5.5 %all-to-all-done.1 = f32[128,16,8]{0,2,1:T(8,128)S(1)} async-done(((f32[128,16,8]{0,2,1:T(8,128)}), f32[128,16,8]{0,2,1:T(8,128)S(1)}, u32[]{:S(2)}, u32[]{:S(2)}) %all-to-all-start.1) | async-done | bytes 65568 | tf_op jit(solution)/shard_map/all_to_all | solution.py:95
  42.8 18.9 %all-to-all-start.2 = ((f32[32,1,2]{2,1,0:T(1,128)}), f32[32,1,2]{2,1,0:T(1,128)S(1)}, u32[]{:S(2)}, u32[]{:S(2)}) async-start(f32[32,1,2]{2,1,0:T(1,128)} %broadcast_in_dim.18), calls=%async_computation.2 | async-start | bytes 32768 | tf_op jit(solution)/shard_map/all_to_all | solution.py:112
  61.7 1.6 %collective-permute-start.2 = (f32[127,1,50]{0,2,1:T(8,128)S(1)}, f32[127,1,50]{0,2,1:T(8,128)S(1)}, u32[]{:S(2)}, u32[]{:S(2)}) collective-permute-start(f32[127,1,50]{0,2,1:T(8,128)S(1)} %get-tuple-element.36), channel_id=1, source_target_pairs={{0,16},{16,32},{32,48},{48,64},{64,80},{80,96},{96,112},{112,128},... | collective-permute-start | bytes 76208 | tf_op jit(solution)/shard_map/ppermute | solution.py:23
  63.4 10.1 %all-to-all-done.2 = f32[32,1,2]{2,1,0:T(1,128)S(1)} async-done(((f32[32,1,2]{2,1,0:T(1,128)}), f32[32,1,2]{2,1,0:T(1,128)S(1)}, u32[]{:S(2)}, u32[]{:S(2)}) %all-to-all-start.2) | async-done | bytes 288 | tf_op jit(solution)/shard_map/all_to_all | solution.py:112
  76.2 2.1 %shard_map.104 = f32[128,127]{1,0:T(8,128)} custom-call(f32[101,127]{1,0:T(8,128)} %convolution_bitcast_fusion.2.taps_ref, f32[228,127]{1,0:T(8,128)} %maximum_bitcast_fusion.1.extended_ref), custom_call_target="tpu_custom_call" | custom-call | tf_op jit(solution)/shard_map/pallas_call | solution.py:84
  78.2 0.8 bitcast_add_fusion
  79.7 1.3 %broadcast_in_dim.19 = f32[32,1,1]{2,1,0:T(1,128)} broadcast(f32[]{:T(128)} %get-tuple-element.30), dimensions={} | broadcast | bytes 132 | tf_op jit(solution)/shard_map/broadcast_in_dim | solution.py:112
  81.0 4.4 %all-to-all-start.3 = ((f32[32,1,1]{2,1,0:T(1,128)}), f32[32,1,1]{2,1,0:T(1,128)S(1)}, u32[]{:S(2)}, u32[]{:S(2)}) async-start(f32[32,1,1]{2,1,0:T(1,128)} %broadcast_in_dim.19), calls=%async_computation.3 | async-start | bytes 32768 | tf_op jit(solution)/shard_map/all_to_all | solution.py:112
  85.5 11.7 %all-to-all-done.3 = f32[32,1,1]{2,1,0:T(1,128)S(1)} async-done(((f32[32,1,1]{2,1,0:T(1,128)}), f32[32,1,1]{2,1,0:T(1,128)S(1)}, u32[]{:S(2)}, u32[]{:S(2)}) %all-to-all-start.3) | async-done | bytes 160 | tf_op jit(solution)/shard_map/all_to_all | solution.py:112
  97.8 1.2 %broadcast_in_dim.20 = f32[16,1,1]{2,1,0:T(1,128)} broadcast(f32[]{:T(128)} %reduce_sum.108), dimensions={} | broadcast | bytes 68 | tf_op jit(solution)/shard_map/broadcast_in_dim | solution.py:112
  99.0 3.5 %all-to-all-start.4 = ((f32[16,1,1]{2,1,0:T(1,128)}), f32[16,1,1]{2,1,0:T(1,128)S(1)}, u32[]{:S(2)}, u32[]{:S(2)}) async-start(f32[16,1,1]{2,1,0:T(1,128)} %broadcast_in_dim.20), calls=%async_computation.4 | async-start | bytes 16384 | tf_op jit(solution)/shard_map/all_to_all | solution.py:112
  102.5 0.7 copy.97
  103.3 5.5 %all-to-all-done.4 = f32[16,1,1]{2,1,0:T(1,128)S(1)} async-done(((f32[16,1,1]{2,1,0:T(1,128)}), f32[16,1,1]{2,1,0:T(1,128)S(1)}, u32[]{:S(2)}, u32[]{:S(2)}) %all-to-all-start.4) | async-done | bytes 96 | tf_op jit(solution)/shard_map/all_to_all | solution.py:112
  110.8 0.7 copy.96
  111.5 0.7 copy.98
  (55 shorter events, 8.4 us)
Async XLA Ops:
  0.6 27.3 %copy-start = (f32[127,127]{1,0:T(8,128)S(1)}, f32[127,127]{1,0:T(8,128)}, u32[]{:S(2)}) copy-start(f32[127,127]{1,0:T(8,128)} %param.14) | copy-start | bytes 193552
  1.6 11.2 %collective-permute-start = (f32[127,1,50]{0,2,1:T(8,128)S(1)}, f32[127,1,50]{0,2,1:T(8,128)S(1)}, u32[]{:S(2)}, u32[]{:S(2)}) collective-permute-start(f32[127,1,50]{0,2,1:T(8,128)S(1)} %get-tuple-element.38), channel_id=1, source_target_pairs={{0,16},{16,32},{32,48},{48,64},{64,80},{80,96},{96,112},{112,128},... | collective-permute-start | bytes 76208 | tf_op jit(solution)/shard_map/ppermute | solution.py:23
  4.7 8.2 %collective-permute-start.1 = (f32[127,1,50]{0,2,1:T(8,128)S(1)}, f32[127,1,50]{0,2,1:T(8,128)S(1)}, u32[]{:S(2)}, u32[]{:S(2)}) collective-permute-start(f32[127,1,50]{0,2,1:T(8,128)S(1)} %get-tuple-element.39), channel_id=1, source_target_pairs={{16,0},{32,16},{48,32},{64,48},{80,64},{96,80},{112,96},{128,112},... | collective-permute-start | bytes 76208 | tf_op jit(solution)/shard_map/ppermute | solution.py:25
  8.6 0.7 copy-start.7
  9.4 0.7 copy-start.6
  11.1 0.7 copy-start.3
  11.8 0.9 copy-start.4
  17.3 3.7 %copy-start.1 = (f32[127,1,128]{2,1,0:T(1,128)S(1)}, f32[127,1,128]{2,1,0:T(1,128)}, u32[]{:S(2)}) copy-start(f32[127,1,128]{2,1,0:T(1,128)} %param.12) | copy-start | bytes 195076
  17.3 10.3 %all-to-all-start = ((f32[254,1,128]{0,1,2:T(1,128)}), f32[254,1,128]{0,1,2:T(1,128)S(1)}, u32[]{:S(2)}, u32[]{:S(2)}) async-start(f32[254,1,128]{0,1,2:T(1,128)} %copy.85), calls=%async_computation | async-start | bytes 262144 | tf_op jit(solution)/shard_map/all_to_all | solution.py:91
  21.0 0.8 copy-start.2
  31.9 10.0 %all-to-all-start.1 = ((f32[128,16,8]{0,2,1:T(8,128)}), f32[128,16,8]{0,2,1:T(8,128)S(1)}, u32[]{:S(2)}, u32[]{:S(2)}) async-start(f32[128,16,8]{0,2,1:T(8,128)} %pad_maximum_fusion.1), calls=%async_computation.1 | async-start | bytes 131072 | tf_op jit(solution)/shard_map/all_to_all | solution.py:95
  42.8 30.7 %all-to-all-start.2 = ((f32[32,1,2]{2,1,0:T(1,128)}), f32[32,1,2]{2,1,0:T(1,128)S(1)}, u32[]{:S(2)}, u32[]{:S(2)}) async-start(f32[32,1,2]{2,1,0:T(1,128)} %broadcast_in_dim.18), calls=%async_computation.2 | async-start | bytes 32768 | tf_op jit(solution)/shard_map/all_to_all | solution.py:112
  61.7 13.8 %collective-permute-start.2 = (f32[127,1,50]{0,2,1:T(8,128)S(1)}, f32[127,1,50]{0,2,1:T(8,128)S(1)}, u32[]{:S(2)}, u32[]{:S(2)}) collective-permute-start(f32[127,1,50]{0,2,1:T(8,128)S(1)} %get-tuple-element.36), channel_id=1, source_target_pairs={{0,16},{16,32},{32,48},{48,64},{64,80},{80,96},{96,112},{112,128},... | collective-permute-start | bytes 76208 | tf_op jit(solution)/shard_map/ppermute | solution.py:23
  63.4 12.1 %collective-permute-start.3 = (f32[127,1,50]{0,2,1:T(8,128)S(1)}, f32[127,1,50]{0,2,1:T(8,128)S(1)}, u32[]{:S(2)}, u32[]{:S(2)}) collective-permute-start(f32[127,1,50]{0,2,1:T(8,128)S(1)} %get-tuple-element.37), channel_id=1, source_target_pairs={{16,0},{32,16},{48,32},{64,48},{80,64},{96,80},{112,96},{128,112},... | collective-permute-start | bytes 76208 | tf_op jit(solution)/shard_map/ppermute | solution.py:25
  79.1 6.3 %copy-start.5 = (f32[127,1,128]{2,1,0:T(1,128)S(1)}, f32[127,1,128]{2,1,0:T(1,128)}, u32[]{:S(2)}) copy-start(f32[127,1,128]{2,1,0:T(1,128)} %param.10) | copy-start | bytes 195076
  81.0 16.2 %all-to-all-start.3 = ((f32[32,1,1]{2,1,0:T(1,128)}), f32[32,1,1]{2,1,0:T(1,128)S(1)}, u32[]{:S(2)}, u32[]{:S(2)}) async-start(f32[32,1,1]{2,1,0:T(1,128)} %broadcast_in_dim.19), calls=%async_computation.3 | async-start | bytes 32768 | tf_op jit(solution)/shard_map/all_to_all | solution.py:112
  99.0 9.8 %all-to-all-start.4 = ((f32[16,1,1]{2,1,0:T(1,128)}), f32[16,1,1]{2,1,0:T(1,128)S(1)}, u32[]{:S(2)}, u32[]{:S(2)}) async-start(f32[16,1,1]{2,1,0:T(1,128)} %broadcast_in_dim.20), calls=%async_computation.4 | async-start | bytes 16384 | tf_op jit(solution)/shard_map/all_to_all | solution.py:112

commit v8 on v7

--- a/solution.py
+++ b/solution.py
@@ -76,14 +76,13 @@
     out_ref[...] = total_sum
 
 
-def lon_pass(grid_field, kernel_groups, groups, adjoint):
-    kernel = kernel_groups[:, ::-1] if adjoint else kernel_groups
+def lon_pass(grid_field, taps_t, adjoint):
+    taps_t = taps_t[::-1] if adjoint else taps_t
     levels, rows, lon_width = grid_field.shape
-    kernels = jnp.repeat(group_rows(groups, kernel), rows, axis=0)
     extended = with_halo(grid_field, (("lon", 2),), HALF)
     filtered = pl.pallas_call(
         lon_kernel, out_shape=jax.ShapeDtypeStruct((lon_width, levels * rows), grid_field.dtype)
-    )(kernels.T, extended.reshape(levels * rows, -1).T)
+    )(taps_t, extended.reshape(levels * rows, -1).T)
     return filtered.T.reshape(levels, rows, lon_width)
 
 
@@ -118,7 +117,9 @@
     bounds = jnp.cumsum(band_sizes)
     levels = jnp.arange(LEV, dtype=jnp.int32)
     groups = jnp.sum((levels[:, None] >= bounds[None, :]).astype(jnp.int32), axis=1)
-    lon_part = lon_pass(direction, lon_taps, groups, False)
+    rows = direction.shape[1]
+    lon_t = jnp.repeat(group_rows(groups, lon_taps), rows, axis=0).T
+    lon_part = lon_pass(direction, lon_t, False)
     both = to_columns(jnp.concatenate([lon_part, obs_weight], axis=0))
     lat_width = both.shape[1]
     matrices = band_matrices(group_rows(groups, lat_taps), lat_width, lat_width)
@@ -136,7 +137,7 @@
     back_lat = returned[:LEV]
     lat_sums = jnp.sum(returned[LEV, 0].reshape(-1, chunk)[:, :2], axis=0)
     norm_old, curvature = total((lat_sums[0], lat_sums[1]), ("lon",))
-    applied = lax.optimization_barrier(direction + lon_pass(back_lat, lon_taps, groups, True))
+    applied = lax.optimization_barrier(direction + lon_pass(back_lat, lon_t, True))
     step_length = norm_old / curvature
     residual_next = residual - step_length * applied
     (norm_new,) = total((jnp.sum(residual_next * residual_next),), ("lon", "lat"))

time: 113 us -> 113 us (level)
    unnamed x24 -> x26, local copies, waits for them, and re-layouts: 5.28 us -> 5.35 us
where the time goes in v8:
time: 113 us; the launch traced here: 112 us
  starting transfers between devices  42.5 us (38%)
  waiting for transfers between devices  38.1 us (34%)
  local copies, waits for them, and re-layouts  11.8 us (10%)
  other arithmetic  8.56 us (8%)
  between operations  4.87 us (4%)
  Pallas kernels  4.16 us (4%)
  matrix products  2.26 us (2%)
    all_to_all x3, waiting for transfers between devices, total(): lax.all_to_all(jnp.broadcast_to(v[None], (n,) + v.shape), axis, 0, 0, til...  27.4 us
    all_to_all x3, starting transfers between devices, total(): lax.all_to_all(jnp.broadcast_to(v[None], (n,) + v.shape), axis, 0, 0, til...  26.7 us
    all_to_all x1, waiting for transfers between devices, to_rows(): return lax.all_to_all(grid_field, 'lat', 1, 2, tiled=True)  5.71 us
    unnamed x26, local copies, waits for them, and re-layouts  5.35 us
    all_to_all x1, waiting for transfers between devices, to_columns(): return lax.all_to_all(grid_field, 'lat', 2, 1, tiled=True)  5.05 us
    ppermute x2, starting transfers between devices, with_halo(): lax.ppermute(tail, axis, [(i, (i + 1) % count) for i in range(count)])  4.68 us
    pallas_call x2, Pallas kernels, lon_pass(): pl.pallas_call(lon_kernel, out_shape=jax.ShapeDtypeStruct((lon_width, lev...  4.16 us
    ppermute x2, starting transfers between devices, with_halo(): lax.ppermute(head, axis, [((i + 1) % count, i) for i in range(count)])  3.88 us
  transfers between devices with their start and end apart: 9, of which 5 were waited for; matrix products, arithmetic and copies ran while one was open for 6% of the time, Pallas kernels for 0%

profile of v8, /device:TPU:1, one launch (start us, length us, event | category | flops | bytes accessed | tf_op | source)
XLA Modules:
  0.0 112.3 jit_solution(1027391149648017862)
XLA Ops:
  0.6 1.0 copy.81
  1.6 3.0 %collective-permute-start = (f32[127,1,50]{0,2,1:T(8,128)S(1)}, f32[127,1,50]{0,2,1:T(8,128)S(1)}, u32[]{:S(2)}, u32[]{:S(2)}) collective-permute-start(f32[127,1,50]{0,2,1:T(8,128)S(1)} %get-tuple-element.38), channel_id=1, source_target_pairs={{0,16},{16,32},{32,48},{48,64},{64,80},{80,96},{96,112},{112,128},... | collective-permute-start | bytes 76208 | tf_op jit(solution)/shard_map/ppermute | solution.py:23
  4.7 3.9 %collective-permute-start.1 = (f32[127,1,50]{0,2,1:T(8,128)S(1)}, f32[127,1,50]{0,2,1:T(8,128)S(1)}, u32[]{:S(2)}, u32[]{:S(2)}) collective-permute-start(f32[127,1,50]{0,2,1:T(8,128)S(1)} %get-tuple-element.39), channel_id=1, source_target_pairs={{16,0},{32,16},{48,32},{64,48},{80,64},{96,80},{112,96},{128,112},... | collective-permute-start | bytes 76208 | tf_op jit(solution)/shard_map/ppermute | solution.py:25
  10.4 0.7 gather_fusion
  11.8 0.9 convolution_bitcast_fusion.2.taps_ref
  12.9 0.7 maximum_bitcast_fusion.extended_ref
  13.5 2.1 %shard_map.103 = f32[128,127]{1,0:T(8,128)} custom-call(f32[101,127]{1,0:T(8,128)} %convolution_bitcast_fusion.2.taps_ref, f32[228,127]{1,0:T(8,128)} %maximum_bitcast_fusion.extended_ref), custom_call_target="tpu_custom_call" | custom-call | tf_op jit(solution)/shard_map/pallas_call | solution.py:83
  15.6 0.9 pad_maximum_fusion
  16.5 0.8 copy.85
  17.3 3.6 %all-to-all-start = ((f32[254,1,128]{0,1,2:T(1,128)}), f32[254,1,128]{0,1,2:T(1,128)S(1)}, u32[]{:S(2)}, u32[]{:S(2)}) async-start(f32[254,1,128]{0,1,2:T(1,128)} %copy.85), calls=%async_computation | async-start | bytes 262144 | tf_op jit(solution)/shard_map/all_to_all | solution.py:90
  21.0 0.7 multiply_reduce_fusion.4
  21.8 0.7 multiply_reduce_fusion.5
  22.5 5.1 %all-to-all-done = f32[254,1,128]{0,1,2:T(1,128)S(1)} async-done(((f32[254,1,128]{0,1,2:T(1,128)}), f32[254,1,128]{0,1,2:T(1,128)S(1)}, u32[]{:S(2)}, u32[]{:S(2)}) %all-to-all-start) | async-done | bytes 130080 | tf_op jit(solution)/shard_map/all_to_all | solution.py:90
  27.9 0.9 multiply_reduce_fusion.3
  31.1 0.7 pad_maximum_fusion.1
  31.8 3.6 %all-to-all-start.1 = ((f32[128,16,8]{0,2,1:T(8,128)}), f32[128,16,8]{0,2,1:T(8,128)S(1)}, u32[]{:S(2)}, u32[]{:S(2)}) async-start(f32[128,16,8]{0,2,1:T(8,128)} %pad_maximum_fusion.1), calls=%async_computation.1 | async-start | bytes 131072 | tf_op jit(solution)/shard_map/all_to_all | solution.py:94
  36.2 5.7 %all-to-all-done.1 = f32[128,16,8]{0,2,1:T(8,128)S(1)} async-done(((f32[128,16,8]{0,2,1:T(8,128)}), f32[128,16,8]{0,2,1:T(8,128)S(1)}, u32[]{:S(2)}, u32[]{:S(2)}) %all-to-all-start.1) | async-done | bytes 65568 | tf_op jit(solution)/shard_map/all_to_all | solution.py:94
  42.9 18.9 %all-to-all-start.2 = ((f32[32,1,2]{2,1,0:T(1,128)}), f32[32,1,2]{2,1,0:T(1,128)S(1)}, u32[]{:S(2)}, u32[]{:S(2)}) async-start(f32[32,1,2]{2,1,0:T(1,128)} %broadcast_in_dim.18), calls=%async_computation.2 | async-start | bytes 32768 | tf_op jit(solution)/shard_map/all_to_all | solution.py:111
  61.8 1.6 %collective-permute-start.2 = (f32[127,1,50]{0,2,1:T(8,128)S(1)}, f32[127,1,50]{0,2,1:T(8,128)S(1)}, u32[]{:S(2)}, u32[]{:S(2)}) collective-permute-start(f32[127,1,50]{0,2,1:T(8,128)S(1)} %get-tuple-element.36), channel_id=1, source_target_pairs={{0,16},{16,32},{32,48},{48,64},{64,80},{80,96},{96,112},{112,128},... | collective-permute-start | bytes 76208 | tf_op jit(solution)/shard_map/ppermute | solution.py:23
  63.4 10.1 %all-to-all-done.2 = f32[32,1,2]{2,1,0:T(1,128)S(1)} async-done(((f32[32,1,2]{2,1,0:T(1,128)}), f32[32,1,2]{2,1,0:T(1,128)S(1)}, u32[]{:S(2)}, u32[]{:S(2)}) %all-to-all-start.2) | async-done | bytes 288 | tf_op jit(solution)/shard_map/all_to_all | solution.py:111
  75.5 0.7 maximum_bitcast_fusion.1.extended_ref
  76.2 2.1 %shard_map.104 = f32[128,127]{1,0:T(8,128)} custom-call(f32[101,127]{1,0:T(8,128)} %rev.3.taps_ref, f32[228,127]{1,0:T(8,128)} %maximum_bitcast_fusion.1.extended_ref), custom_call_target="tpu_custom_call" | custom-call | tf_op jit(solution)/shard_map/pallas_call | solution.py:83
  78.3 0.8 bitcast_add_fusion
  79.8 1.3 %broadcast_in_dim.19 = f32[32,1,1]{2,1,0:T(1,128)} broadcast(f32[]{:T(128)} %get-tuple-element.30), dimensions={} | broadcast | bytes 132 | tf_op jit(solution)/shard_map/broadcast_in_dim | solution.py:111
  81.0 4.4 %all-to-all-start.3 = ((f32[32,1,1]{2,1,0:T(1,128)}), f32[32,1,1]{2,1,0:T(1,128)S(1)}, u32[]{:S(2)}, u32[]{:S(2)}) async-start(f32[32,1,1]{2,1,0:T(1,128)} %broadcast_in_dim.19), calls=%async_computation.3 | async-start | bytes 32768 | tf_op jit(solution)/shard_map/all_to_all | solution.py:111
  85.5 11.7 %all-to-all-done.3 = f32[32,1,1]{2,1,0:T(1,128)S(1)} async-done(((f32[32,1,1]{2,1,0:T(1,128)}), f32[32,1,1]{2,1,0:T(1,128)S(1)}, u32[]{:S(2)}, u32[]{:S(2)}) %all-to-all-start.3) | async-done | bytes 160 | tf_op jit(solution)/shard_map/all_to_all | solution.py:111
  97.8 1.2 %broadcast_in_dim.20 = f32[16,1,1]{2,1,0:T(1,128)} broadcast(f32[]{:T(128)} %reduce_sum.108), dimensions={} | broadcast | bytes 68 | tf_op jit(solution)/shard_map/broadcast_in_dim | solution.py:111
  99.1 3.5 %all-to-all-start.4 = ((f32[16,1,1]{2,1,0:T(1,128)}), f32[16,1,1]{2,1,0:T(1,128)S(1)}, u32[]{:S(2)}, u32[]{:S(2)}) async-start(f32[16,1,1]{2,1,0:T(1,128)} %broadcast_in_dim.20), calls=%async_computation.4 | async-start | bytes 16384 | tf_op jit(solution)/shard_map/all_to_all | solution.py:111
  102.6 0.7 copy.97
  103.3 5.5 %all-to-all-done.4 = f32[16,1,1]{2,1,0:T(1,128)S(1)} async-done(((f32[16,1,1]{2,1,0:T(1,128)}), f32[16,1,1]{2,1,0:T(1,128)S(1)}, u32[]{:S(2)}, u32[]{:S(2)}) %all-to-all-start.4) | async-done | bytes 96 | tf_op jit(solution)/shard_map/all_to_all | solution.py:111
  110.8 0.7 copy.96
  111.6 0.7 copy.98
  (56 shorter events, 8.4 us)
Async XLA Ops:
  0.6 27.3 %copy-start = (f32[127,127]{1,0:T(8,128)S(1)}, f32[127,127]{1,0:T(8,128)}, u32[]{:S(2)}) copy-start(f32[127,127]{1,0:T(8,128)} %param.14) | copy-start | bytes 193552
  1.6 11.2 %collective-permute-start = (f32[127,1,50]{0,2,1:T(8,128)S(1)}, f32[127,1,50]{0,2,1:T(8,128)S(1)}, u32[]{:S(2)}, u32[]{:S(2)}) collective-permute-start(f32[127,1,50]{0,2,1:T(8,128)S(1)} %get-tuple-element.38), channel_id=1, source_target_pairs={{0,16},{16,32},{32,48},{48,64},{64,80},{80,96},{96,112},{112,128},... | collective-permute-start | bytes 76208 | tf_op jit(solution)/shard_map/ppermute | solution.py:23
  4.7 8.2 %collective-permute-start.1 = (f32[127,1,50]{0,2,1:T(8,128)S(1)}, f32[127,1,50]{0,2,1:T(8,128)S(1)}, u32[]{:S(2)}, u32[]{:S(2)}) collective-permute-start(f32[127,1,50]{0,2,1:T(8,128)S(1)} %get-tuple-element.39), channel_id=1, source_target_pairs={{16,0},{32,16},{48,32},{64,48},{80,64},{96,80},{112,96},{128,112},... | collective-permute-start | bytes 76208 | tf_op jit(solution)/shard_map/ppermute | solution.py:25
  8.6 0.7 copy-start.8
  9.4 0.7 copy-start.6
  11.1 0.7 copy-start.7
  11.8 0.9 copy-start.4
  17.3 3.7 %copy-start.2 = (f32[127,1,128]{2,1,0:T(1,128)S(1)}, f32[127,1,128]{2,1,0:T(1,128)}, u32[]{:S(2)}) copy-start(f32[127,1,128]{2,1,0:T(1,128)} %param.12) | copy-start | bytes 195076
  17.3 10.3 %all-to-all-start = ((f32[254,1,128]{0,1,2:T(1,128)}), f32[254,1,128]{0,1,2:T(1,128)S(1)}, u32[]{:S(2)}, u32[]{:S(2)}) async-start(f32[254,1,128]{0,1,2:T(1,128)} %copy.85), calls=%async_computation | async-start | bytes 262144 | tf_op jit(solution)/shard_map/all_to_all | solution.py:90
  21.0 0.8 copy-start.3
  31.8 3.6 %copy-start.1 = (f32[101,127]{1,0:T(8,128)S(1)}, f32[101,127]{1,0:T(8,128)}, u32[]{:S(2)}) copy-start(f32[101,127]{1,0:T(8,128)} %convolution_bitcast_fusion.2.taps_ref) | copy-start | bytes 153928
  31.8 10.1 %all-to-all-start.1 = ((f32[128,16,8]{0,2,1:T(8,128)}), f32[128,16,8]{0,2,1:T(8,128)S(1)}, u32[]{:S(2)}, u32[]{:S(2)}) async-start(f32[128,16,8]{0,2,1:T(8,128)} %pad_maximum_fusion.1), calls=%async_computation.1 | async-start | bytes 131072 | tf_op jit(solution)/shard_map/all_to_all | solution.py:94
  42.9 30.7 %all-to-all-start.2 = ((f32[32,1,2]{2,1,0:T(1,128)}), f32[32,1,2]{2,1,0:T(1,128)S(1)}, u32[]{:S(2)}, u32[]{:S(2)}) async-start(f32[32,1,2]{2,1,0:T(1,128)} %broadcast_in_dim.18), calls=%async_computation.2 | async-start | bytes 32768 | tf_op jit(solution)/shard_map/all_to_all | solution.py:111
  61.8 13.8 %collective-permute-start.2 = (f32[127,1,50]{0,2,1:T(8,128)S(1)}, f32[127,1,50]{0,2,1:T(8,128)S(1)}, u32[]{:S(2)}, u32[]{:S(2)}) collective-permute-start(f32[127,1,50]{0,2,1:T(8,128)S(1)} %get-tuple-element.36), channel_id=1, source_target_pairs={{0,16},{16,32},{32,48},{48,64},{64,80},{80,96},{96,112},{112,128},... | collective-permute-start | bytes 76208 | tf_op jit(solution)/shard_map/ppermute | solution.py:23
  63.4 12.1 %collective-permute-start.3 = (f32[127,1,50]{0,2,1:T(8,128)S(1)}, f32[127,1,50]{0,2,1:T(8,128)S(1)}, u32[]{:S(2)}, u32[]{:S(2)}) collective-permute-start(f32[127,1,50]{0,2,1:T(8,128)S(1)} %get-tuple-element.37), channel_id=1, source_target_pairs={{16,0},{32,16},{48,32},{64,48},{80,64},{96,80},{112,96},{128,112},... | collective-permute-start | bytes 76208 | tf_op jit(solution)/shard_map/ppermute | solution.py:25
  79.1 6.3 %copy-start.5 = (f32[127,1,128]{2,1,0:T(1,128)S(1)}, f32[127,1,128]{2,1,0:T(1,128)}, u32[]{:S(2)}) copy-start(f32[127,1,128]{2,1,0:T(1,128)} %param.10) | copy-start | bytes 195076
  81.0 16.2 %all-to-all-start.3 = ((f32[32,1,1]{2,1,0:T(1,128)}), f32[32,1,1]{2,1,0:T(1,128)S(1)}, u32[]{:S(2)}, u32[]{:S(2)}) async-start(f32[32,1,1]{2,1,0:T(1,128)} %broadcast_in_dim.19), calls=%async_computation.3 | async-start | bytes 32768 | tf_op jit(solution)/shard_map/all_to_all | solution.py:111
  99.1 9.8 %all-to-all-start.4 = ((f32[16,1,1]{2,1,0:T(1,128)}), f32[16,1,1]{2,1,0:T(1,128)S(1)}, u32[]{:S(2)}, u32[]{:S(2)}) async-start(f32[16,1,1]{2,1,0:T(1,128)} %broadcast_in_dim.20), calls=%async_computation.4 | async-start | bytes 16384 | tf_op jit(solution)/shard_map/all_to_all | solution.py:111

commit v9 on v6

--- a/solution.py
+++ b/solution.py
@@ -76,6 +76,28 @@
     out_ref[...] = total_sum
 
 
+def lon_add_kernel(taps_ref, extended_ref, base_ref, out_ref):
+    width = out_ref.shape[1]
+    total_sum = taps_ref[0:1, :] * extended_ref[0:width, :]
+    for shift_tap in range(1, TAPS):
+        total_sum = total_sum + taps_ref[shift_tap : shift_tap + 1, :] * extended_ref[
+            shift_tap : shift_tap + width, :
+        ]
+    out_ref[...] = base_ref[...] + total_sum.T
+
+
+def lon_pass_add(grid_field, base, kernel_groups, groups):
+    kernel = kernel_groups[:, ::-1]
+    levels, rows, lon_width = grid_field.shape
+    kernels = jnp.repeat(group_rows(groups, kernel), rows, axis=0)
+    extended = with_halo(grid_field, (("lon", 2),), HALF)
+    filtered = pl.pallas_call(
+        lon_add_kernel,
+        out_shape=jax.ShapeDtypeStruct((levels * rows, lon_width), grid_field.dtype),
+    )(kernels.T, extended.reshape(levels * rows, -1).T, base.reshape(levels * rows, lon_width))
+    return filtered.reshape(levels, rows, lon_width)
+
+
 def lon_pass(grid_field, kernel_groups, groups, adjoint):
     kernel = kernel_groups[:, ::-1] if adjoint else kernel_groups
     levels, rows, lon_width = grid_field.shape
@@ -136,7 +158,7 @@
     back_lat = returned[:LEV]
     lat_sums = jnp.sum(returned[LEV, 0].reshape(-1, chunk)[:, :2], axis=0)
     norm_old, curvature = total((lat_sums[0], lat_sums[1]), ("lon",))
-    applied = lax.optimization_barrier(direction + lon_pass(back_lat, lon_taps, groups, True))
+    applied = lon_pass_add(back_lat, direction, lon_taps, groups)
     step_length = norm_old / curvature
     residual_next = residual - step_length * applied
     (norm_new,) = total((jnp.sum(residual_next * residual_next),))

time: 114 us -> 113 us (level)
    pallas_call x2 -> x1, Pallas kernels: 4.16 us -> 2.08 us  [lon_pass(): pl.pallas_call(lon_kernel, out_shape=jax.ShapeDtypeStruct((lon_width, lev...]
    pallas_call x0 -> x1, Pallas kernels: none -> 2.06 us  [lon_pass_add(): pl.pallas_call(lon_add_kernel, out_shape=jax.ShapeDtypeStruct((levels * r...]
    unnamed x24 -> x22, local copies, waits for them, and re-layouts: 5.28 us -> 4.91 us
  transfers between devices with their start and end apart: 8 -> 8, of which waited for: 4 -> 4; matrix products, arithmetic and copies ran while one was open for 6% -> 7% of each run, Pallas kernels for 0% -> 0%
where the time goes in v9:
time: 113 us; the launch traced here: 112 us
  starting transfers between devices  40.4 us (36%)
  waiting for transfers between devices  30.5 us (27%)
  local copies, waits for them, and re-layouts  10.2 us (9%)
  blocking collectives  9.35 us (8%)
  other arithmetic  9.34 us (8%)
  between operations  4.79 us (4%)
  Pallas kernels  4.14 us (4%)
  matrix products  3.17 us (3%)
    all_to_all x2, starting transfers between devices, total(): lax.all_to_all(jnp.broadcast_to(v[None], (n,) + v.shape), axis, 0, 0, til...  24.7 us
    all_to_all x2, waiting for transfers between devices, total(): lax.all_to_all(jnp.broadcast_to(v[None], (n,) + v.shape), axis, 0, 0, til...  20.5 us
    all_to_all x1, blocking collectives, total(): lax.all_to_all(jnp.broadcast_to(v[None], (n,) + v.shape), axis, 0, 0, til...  9.35 us
    all_to_all x1, waiting for transfers between devices, to_columns(): return lax.all_to_all(grid_field, 'lat', 2, 1, tiled=True)  5.05 us
    all_to_all x1, waiting for transfers between devices, to_rows(): return lax.all_to_all(grid_field, 'lat', 1, 2, tiled=True)  4.92 us
    unnamed x22, local copies, waits for them, and re-layouts  4.91 us
    ppermute x2, starting transfers between devices, with_halo(): lax.ppermute(tail, axis, [(i, (i + 1) % count) for i in range(count)])  4.68 us
    ppermute x2, starting transfers between devices, with_halo(): lax.ppermute(head, axis, [((i + 1) % count, i) for i in range(count)])  3.88 us
  transfers between devices with their start and end apart: 8, of which 4 were waited for; matrix products, arithmetic and copies ran while one was open for 7% of the time, Pallas kernels for 0%

profile of v9, /device:TPU:1, one launch (start us, length us, event | category | flops | bytes accessed | tf_op | source)
XLA Modules:
  0.0 111.8 jit_solution(5823171047569100272)
XLA Ops:
  0.6 1.0 copy.65
  1.6 3.0 %collective-permute-start = (f32[127,1,50]{0,2,1:T(8,128)S(1)}, f32[127,1,50]{0,2,1:T(8,128)S(1)}, u32[]{:S(2)}, u32[]{:S(2)}) collective-permute-start(f32[127,1,50]{0,2,1:T(8,128)S(1)} %get-tuple-element.36), channel_id=1, source_target_pairs={{0,16},{16,32},{32,48},{48,64},{64,80},{80,96},{96,112},{112,128},... | collective-permute-start | bytes 76208 | tf_op jit(solution)/shard_map/ppermute | solution.py:23
  4.7 3.9 %collective-permute-start.1 = (f32[127,1,50]{0,2,1:T(8,128)S(1)}, f32[127,1,50]{0,2,1:T(8,128)S(1)}, u32[]{:S(2)}, u32[]{:S(2)}) collective-permute-start(f32[127,1,50]{0,2,1:T(8,128)S(1)} %get-tuple-element.37), channel_id=1, source_target_pairs={{16,0},{32,16},{48,32},{64,48},{80,64},{96,80},{112,96},{128,112},... | collective-permute-start | bytes 76208 | tf_op jit(solution)/shard_map/ppermute | solution.py:25
  10.4 0.7 gather_fusion
  11.8 0.9 convolution_bitcast_fusion.3.taps_ref
  12.9 0.7 maximum_bitcast_fusion.extended_ref
  13.5 2.1 %shard_map.103 = f32[128,127]{1,0:T(8,128)} custom-call(f32[101,127]{1,0:T(8,128)} %convolution_bitcast_fusion.3.taps_ref, f32[228,127]{1,0:T(8,128)} %maximum_bitcast_fusion.extended_ref), custom_call_target="tpu_custom_call" | custom-call | tf_op jit(solution)/shard_map/pallas_call | solution.py:106
  15.6 0.9 pad_maximum_fusion
  16.5 0.8 copy.69
  17.3 3.6 %all-to-all-start = ((f32[254,1,128]{0,1,2:T(1,128)}), f32[254,1,128]{0,1,2:T(1,128)S(1)}, u32[]{:S(2)}, u32[]{:S(2)}) async-start(f32[254,1,128]{0,1,2:T(1,128)} %copy.69), calls=%async_computation | async-start | bytes 262144 | tf_op jit(solution)/shard_map/all_to_all | solution.py:113
  21.0 0.7 multiply_reduce_fusion.4
  21.8 0.7 multiply_reduce_fusion.5
  22.5 5.0 %all-to-all-done = f32[254,1,128]{0,1,2:T(1,128)S(1)} async-done(((f32[254,1,128]{0,1,2:T(1,128)}), f32[254,1,128]{0,1,2:T(1,128)S(1)}, u32[]{:S(2)}, u32[]{:S(2)}) %all-to-all-start) | async-done | bytes 130080 | tf_op jit(solution)/shard_map/all_to_all | solution.py:113
  27.9 0.9 multiply_reduce_fusion.3
  30.4 0.7 fusion.9
  31.2 0.7 pad_maximum_fusion.1
  31.9 3.5 %all-to-all-start.1 = ((f32[128,16,8]{0,2,1:T(8,128)}), f32[128,16,8]{0,2,1:T(8,128)S(1)}, u32[]{:S(2)}, u32[]{:S(2)}) async-start(f32[128,16,8]{0,2,1:T(8,128)} %pad_maximum_fusion.1), calls=%async_computation.1 | async-start | bytes 131072 | tf_op jit(solution)/shard_map/all_to_all | solution.py:117
  35.4 0.9 convolution_bitcast_fusion.2.taps_ref
  37.0 4.9 %all-to-all-done.1 = f32[128,16,8]{0,2,1:T(8,128)S(1)} async-done(((f32[128,16,8]{0,2,1:T(8,128)}), f32[128,16,8]{0,2,1:T(8,128)S(1)}, u32[]{:S(2)}, u32[]{:S(2)}) %all-to-all-start.1) | async-done | bytes 65568 | tf_op jit(solution)/shard_map/all_to_all | solution.py:117
  42.8 18.9 %all-to-all-start.2 = ((f32[32,1,2]{2,1,0:T(1,128)}), f32[32,1,2]{2,1,0:T(1,128)S(1)}, u32[]{:S(2)}, u32[]{:S(2)}) async-start(f32[32,1,2]{2,1,0:T(1,128)} %broadcast_in_dim.18), calls=%async_computation.2 | async-start | bytes 32768 | tf_op jit(solution)/shard_map/all_to_all | solution.py:134
  61.7 1.6 %collective-permute-start.2 = (f32[127,1,50]{0,2,1:T(8,128)S(1)}, f32[127,1,50]{0,2,1:T(8,128)S(1)}, u32[]{:S(2)}, u32[]{:S(2)}) collective-permute-start(f32[127,1,50]{0,2,1:T(8,128)S(1)} %get-tuple-element.34), channel_id=1, source_target_pairs={{0,16},{16,32},{32,48},{48,64},{64,80},{80,96},{96,112},{112,128},... | collective-permute-start | bytes 76208 | tf_op jit(solution)/shard_map/ppermute | solution.py:23
  63.4 10.1 %all-to-all-done.2 = f32[32,1,2]{2,1,0:T(1,128)S(1)} async-done(((f32[32,1,2]{2,1,0:T(1,128)}), f32[32,1,2]{2,1,0:T(1,128)S(1)}, u32[]{:S(2)}, u32[]{:S(2)}) %all-to-all-start.2) | async-done | bytes 288 | tf_op jit(solution)/shard_map/all_to_all | solution.py:134
  76.1 2.1 %shard_map.104 = f32[127,128]{1,0:T(8,128)} custom-call(f32[101,127]{1,0:T(8,128)} %convolution_bitcast_fusion.2.taps_ref, f32[228,127]{1,0:T(8,128)} %maximum_bitcast_fusion.1.extended_ref, f32[127,128]{1,0:T(8,128)} %bitcast.57), custom_call_target="tpu_custom_call" | custom-call | tf_op jit(solution)/shard_map/pallas_call | solution.py:94
  78.2 1.5 %multiply_reduce_fusion.2 = (f32[]{:T(128)}, f32[127,1,128]{2,0,1:T(8,128)S(1)}) fusion(f32[127,128]{1,0:T(8,128)} %shard_map.104, f32[]{:T(128)S(6)} %div.6, f32[127,1,128]{2,1,0:T(1,128)S(1)} %copy-done.2), kind=kLoop, calls=%fused_computation.16 | loop fusion | flops 65023 | bytes 195080 | tf_op jit(solution)/shard_map/reduce_sum | solution.py:164
  79.7 0.7 broadcast_in_dim.19
  80.3 9.4 %all_to_all.36 = f32[16,1,1]{2,1,0:T(1,128)S(1)} all-to-all(f32[16,1,1]{2,1,0:T(1,128)S(1)} %broadcast_in_dim.19), channel_id=1, replica_groups=mesh['lon'=32,'lat'=16] {'lat'}, dimensions={0} | all-to-all | bytes 128 | tf_op jit(solution)/shard_map/all_to_all | solution.py:134
  90.3 1.3 %broadcast_in_dim.20 = f32[32,1,1]{2,1,0:T(1,128)} broadcast(f32[]{:T(128)} %reduce_sum.108), dimensions={} | broadcast | bytes 132 | tf_op jit(solution)/shard_map/broadcast_in_dim | solution.py:134
  91.6 5.8 %all-to-all-start.4 = ((f32[32,1,1]{2,1,0:T(1,128)}), f32[32,1,1]{2,1,0:T(1,128)S(1)}, u32[]{:S(2)}, u32[]{:S(2)}) async-start(f32[32,1,1]{2,1,0:T(1,128)} %broadcast_in_dim.20), calls=%async_computation.4 | async-start | bytes 32768 | tf_op jit(solution)/shard_map/all_to_all | solution.py:134
  97.4 0.7 multiply_add_fusion.1
  98.1 0.7 copy.77
  98.8 10.4 %all-to-all-done.4 = f32[32,1,1]{2,1,0:T(1,128)S(1)} async-done(((f32[32,1,1]{2,1,0:T(1,128)}), f32[32,1,1]{2,1,0:T(1,128)S(1)}, u32[]{:S(2)}, u32[]{:S(2)}) %all-to-all-start.4) | async-done | bytes 160 | tf_op jit(solution)/shard_map/all_to_all | solution.py:134
  111.1 0.7 copy.78
  (52 shorter events, 7.6 us)
Async XLA Ops:
  0.6 27.3 %copy-start = (f32[127,127]{1,0:T(8,128)S(1)}, f32[127,127]{1,0:T(8,128)}, u32[]{:S(2)}) copy-start(f32[127,127]{1,0:T(8,128)} %param.14) | copy-start | bytes 193552
  1.6 11.2 %collective-permute-start = (f32[127,1,50]{0,2,1:T(8,128)S(1)}, f32[127,1,50]{0,2,1:T(8,128)S(1)}, u32[]{:S(2)}, u32[]{:S(2)}) collective-permute-start(f32[127,1,50]{0,2,1:T(8,128)S(1)} %get-tuple-element.36), channel_id=1, source_target_pairs={{0,16},{16,32},{32,48},{48,64},{64,80},{80,96},{96,112},{112,128},... | collective-permute-start | bytes 76208 | tf_op jit(solution)/shard_map/ppermute | solution.py:23
  4.7 8.2 %collective-permute-start.1 = (f32[127,1,50]{0,2,1:T(8,128)S(1)}, f32[127,1,50]{0,2,1:T(8,128)S(1)}, u32[]{:S(2)}, u32[]{:S(2)}) collective-permute-start(f32[127,1,50]{0,2,1:T(8,128)S(1)} %get-tuple-element.37), channel_id=1, source_target_pairs={{16,0},{32,16},{48,32},{64,48},{80,64},{96,80},{112,96},{128,112},... | collective-permute-start | bytes 76208 | tf_op jit(solution)/shard_map/ppermute | solution.py:25
  8.6 0.7 copy-start.7
  9.4 0.7 copy-start.6
  11.1 0.7 copy-start.3
  11.8 0.9 copy-start.5
  17.3 3.7 %copy-start.1 = (f32[127,1,128]{2,1,0:T(1,128)S(1)}, f32[127,1,128]{2,1,0:T(1,128)}, u32[]{:S(2)}) copy-start(f32[127,1,128]{2,1,0:T(1,128)} %param.12) | copy-start | bytes 195076
  17.3 10.3 %all-to-all-start = ((f32[254,1,128]{0,1,2:T(1,128)}), f32[254,1,128]{0,1,2:T(1,128)S(1)}, u32[]{:S(2)}, u32[]{:S(2)}) async-start(f32[254,1,128]{0,1,2:T(1,128)} %copy.69), calls=%async_computation | async-start | bytes 262144 | tf_op jit(solution)/shard_map/all_to_all | solution.py:113
  21.0 0.8 copy-start.2
  31.9 10.0 %all-to-all-start.1 = ((f32[128,16,8]{0,2,1:T(8,128)}), f32[128,16,8]{0,2,1:T(8,128)S(1)}, u32[]{:S(2)}, u32[]{:S(2)}) async-start(f32[128,16,8]{0,2,1:T(8,128)} %pad_maximum_fusion.1), calls=%async_computation.1 | async-start | bytes 131072 | tf_op jit(solution)/shard_map/all_to_all | solution.py:117
  42.8 30.7 %all-to-all-start.2 = ((f32[32,1,2]{2,1,0:T(1,128)}), f32[32,1,2]{2,1,0:T(1,128)S(1)}, u32[]{:S(2)}, u32[]{:S(2)}) async-start(f32[32,1,2]{2,1,0:T(1,128)} %broadcast_in_dim.18), calls=%async_computation.2 | async-start | bytes 32768 | tf_op jit(solution)/shard_map/all_to_all | solution.py:134
  61.7 13.7 %collective-permute-start.2 = (f32[127,1,50]{0,2,1:T(8,128)S(1)}, f32[127,1,50]{0,2,1:T(8,128)S(1)}, u32[]{:S(2)}, u32[]{:S(2)}) collective-permute-start(f32[127,1,50]{0,2,1:T(8,128)S(1)} %get-tuple-element.34), channel_id=1, source_target_pairs={{0,16},{16,32},{32,48},{48,64},{64,80},{80,96},{96,112},{112,128},... | collective-permute-start | bytes 76208 | tf_op jit(solution)/shard_map/ppermute | solution.py:23
  63.4 12.1 %collective-permute-start.3 = (f32[127,1,50]{0,2,1:T(8,128)S(1)}, f32[127,1,50]{0,2,1:T(8,128)S(1)}, u32[]{:S(2)}, u32[]{:S(2)}) collective-permute-start(f32[127,1,50]{0,2,1:T(8,128)S(1)} %get-tuple-element.35), channel_id=1, source_target_pairs={{16,0},{32,16},{48,32},{64,48},{80,64},{96,80},{112,96},{128,112},... | collective-permute-start | bytes 76208 | tf_op jit(solution)/shard_map/ppermute | solution.py:25
  79.7 17.7 %copy-start.4 = (f32[127,1,128]{2,1,0:T(1,128)S(1)}, f32[127,1,128]{2,1,0:T(1,128)}, u32[]{:S(2)}) copy-start(f32[127,1,128]{2,1,0:T(1,128)} %param.10) | copy-start | bytes 195076
  91.6 17.6 %all-to-all-start.4 = ((f32[32,1,1]{2,1,0:T(1,128)}), f32[32,1,1]{2,1,0:T(1,128)S(1)}, u32[]{:S(2)}, u32[]{:S(2)}) async-start(f32[32,1,1]{2,1,0:T(1,128)} %broadcast_in_dim.20), calls=%async_computation.4 | async-start | bytes 32768 | tf_op jit(solution)/shard_map/all_to_all | solution.py:134

commit v10 on v9

--- a/solution.py
+++ b/solution.py
@@ -67,13 +67,13 @@
 
 
 def lon_kernel(taps_ref, extended_ref, out_ref):
-    width = out_ref.shape[0]
+    width = out_ref.shape[1]
     total_sum = taps_ref[0:1, :] * extended_ref[0:width, :]
     for shift_tap in range(1, TAPS):
         total_sum = total_sum + taps_ref[shift_tap : shift_tap + 1, :] * extended_ref[
             shift_tap : shift_tap + width, :
         ]
-    out_ref[...] = total_sum
+    out_ref[...] = total_sum.T
 
 
 def lon_add_kernel(taps_ref, extended_ref, base_ref, out_ref):
@@ -104,9 +104,9 @@
     kernels = jnp.repeat(group_rows(groups, kernel), rows, axis=0)
     extended = with_halo(grid_field, (("lon", 2),), HALF)
     filtered = pl.pallas_call(
-        lon_kernel, out_shape=jax.ShapeDtypeStruct((lon_width, levels * rows), grid_field.dtype)
+        lon_kernel, out_shape=jax.ShapeDtypeStruct((levels * rows, lon_width), grid_field.dtype)
     )(kernels.T, extended.reshape(levels * rows, -1).T)
-    return filtered.T.reshape(levels, rows, lon_width)
+    return filtered.reshape(levels, rows, lon_width)
 
 
 def to_columns(grid_field):

time: 113 us -> 112 us (level)
  no operation moved by 1% of the time
where the time goes in v10:
time: 112 us
  starting transfers between devices  40.4 us (36%)
  waiting for transfers between devices  30.5 us (27%)
  local copies, waits for them, and re-layouts  10 us (9%)
  blocking collectives  9.35 us (8%)
  other arithmetic  9.26 us (8%)
  between operations  4.79 us (4%)
  Pallas kernels  4.14 us (4%)
  matrix products  3.17 us (3%)
    all_to_all x2, starting transfers between devices, total(): lax.all_to_all(jnp.broadcast_to(v[None], (n,) + v.shape), axis, 0, 0, til...  24.7 us
    all_to_all x2, waiting for transfers between devices, total(): lax.all_to_all(jnp.broadcast_to(v[None], (n,) + v.shape), axis, 0, 0, til...  20.5 us
    all_to_all x1, blocking collectives, total(): lax.all_to_all(jnp.broadcast_to(v[None], (n,) + v.shape), axis, 0, 0, til...  9.35 us
    all_to_all x1, waiting for transfers between devices, to_columns(): return lax.all_to_all(grid_field, 'lat', 2, 1, tiled=True)  5.05 us
    all_to_all x1, waiting for transfers between devices, to_rows(): return lax.all_to_all(grid_field, 'lat', 1, 2, tiled=True)  4.92 us
    unnamed x22, local copies, waits for them, and re-layouts  4.83 us
    ppermute x2, starting transfers between devices, with_halo(): lax.ppermute(tail, axis, [(i, (i + 1) % count) for i in range(count)])  4.68 us
    ppermute x2, starting transfers between devices, with_halo(): lax.ppermute(head, axis, [((i + 1) % count, i) for i in range(count)])  3.88 us
  transfers between devices with their start and end apart: 8, of which 4 were waited for; matrix products, arithmetic and copies ran while one was open for 7% of the time, Pallas kernels for 0%

profile of v10, /device:TPU:1, one launch (start us, length us, event | category | flops | bytes accessed | tf_op | source)
XLA Modules:
  0.0 111.6 jit_solution(11720345538914312370)
XLA Ops:
  0.6 1.0 copy.69
  1.6 3.0 %collective-permute-start = (f32[127,1,50]{0,2,1:T(8,128)S(1)}, f32[127,1,50]{0,2,1:T(8,128)S(1)}, u32[]{:S(2)}, u32[]{:S(2)}) collective-permute-start(f32[127,1,50]{0,2,1:T(8,128)S(1)} %get-tuple-element.36), channel_id=1, source_target_pairs={{0,16},{16,32},{32,48},{48,64},{64,80},{80,96},{96,112},{112,128},... | collective-permute-start | bytes 76208 | tf_op jit(solution)/shard_map/ppermute | solution.py:23
  4.7 3.9 %collective-permute-start.1 = (f32[127,1,50]{0,2,1:T(8,128)S(1)}, f32[127,1,50]{0,2,1:T(8,128)S(1)}, u32[]{:S(2)}, u32[]{:S(2)}) collective-permute-start(f32[127,1,50]{0,2,1:T(8,128)S(1)} %get-tuple-element.37), channel_id=1, source_target_pairs={{16,0},{32,16},{48,32},{64,48},{80,64},{96,80},{112,96},{128,112},... | collective-permute-start | bytes 76208 | tf_op jit(solution)/shard_map/ppermute | solution.py:25
  10.4 0.7 gather_fusion
  11.8 0.9 convolution_bitcast_fusion.3.taps_ref
  12.8 0.7 maximum_bitcast_fusion.extended_ref
  13.4 2.1 %shard_map.103 = f32[127,128]{1,0:T(8,128)} custom-call(f32[101,127]{1,0:T(8,128)} %convolution_bitcast_fusion.3.taps_ref, f32[228,127]{1,0:T(8,128)} %maximum_bitcast_fusion.extended_ref), custom_call_target="tpu_custom_call" | custom-call | tf_op jit(solution)/shard_map/pallas_call | solution.py:106
  15.5 0.8 pad_maximum_fusion
  16.4 0.7 copy.73
  17.1 3.6 %all-to-all-start = ((f32[254,1,128]{0,1,2:T(1,128)}), f32[254,1,128]{0,1,2:T(1,128)S(1)}, u32[]{:S(2)}, u32[]{:S(2)}) async-start(f32[254,1,128]{0,1,2:T(1,128)} %copy.73), calls=%async_computation | async-start | bytes 262144 | tf_op jit(solution)/shard_map/all_to_all | solution.py:113
  20.8 0.7 multiply_reduce_fusion.4
  21.6 0.7 multiply_reduce_fusion.5
  22.3 5.0 %all-to-all-done = f32[254,1,128]{0,1,2:T(1,128)S(1)} async-done(((f32[254,1,128]{0,1,2:T(1,128)}), f32[254,1,128]{0,1,2:T(1,128)S(1)}, u32[]{:S(2)}, u32[]{:S(2)}) %all-to-all-start) | async-done | bytes 130080 | tf_op jit(solution)/shard_map/all_to_all | solution.py:113
  27.7 0.9 multiply_reduce_fusion.3
  30.2 0.7 fusion.9
  31.0 0.7 pad_maximum_fusion.1
  31.7 3.5 %all-to-all-start.1 = ((f32[128,16,8]{0,2,1:T(8,128)}), f32[128,16,8]{0,2,1:T(8,128)S(1)}, u32[]{:S(2)}, u32[]{:S(2)}) async-start(f32[128,16,8]{0,2,1:T(8,128)} %pad_maximum_fusion.1), calls=%async_computation.1 | async-start | bytes 131072 | tf_op jit(solution)/shard_map/all_to_all | solution.py:117
  35.2 0.9 convolution_bitcast_fusion.2.taps_ref
  36.7 4.9 %all-to-all-done.1 = f32[128,16,8]{0,2,1:T(8,128)S(1)} async-done(((f32[128,16,8]{0,2,1:T(8,128)}), f32[128,16,8]{0,2,1:T(8,128)S(1)}, u32[]{:S(2)}, u32[]{:S(2)}) %all-to-all-start.1) | async-done | bytes 65568 | tf_op jit(solution)/shard_map/all_to_all | solution.py:117
  42.6 18.9 %all-to-all-start.2 = ((f32[32,1,2]{2,1,0:T(1,128)}), f32[32,1,2]{2,1,0:T(1,128)S(1)}, u32[]{:S(2)}, u32[]{:S(2)}) async-start(f32[32,1,2]{2,1,0:T(1,128)} %broadcast_in_dim.18), calls=%async_computation.2 | async-start | bytes 32768 | tf_op jit(solution)/shard_map/all_to_all | solution.py:134
  61.5 1.6 %collective-permute-start.2 = (f32[127,1,50]{0,2,1:T(8,128)S(1)}, f32[127,1,50]{0,2,1:T(8,128)S(1)}, u32[]{:S(2)}, u32[]{:S(2)}) collective-permute-start(f32[127,1,50]{0,2,1:T(8,128)S(1)} %get-tuple-element.34), channel_id=1, source_target_pairs={{0,16},{16,32},{32,48},{48,64},{64,80},{80,96},{96,112},{112,128},... | collective-permute-start | bytes 76208 | tf_op jit(solution)/shard_map/ppermute | solution.py:23
  63.2 10.1 %all-to-all-done.2 = f32[32,1,2]{2,1,0:T(1,128)S(1)} async-done(((f32[32,1,2]{2,1,0:T(1,128)}), f32[32,1,2]{2,1,0:T(1,128)S(1)}, u32[]{:S(2)}, u32[]{:S(2)}) %all-to-all-start.2) | async-done | bytes 288 | tf_op jit(solution)/shard_map/all_to_all | solution.py:134
  75.9 2.1 %shard_map.104 = f32[127,128]{1,0:T(8,128)} custom-call(f32[101,127]{1,0:T(8,128)} %convolution_bitcast_fusion.2.taps_ref, f32[228,127]{1,0:T(8,128)} %maximum_bitcast_fusion.1.extended_ref, f32[127,128]{1,0:T(8,128)} %bitcast.57), custom_call_target="tpu_custom_call" | custom-call | tf_op jit(solution)/shard_map/pallas_call | solution.py:94
  78.0 1.5 %multiply_reduce_fusion.2 = (f32[]{:T(128)}, f32[127,1,128]{2,0,1:T(8,128)S(1)}) fusion(f32[127,128]{1,0:T(8,128)} %shard_map.104, f32[]{:T(128)S(6)} %div.6, f32[127,1,128]{2,1,0:T(1,128)S(1)} %copy-done.2), kind=kLoop, calls=%fused_computation.16 | loop fusion | flops 65023 | bytes 195080 | tf_op jit(solution)/shard_map/reduce_sum | solution.py:164
  79.4 0.7 broadcast_in_dim.19
  80.1 9.4 %all_to_all.36 = f32[16,1,1]{2,1,0:T(1,128)S(1)} all-to-all(f32[16,1,1]{2,1,0:T(1,128)S(1)} %broadcast_in_dim.19), channel_id=1, replica_groups=mesh['lon'=32,'lat'=16] {'lat'}, dimensions={0} | all-to-all | bytes 128 | tf_op jit(solution)/shard_map/all_to_all | solution.py:134
  90.1 1.3 %broadcast_in_dim.20 = f32[32,1,1]{2,1,0:T(1,128)} broadcast(f32[]{:T(128)} %reduce_sum.108), dimensions={} | broadcast | bytes 132 | tf_op jit(solution)/shard_map/broadcast_in_dim | solution.py:134
  91.3 5.8 %all-to-all-start.4 = ((f32[32,1,1]{2,1,0:T(1,128)}), f32[32,1,1]{2,1,0:T(1,128)S(1)}, u32[]{:S(2)}, u32[]{:S(2)}) async-start(f32[32,1,1]{2,1,0:T(1,128)} %broadcast_in_dim.20), calls=%async_computation.4 | async-start | bytes 32768 | tf_op jit(solution)/shard_map/all_to_all | solution.py:134
  97.2 0.7 multiply_add_fusion.1
  97.9 0.7 copy.82
  98.6 10.4 %all-to-all-done.4 = f32[32,1,1]{2,1,0:T(1,128)S(1)} async-done(((f32[32,1,1]{2,1,0:T(1,128)}), f32[32,1,1]{2,1,0:T(1,128)S(1)}, u32[]{:S(2)}, u32[]{:S(2)}) %all-to-all-start.4) | async-done | bytes 160 | tf_op jit(solution)/shard_map/all_to_all | solution.py:134
  110.9 0.7 copy.83
  (52 shorter events, 7.5 us)
Async XLA Ops:
  0.6 27.1 %copy-start = (f32[127,127]{1,0:T(8,128)S(1)}, f32[127,127]{1,0:T(8,128)}, u32[]{:S(2)}) copy-start(f32[127,127]{1,0:T(8,128)} %param.14) | copy-start | bytes 193552
  1.6 11.1 %collective-permute-start = (f32[127,1,50]{0,2,1:T(8,128)S(1)}, f32[127,1,50]{0,2,1:T(8,128)S(1)}, u32[]{:S(2)}, u32[]{:S(2)}) collective-permute-start(f32[127,1,50]{0,2,1:T(8,128)S(1)} %get-tuple-element.36), channel_id=1, source_target_pairs={{0,16},{16,32},{32,48},{48,64},{64,80},{80,96},{96,112},{112,128},... | collective-permute-start | bytes 76208 | tf_op jit(solution)/shard_map/ppermute | solution.py:23
  4.7 8.1 %collective-permute-start.1 = (f32[127,1,50]{0,2,1:T(8,128)S(1)}, f32[127,1,50]{0,2,1:T(8,128)S(1)}, u32[]{:S(2)}, u32[]{:S(2)}) collective-permute-start(f32[127,1,50]{0,2,1:T(8,128)S(1)} %get-tuple-element.37), channel_id=1, source_target_pairs={{16,0},{32,16},{48,32},{64,48},{80,64},{96,80},{112,96},{128,112},... | collective-permute-start | bytes 76208 | tf_op jit(solution)/shard_map/ppermute | solution.py:25
  8.6 0.7 copy-start.7
  9.4 0.7 copy-start.6
  11.1 0.7 copy-start.3
  11.8 0.9 copy-start.5
  17.1 3.7 %copy-start.1 = (f32[127,1,128]{2,1,0:T(1,128)S(1)}, f32[127,1,128]{2,1,0:T(1,128)}, u32[]{:S(2)}) copy-start(f32[127,1,128]{2,1,0:T(1,128)} %param.12) | copy-start | bytes 195076
  17.1 10.3 %all-to-all-start = ((f32[254,1,128]{0,1,2:T(1,128)}), f32[254,1,128]{0,1,2:T(1,128)S(1)}, u32[]{:S(2)}, u32[]{:S(2)}) async-start(f32[254,1,128]{0,1,2:T(1,128)} %copy.73), calls=%async_computation | async-start | bytes 262144 | tf_op jit(solution)/shard_map/all_to_all | solution.py:113
  20.8 0.8 copy-start.2
  31.7 10.0 %all-to-all-start.1 = ((f32[128,16,8]{0,2,1:T(8,128)}), f32[128,16,8]{0,2,1:T(8,128)S(1)}, u32[]{:S(2)}, u32[]{:S(2)}) async-start(f32[128,16,8]{0,2,1:T(8,128)} %pad_maximum_fusion.1), calls=%async_computation.1 | async-start | bytes 131072 | tf_op jit(solution)/shard_map/all_to_all | solution.py:117
  42.6 30.7 %all-to-all-start.2 = ((f32[32,1,2]{2,1,0:T(1,128)}), f32[32,1,2]{2,1,0:T(1,128)S(1)}, u32[]{:S(2)}, u32[]{:S(2)}) async-start(f32[32,1,2]{2,1,0:T(1,128)} %broadcast_in_dim.18), calls=%async_computation.2 | async-start | bytes 32768 | tf_op jit(solution)/shard_map/all_to_all | solution.py:134
  61.5 13.7 %collective-permute-start.2 = (f32[127,1,50]{0,2,1:T(8,128)S(1)}, f32[127,1,50]{0,2,1:T(8,128)S(1)}, u32[]{:S(2)}, u32[]{:S(2)}) collective-permute-start(f32[127,1,50]{0,2,1:T(8,128)S(1)} %get-tuple-element.34), channel_id=1, source_target_pairs={{0,16},{16,32},{32,48},{48,64},{64,80},{80,96},{96,112},{112,128},... | collective-permute-start | bytes 76208 | tf_op jit(solution)/shard_map/ppermute | solution.py:23
  63.1 12.1 %collective-permute-start.3 = (f32[127,1,50]{0,2,1:T(8,128)S(1)}, f32[127,1,50]{0,2,1:T(8,128)S(1)}, u32[]{:S(2)}, u32[]{:S(2)}) collective-permute-start(f32[127,1,50]{0,2,1:T(8,128)S(1)} %get-tuple-element.35), channel_id=1, source_target_pairs={{16,0},{32,16},{48,32},{64,48},{80,64},{96,80},{112,96},{128,112},... | collective-permute-start | bytes 76208 | tf_op jit(solution)/shard_map/ppermute | solution.py:25
  79.4 17.7 %copy-start.4 = (f32[127,1,128]{2,1,0:T(1,128)S(1)}, f32[127,1,128]{2,1,0:T(1,128)}, u32[]{:S(2)}) copy-start(f32[127,1,128]{2,1,0:T(1,128)} %param.10) | copy-start | bytes 195076
  91.3 17.6 %all-to-all-start.4 = ((f32[32,1,1]{2,1,0:T(1,128)}), f32[32,1,1]{2,1,0:T(1,128)S(1)}, u32[]{:S(2)}, u32[]{:S(2)}) async-start(f32[32,1,1]{2,1,0:T(1,128)} %broadcast_in_dim.20), calls=%async_computation.4 | async-start | bytes 32768 | tf_op jit(solution)/shard_map/all_to_all | solution.py:134

commit v11 on v9

--- a/solution.py
+++ b/solution.py
@@ -161,7 +161,7 @@
     applied = lon_pass_add(back_lat, direction, lon_taps, groups)
     step_length = norm_old / curvature
     residual_next = residual - step_length * applied
-    (norm_new,) = total((jnp.sum(residual_next * residual_next),))
+    (norm_new,) = total((jnp.sum(residual_next * residual_next),), ("lon", "lat"))
     iterate_next = iterate + step_length * direction
     direction_next = residual_next + norm_new / norm_old * direction
     return (iterate_next, residual_next, direction_next)

time: 113 us -> 112 us (level)
  blocking collectives: 9.35 us -> 0 us
  waiting for transfers between devices: 30.5 us -> 36.8 us
  starting transfers between devices: 40.4 us -> 42.4 us
    all_to_all x1 -> x0, blocking collectives: 9.35 us -> none  [total(): lax.all_to_all(jnp.broadcast_to(v[None], (n,) + v.shape), axis, 0, 0, til...]
    all_to_all x2 -> x3, waiting for transfers between devices: 20.5 us -> 26.8 us  [total(): lax.all_to_all(jnp.broadcast_to(v[None], (n,) + v.shape), axis, 0, 0, til...]
    all_to_all x2 -> x3, starting transfers between devices: 24.7 us -> 26.7 us  [total(): lax.all_to_all(jnp.broadcast_to(v[None], (n,) + v.shape), axis, 0, 0, til...]
  transfers between devices with their start and end apart: 8 -> 9, of which waited for: 4 -> 5; matrix products, arithmetic and copies ran while one was open for 7% -> 7% of each run, Pallas kernels for 0% -> 0%
where the time goes in v11:
time: 112 us; the launch traced here: 111 us
  starting transfers between devices  42.4 us (38%)
  waiting for transfers between devices  36.8 us (33%)
  local copies, waits for them, and re-layouts  10.7 us (10%)
  other arithmetic  9.35 us (8%)
  between operations  4.79 us (4%)
  Pallas kernels  4.14 us (4%)
  matrix products  3.17 us (3%)
    all_to_all x3, waiting for transfers between devices, total(): lax.all_to_all(jnp.broadcast_to(v[None], (n,) + v.shape), axis, 0, 0, til...  26.8 us
    all_to_all x3, starting transfers between devices, total(): lax.all_to_all(jnp.broadcast_to(v[None], (n,) + v.shape), axis, 0, 0, til...  26.7 us
    all_to_all x1, waiting for transfers between devices, to_columns(): return lax.all_to_all(grid_field, 'lat', 2, 1, tiled=True)  5.05 us
    all_to_all x1, waiting for transfers between devices, to_rows(): return lax.all_to_all(grid_field, 'lat', 1, 2, tiled=True)  4.92 us
    unnamed x22, local copies, waits for them, and re-layouts  4.91 us
    ppermute x2, starting transfers between devices, with_halo(): lax.ppermute(tail, axis, [(i, (i + 1) % count) for i in range(count)])  4.68 us
    ppermute x2, starting transfers between devices, with_halo(): lax.ppermute(head, axis, [((i + 1) % count, i) for i in range(count)])  3.88 us
    all_to_all x1, starting transfers between devices, to_columns(): return lax.all_to_all(grid_field, 'lat', 2, 1, tiled=True)  3.64 us
  transfers between devices with their start and end apart: 9, of which 5 were waited for; matrix products, arithmetic and copies ran while one was open for 7% of the time, Pallas kernels for 0%

profile of v11, /device:TPU:1, one launch (start us, length us, event | category | flops | bytes accessed | tf_op | source)
XLA Modules:
  0.0 111.4 jit_solution(821713232138921985)
XLA Ops:
  0.6 1.0 copy.65
  1.6 3.0 %collective-permute-start = (f32[127,1,50]{0,2,1:T(8,128)S(1)}, f32[127,1,50]{0,2,1:T(8,128)S(1)}, u32[]{:S(2)}, u32[]{:S(2)}) collective-permute-start(f32[127,1,50]{0,2,1:T(8,128)S(1)} %get-tuple-element.36), channel_id=1, source_target_pairs={{0,16},{16,32},{32,48},{48,64},{64,80},{80,96},{96,112},{112,128},... | collective-permute-start | bytes 76208 | tf_op jit(solution)/shard_map/ppermute | solution.py:23
  4.7 3.9 %collective-permute-start.1 = (f32[127,1,50]{0,2,1:T(8,128)S(1)}, f32[127,1,50]{0,2,1:T(8,128)S(1)}, u32[]{:S(2)}, u32[]{:S(2)}) collective-permute-start(f32[127,1,50]{0,2,1:T(8,128)S(1)} %get-tuple-element.37), channel_id=1, source_target_pairs={{16,0},{32,16},{48,32},{64,48},{80,64},{96,80},{112,96},{128,112},... | collective-permute-start | bytes 76208 | tf_op jit(solution)/shard_map/ppermute | solution.py:25
  10.4 0.7 gather_fusion
  11.8 0.9 convolution_bitcast_fusion.3.taps_ref
  13.5 2.1 %shard_map.103 = f32[128,127]{1,0:T(8,128)} custom-call(f32[101,127]{1,0:T(8,128)} %convolution_bitcast_fusion.3.taps_ref, f32[228,127]{1,0:T(8,128)} %maximum_bitcast_fusion.extended_ref), custom_call_target="tpu_custom_call" | custom-call | tf_op jit(solution)/shard_map/pallas_call | solution.py:106
  15.6 0.9 pad_maximum_fusion
  16.5 0.8 copy.69
  17.3 3.6 %all-to-all-start = ((f32[254,1,128]{0,1,2:T(1,128)}), f32[254,1,128]{0,1,2:T(1,128)S(1)}, u32[]{:S(2)}, u32[]{:S(2)}) async-start(f32[254,1,128]{0,1,2:T(1,128)} %copy.69), calls=%async_computation | async-start | bytes 262144 | tf_op jit(solution)/shard_map/all_to_all | solution.py:113
  21.0 0.7 multiply_reduce_fusion.4
  21.8 0.7 multiply_reduce_fusion.5
  22.5 5.0 %all-to-all-done = f32[254,1,128]{0,1,2:T(1,128)S(1)} async-done(((f32[254,1,128]{0,1,2:T(1,128)}), f32[254,1,128]{0,1,2:T(1,128)S(1)}, u32[]{:S(2)}, u32[]{:S(2)}) %all-to-all-start) | async-done | bytes 130080 | tf_op jit(solution)/shard_map/all_to_all | solution.py:113
  27.9 0.9 multiply_reduce_fusion.3
  30.4 0.7 fusion.9
  31.2 0.7 pad_maximum_fusion.1
  31.9 3.5 %all-to-all-start.1 = ((f32[128,16,8]{0,2,1:T(8,128)}), f32[128,16,8]{0,2,1:T(8,128)S(1)}, u32[]{:S(2)}, u32[]{:S(2)}) async-start(f32[128,16,8]{0,2,1:T(8,128)} %pad_maximum_fusion.1), calls=%async_computation.1 | async-start | bytes 131072 | tf_op jit(solution)/shard_map/all_to_all | solution.py:117
  35.4 0.9 convolution_bitcast_fusion.2.taps_ref
  37.0 4.9 %all-to-all-done.1 = f32[128,16,8]{0,2,1:T(8,128)S(1)} async-done(((f32[128,16,8]{0,2,1:T(8,128)}), f32[128,16,8]{0,2,1:T(8,128)S(1)}, u32[]{:S(2)}, u32[]{:S(2)}) %all-to-all-start.1) | async-done | bytes 65568 | tf_op jit(solution)/shard_map/all_to_all | solution.py:117
  42.8 18.9 %all-to-all-start.2 = ((f32[32,1,2]{2,1,0:T(1,128)}), f32[32,1,2]{2,1,0:T(1,128)S(1)}, u32[]{:S(2)}, u32[]{:S(2)}) async-start(f32[32,1,2]{2,1,0:T(1,128)} %broadcast_in_dim.18), calls=%async_computation.2 | async-start | bytes 32768 | tf_op jit(solution)/shard_map/all_to_all | solution.py:134
  61.7 1.6 %collective-permute-start.2 = (f32[127,1,50]{0,2,1:T(8,128)S(1)}, f32[127,1,50]{0,2,1:T(8,128)S(1)}, u32[]{:S(2)}, u32[]{:S(2)}) collective-permute-start(f32[127,1,50]{0,2,1:T(8,128)S(1)} %get-tuple-element.34), channel_id=1, source_target_pairs={{0,16},{16,32},{32,48},{48,64},{64,80},{80,96},{96,112},{112,128},... | collective-permute-start | bytes 76208 | tf_op jit(solution)/shard_map/ppermute | solution.py:23
  63.4 10.1 %all-to-all-done.2 = f32[32,1,2]{2,1,0:T(1,128)S(1)} async-done(((f32[32,1,2]{2,1,0:T(1,128)}), f32[32,1,2]{2,1,0:T(1,128)S(1)}, u32[]{:S(2)}, u32[]{:S(2)}) %all-to-all-start.2) | async-done | bytes 288 | tf_op jit(solution)/shard_map/all_to_all | solution.py:134
  76.1 2.1 %shard_map.104 = f32[127,128]{1,0:T(8,128)} custom-call(f32[101,127]{1,0:T(8,128)} %convolution_bitcast_fusion.2.taps_ref, f32[228,127]{1,0:T(8,128)} %maximum_bitcast_fusion.1.extended_ref, f32[127,128]{1,0:T(8,128)} %bitcast.57), custom_call_target="tpu_custom_call" | custom-call | tf_op jit(solution)/shard_map/pallas_call | solution.py:94
  78.2 1.5 %multiply_reduce_fusion.2 = (f32[]{:T(128)}, f32[127,1,128]{2,0,1:T(8,128)S(1)}) fusion(f32[127,128]{1,0:T(8,128)} %shard_map.104, f32[]{:T(128)S(6)} %div.6, f32[127,1,128]{2,1,0:T(1,128)S(1)} %copy-done.2), kind=kLoop, calls=%fused_computation.16 | loop fusion | flops 65023 | bytes 195080 | tf_op jit(solution)/shard_map/reduce_sum | solution.py:164
  79.7 1.3 %broadcast_in_dim.19 = f32[32,1,1]{2,1,0:T(1,128)} broadcast(f32[]{:T(128)} %get-tuple-element.30), dimensions={} | broadcast | bytes 132 | tf_op jit(solution)/shard_map/broadcast_in_dim | solution.py:134
  80.9 4.4 %all-to-all-start.3 = ((f32[32,1,1]{2,1,0:T(1,128)}), f32[32,1,1]{2,1,0:T(1,128)S(1)}, u32[]{:S(2)}, u32[]{:S(2)}) async-start(f32[32,1,1]{2,1,0:T(1,128)} %broadcast_in_dim.19), calls=%async_computation.3 | async-start | bytes 32768 | tf_op jit(solution)/shard_map/all_to_all | solution.py:134
  85.3 0.7 multiply_add_fusion.1
  86.0 11.1 %all-to-all-done.3 = f32[32,1,1]{2,1,0:T(1,128)S(1)} async-done(((f32[32,1,1]{2,1,0:T(1,128)}), f32[32,1,1]{2,1,0:T(1,128)S(1)}, u32[]{:S(2)}, u32[]{:S(2)}) %all-to-all-start.3) | async-done | bytes 160 | tf_op jit(solution)/shard_map/all_to_all | solution.py:134
  97.8 1.2 %broadcast_in_dim.20 = f32[16,1,1]{2,1,0:T(1,128)} broadcast(f32[]{:T(128)} %reduce_sum.108), dimensions={} | broadcast | bytes 68 | tf_op jit(solution)/shard_map/broadcast_in_dim | solution.py:134
  99.0 3.5 %all-to-all-start.4 = ((f32[16,1,1]{2,1,0:T(1,128)}), f32[16,1,1]{2,1,0:T(1,128)S(1)}, u32[]{:S(2)}, u32[]{:S(2)}) async-start(f32[16,1,1]{2,1,0:T(1,128)} %broadcast_in_dim.20), calls=%async_computation.4 | async-start | bytes 16384 | tf_op jit(solution)/shard_map/all_to_all | solution.py:134
  102.5 0.7 copy.77
  103.2 5.6 %all-to-all-done.4 = f32[16,1,1]{2,1,0:T(1,128)S(1)} async-done(((f32[16,1,1]{2,1,0:T(1,128)}), f32[16,1,1]{2,1,0:T(1,128)S(1)}, u32[]{:S(2)}, u32[]{:S(2)}) %all-to-all-start.4) | async-done | bytes 96 | tf_op jit(solution)/shard_map/all_to_all | solution.py:134
  110.7 0.7 copy.78
  (53 shorter events, 8.2 us)
Async XLA Ops:
  0.6 27.3 %copy-start = (f32[127,127]{1,0:T(8,128)S(1)}, f32[127,127]{1,0:T(8,128)}, u32[]{:S(2)}) copy-start(f32[127,127]{1,0:T(8,128)} %param.14) | copy-start | bytes 193552
  1.6 11.2 %collective-permute-start = (f32[127,1,50]{0,2,1:T(8,128)S(1)}, f32[127,1,50]{0,2,1:T(8,128)S(1)}, u32[]{:S(2)}, u32[]{:S(2)}) collective-permute-start(f32[127,1,50]{0,2,1:T(8,128)S(1)} %get-tuple-element.36), channel_id=1, source_target_pairs={{0,16},{16,32},{32,48},{48,64},{64,80},{80,96},{96,112},{112,128},... | collective-permute-start | bytes 76208 | tf_op jit(solution)/shard_map/ppermute | solution.py:23
  4.7 8.2 %collective-permute-start.1 = (f32[127,1,50]{0,2,1:T(8,128)S(1)}, f32[127,1,50]{0,2,1:T(8,128)S(1)}, u32[]{:S(2)}, u32[]{:S(2)}) collective-permute-start(f32[127,1,50]{0,2,1:T(8,128)S(1)} %get-tuple-element.37), channel_id=1, source_target_pairs={{16,0},{32,16},{48,32},{64,48},{80,64},{96,80},{112,96},{128,112},... | collective-permute-start | bytes 76208 | tf_op jit(solution)/shard_map/ppermute | solution.py:25
  8.6 0.7 copy-start.7
  9.4 0.7 copy-start.6
  11.1 0.7 copy-start.3
  11.8 0.9 copy-start.5
  17.3 3.7 %copy-start.1 = (f32[127,1,128]{2,1,0:T(1,128)S(1)}, f32[127,1,128]{2,1,0:T(1,128)}, u32[]{:S(2)}) copy-start(f32[127,1,128]{2,1,0:T(1,128)} %param.12) | copy-start | bytes 195076
  17.3 10.3 %all-to-all-start = ((f32[254,1,128]{0,1,2:T(1,128)}), f32[254,1,128]{0,1,2:T(1,128)S(1)}, u32[]{:S(2)}, u32[]{:S(2)}) async-start(f32[254,1,128]{0,1,2:T(1,128)} %copy.69), calls=%async_computation | async-start | bytes 262144 | tf_op jit(solution)/shard_map/all_to_all | solution.py:113
  21.0 0.8 copy-start.2
  31.9 10.0 %all-to-all-start.1 = ((f32[128,16,8]{0,2,1:T(8,128)}), f32[128,16,8]{0,2,1:T(8,128)S(1)}, u32[]{:S(2)}, u32[]{:S(2)}) async-start(f32[128,16,8]{0,2,1:T(8,128)} %pad_maximum_fusion.1), calls=%async_computation.1 | async-start | bytes 131072 | tf_op jit(solution)/shard_map/all_to_all | solution.py:117
  42.8 30.7 %all-to-all-start.2 = ((f32[32,1,2]{2,1,0:T(1,128)}), f32[32,1,2]{2,1,0:T(1,128)S(1)}, u32[]{:S(2)}, u32[]{:S(2)}) async-start(f32[32,1,2]{2,1,0:T(1,128)} %broadcast_in_dim.18), calls=%async_computation.2 | async-start | bytes 32768 | tf_op jit(solution)/shard_map/all_to_all | solution.py:134
  61.7 13.7 %collective-permute-start.2 = (f32[127,1,50]{0,2,1:T(8,128)S(1)}, f32[127,1,50]{0,2,1:T(8,128)S(1)}, u32[]{:S(2)}, u32[]{:S(2)}) collective-permute-start(f32[127,1,50]{0,2,1:T(8,128)S(1)} %get-tuple-element.34), channel_id=1, source_target_pairs={{0,16},{16,32},{32,48},{48,64},{64,80},{80,96},{96,112},{112,128},... | collective-permute-start | bytes 76208 | tf_op jit(solution)/shard_map/ppermute | solution.py:23
  63.4 12.1 %collective-permute-start.3 = (f32[127,1,50]{0,2,1:T(8,128)S(1)}, f32[127,1,50]{0,2,1:T(8,128)S(1)}, u32[]{:S(2)}, u32[]{:S(2)}) collective-permute-start(f32[127,1,50]{0,2,1:T(8,128)S(1)} %get-tuple-element.35), channel_id=1, source_target_pairs={{16,0},{32,16},{48,32},{64,48},{80,64},{96,80},{112,96},{128,112},... | collective-permute-start | bytes 76208 | tf_op jit(solution)/shard_map/ppermute | solution.py:25
  78.2 7.1 %copy-start.4 = (f32[127,1,128]{2,1,0:T(1,128)S(1)}, f32[127,1,128]{2,1,0:T(1,128)}, u32[]{:S(2)}) copy-start(f32[127,1,128]{2,1,0:T(1,128)} %param.10) | copy-start | bytes 195076
  80.9 16.2 %all-to-all-start.3 = ((f32[32,1,1]{2,1,0:T(1,128)}), f32[32,1,1]{2,1,0:T(1,128)S(1)}, u32[]{:S(2)}, u32[]{:S(2)}) async-start(f32[32,1,1]{2,1,0:T(1,128)} %broadcast_in_dim.19), calls=%async_computation.3 | async-start | bytes 32768 | tf_op jit(solution)/shard_map/all_to_all | solution.py:134
  99.0 9.8 %all-to-all-start.4 = ((f32[16,1,1]{2,1,0:T(1,128)}), f32[16,1,1]{2,1,0:T(1,128)S(1)}, u32[]{:S(2)}, u32[]{:S(2)}) async-start(f32[16,1,1]{2,1,0:T(1,128)} %broadcast_in_dim.20), calls=%async_computation.4 | async-start | bytes 16384 | tf_op jit(solution)/shard_map/all_to_all | solution.py:134

commit v12 on v9

--- a/solution.py
+++ b/solution.py
@@ -86,10 +86,9 @@
     out_ref[...] = base_ref[...] + total_sum.T
 
 
-def lon_pass_add(grid_field, base, kernel_groups, groups):
-    kernel = kernel_groups[:, ::-1]
+def lon_pass_add(grid_field, base, kernels):
+    kernels = kernels[:, ::-1]
     levels, rows, lon_width = grid_field.shape
-    kernels = jnp.repeat(group_rows(groups, kernel), rows, axis=0)
     extended = with_halo(grid_field, (("lon", 2),), HALF)
     filtered = pl.pallas_call(
         lon_add_kernel,
@@ -158,7 +157,7 @@
     back_lat = returned[:LEV]
     lat_sums = jnp.sum(returned[LEV, 0].reshape(-1, chunk)[:, :2], axis=0)
     norm_old, curvature = total((lat_sums[0], lat_sums[1]), ("lon",))
-    applied = lon_pass_add(back_lat, direction, lon_taps, groups)
+    applied = lon_pass_add(back_lat, direction, jnp.repeat(group_rows(groups, lon_taps), direction.shape[1], axis=0))
     step_length = norm_old / curvature
     residual_next = residual - step_length * applied
     (norm_new,) = total((jnp.sum(residual_next * residual_next),))

time: 113 us -> 113 us (level)
    unnamed x22 -> x24, local copies, waits for them, and re-layouts: 4.91 us -> 4.99 us
where the time goes in v12:
time: 113 us; the launch traced here: 112 us
  starting transfers between devices  40.5 us (36%)
  waiting for transfers between devices  30.8 us (27%)
  local copies, waits for them, and re-layouts  10.8 us (10%)
  blocking collectives  9.35 us (8%)
  other arithmetic  9.25 us (8%)
  between operations  4.8 us (4%)
  Pallas kernels  4.14 us (4%)
  matrix products  2.26 us (2%)
    all_to_all x2, starting transfers between devices, total(): lax.all_to_all(jnp.broadcast_to(v[None], (n,) + v.shape), axis, 0, 0, til...  24.7 us
    all_to_all x2, waiting for transfers between devices, total(): lax.all_to_all(jnp.broadcast_to(v[None], (n,) + v.shape), axis, 0, 0, til...  20.5 us
    all_to_all x1, blocking collectives, total(): lax.all_to_all(jnp.broadcast_to(v[None], (n,) + v.shape), axis, 0, 0, til...  9.35 us
    all_to_all x1, waiting for transfers between devices, to_rows(): return lax.all_to_all(grid_field, 'lat', 1, 2, tiled=True)  5.18 us
    all_to_all x1, waiting for transfers between devices, to_columns(): return lax.all_to_all(grid_field, 'lat', 2, 1, tiled=True)  5.05 us
    unnamed x24, local copies, waits for them, and re-layouts  4.99 us
    ppermute x2, starting transfers between devices, with_halo(): lax.ppermute(tail, axis, [(i, (i + 1) % count) for i in range(count)])  4.68 us
    ppermute x2, starting transfers between devices, with_halo(): lax.ppermute(head, axis, [((i + 1) % count, i) for i in range(count)])  3.88 us
  transfers between devices with their start and end apart: 8, of which 4 were waited for; matrix products, arithmetic and copies ran while one was open for 7% of the time, Pallas kernels for 0%

profile of v12, /device:TPU:1, one launch (start us, length us, event | category | flops | bytes accessed | tf_op | source)
XLA Modules:
  0.0 111.9 jit_solution(9114647453284206301)
XLA Ops:
  0.6 1.0 copy.65
  1.6 3.0 %collective-permute-start = (f32[127,1,50]{0,2,1:T(8,128)S(1)}, f32[127,1,50]{0,2,1:T(8,128)S(1)}, u32[]{:S(2)}, u32[]{:S(2)}) collective-permute-start(f32[127,1,50]{0,2,1:T(8,128)S(1)} %get-tuple-element.36), channel_id=1, source_target_pairs={{0,16},{16,32},{32,48},{48,64},{64,80},{80,96},{96,112},{112,128},... | collective-permute-start | bytes 76208 | tf_op jit(solution)/shard_map/ppermute | solution.py:23
  4.7 3.9 %collective-permute-start.1 = (f32[127,1,50]{0,2,1:T(8,128)S(1)}, f32[127,1,50]{0,2,1:T(8,128)S(1)}, u32[]{:S(2)}, u32[]{:S(2)}) collective-permute-start(f32[127,1,50]{0,2,1:T(8,128)S(1)} %get-tuple-element.37), channel_id=1, source_target_pairs={{16,0},{32,16},{48,32},{64,48},{80,64},{96,80},{112,96},{128,112},... | collective-permute-start | bytes 76208 | tf_op jit(solution)/shard_map/ppermute | solution.py:25
  8.6 0.6 copy-done.8
  10.4 0.7 gather_fusion
  11.8 0.9 fusion.1
  12.9 0.7 maximum_bitcast_fusion.extended_ref
  13.5 2.1 %shard_map.103 = f32[128,127]{1,0:T(8,128)} custom-call(f32[101,127]{1,0:T(8,128)} %bitcast.54, f32[228,127]{1,0:T(8,128)} %maximum_bitcast_fusion.extended_ref), custom_call_target="tpu_custom_call" | custom-call | tf_op jit(solution)/shard_map/pallas_call | solution.py:105
  15.6 0.9 pad_maximum_fusion
  16.5 0.8 copy.69
  17.3 3.6 %all-to-all-start = ((f32[254,1,128]{0,1,2:T(1,128)}), f32[254,1,128]{0,1,2:T(1,128)S(1)}, u32[]{:S(2)}, u32[]{:S(2)}) async-start(f32[254,1,128]{0,1,2:T(1,128)} %copy.69), calls=%async_computation | async-start | bytes 262144 | tf_op jit(solution)/shard_map/all_to_all | solution.py:112
  21.0 0.7 multiply_reduce_fusion.4
  21.8 0.7 multiply_reduce_fusion.5
  22.5 5.1 %all-to-all-done = f32[254,1,128]{0,1,2:T(1,128)S(1)} async-done(((f32[254,1,128]{0,1,2:T(1,128)}), f32[254,1,128]{0,1,2:T(1,128)S(1)}, u32[]{:S(2)}, u32[]{:S(2)}) %all-to-all-start) | async-done | bytes 130080 | tf_op jit(solution)/shard_map/all_to_all | solution.py:112
  27.9 0.9 multiply_reduce_fusion.3
  31.1 0.7 pad_maximum_fusion.1
  31.8 3.6 %all-to-all-start.1 = ((f32[128,16,8]{0,2,1:T(8,128)}), f32[128,16,8]{0,2,1:T(8,128)S(1)}, u32[]{:S(2)}, u32[]{:S(2)}) async-start(f32[128,16,8]{0,2,1:T(8,128)} %pad_maximum_fusion.1), calls=%async_computation.1 | async-start | bytes 131072 | tf_op jit(solution)/shard_map/all_to_all | solution.py:116
  36.7 5.2 %all-to-all-done.1 = f32[128,16,8]{0,2,1:T(8,128)S(1)} async-done(((f32[128,16,8]{0,2,1:T(8,128)}), f32[128,16,8]{0,2,1:T(8,128)S(1)}, u32[]{:S(2)}, u32[]{:S(2)}) %all-to-all-start.1) | async-done | bytes 65568 | tf_op jit(solution)/shard_map/all_to_all | solution.py:116
  42.9 18.9 %all-to-all-start.2 = ((f32[32,1,2]{2,1,0:T(1,128)}), f32[32,1,2]{2,1,0:T(1,128)S(1)}, u32[]{:S(2)}, u32[]{:S(2)}) async-start(f32[32,1,2]{2,1,0:T(1,128)} %broadcast_in_dim.18), calls=%async_computation.2 | async-start | bytes 32768 | tf_op jit(solution)/shard_map/all_to_all | solution.py:133
  61.8 1.6 %collective-permute-start.2 = (f32[127,1,50]{0,2,1:T(8,128)S(1)}, f32[127,1,50]{0,2,1:T(8,128)S(1)}, u32[]{:S(2)}, u32[]{:S(2)}) collective-permute-start(f32[127,1,50]{0,2,1:T(8,128)S(1)} %get-tuple-element.34), channel_id=1, source_target_pairs={{0,16},{16,32},{32,48},{48,64},{64,80},{80,96},{96,112},{112,128},... | collective-permute-start | bytes 76208 | tf_op jit(solution)/shard_map/ppermute | solution.py:23
  63.4 10.1 %all-to-all-done.2 = f32[32,1,2]{2,1,0:T(1,128)S(1)} async-done(((f32[32,1,2]{2,1,0:T(1,128)}), f32[32,1,2]{2,1,0:T(1,128)S(1)}, u32[]{:S(2)}, u32[]{:S(2)}) %all-to-all-start.2) | async-done | bytes 288 | tf_op jit(solution)/shard_map/all_to_all | solution.py:133
  75.5 0.7 maximum_bitcast_fusion.1.extended_ref
  76.2 2.1 %shard_map.104 = f32[127,128]{1,0:T(8,128)} custom-call(f32[101,127]{1,0:T(8,128)} %bitcast.58, f32[228,127]{1,0:T(8,128)} %maximum_bitcast_fusion.1.extended_ref, f32[127,128]{1,0:T(8,128)} %bitcast.55), custom_call_target="tpu_custom_call" | custom-call | tf_op jit(solution)/shard_map/pallas_call | solution.py:93
  78.2 1.5 %multiply_reduce_fusion.2 = (f32[]{:T(128)}, f32[127,1,128]{2,0,1:T(8,128)S(1)}) fusion(f32[127,128]{1,0:T(8,128)} %shard_map.104, f32[]{:T(128)S(6)} %div.6, f32[127,1,128]{2,1,0:T(1,128)S(1)} %copy-done.3), kind=kLoop, calls=%fused_computation.14 | loop fusion | flops 65023 | bytes 195080 | tf_op jit(solution)/shard_map/reduce_sum | solution.py:163
  79.7 0.7 broadcast_in_dim.19
  80.4 9.4 %all_to_all.36 = f32[16,1,1]{2,1,0:T(1,128)S(1)} all-to-all(f32[16,1,1]{2,1,0:T(1,128)S(1)} %broadcast_in_dim.19), channel_id=1, replica_groups=mesh['lon'=32,'lat'=16] {'lat'}, dimensions={0} | all-to-all | bytes 128 | tf_op jit(solution)/shard_map/all_to_all | solution.py:133
  90.3 1.3 %broadcast_in_dim.20 = f32[32,1,1]{2,1,0:T(1,128)} broadcast(f32[]{:T(128)} %reduce_sum.108), dimensions={} | broadcast | bytes 132 | tf_op jit(solution)/shard_map/broadcast_in_dim | solution.py:133
  91.6 5.8 %all-to-all-start.4 = ((f32[32,1,1]{2,1,0:T(1,128)}), f32[32,1,1]{2,1,0:T(1,128)S(1)}, u32[]{:S(2)}, u32[]{:S(2)}) async-start(f32[32,1,1]{2,1,0:T(1,128)} %broadcast_in_dim.20), calls=%async_computation.4 | async-start | bytes 32768 | tf_op jit(solution)/shard_map/all_to_all | solution.py:133
  97.4 0.7 multiply_add_fusion.1
  98.1 0.7 copy.77
  98.8 10.4 %all-to-all-done.4 = f32[32,1,1]{2,1,0:T(1,128)S(1)} async-done(((f32[32,1,1]{2,1,0:T(1,128)}), f32[32,1,1]{2,1,0:T(1,128)S(1)}, u32[]{:S(2)}, u32[]{:S(2)}) %all-to-all-start.4) | async-done | bytes 160 | tf_op jit(solution)/shard_map/all_to_all | solution.py:133
  111.2 0.7 copy.78
  (53 shorter events, 7.6 us)
Async XLA Ops:
  0.6 27.3 %copy-start = (f32[127,127]{1,0:T(8,128)S(1)}, f32[127,127]{1,0:T(8,128)}, u32[]{:S(2)}) copy-start(f32[127,127]{1,0:T(8,128)} %param.14) | copy-start | bytes 193552
  1.6 11.2 %collective-permute-start = (f32[127,1,50]{0,2,1:T(8,128)S(1)}, f32[127,1,50]{0,2,1:T(8,128)S(1)}, u32[]{:S(2)}, u32[]{:S(2)}) collective-permute-start(f32[127,1,50]{0,2,1:T(8,128)S(1)} %get-tuple-element.36), channel_id=1, source_target_pairs={{0,16},{16,32},{32,48},{48,64},{64,80},{80,96},{96,112},{112,128},... | collective-permute-start | bytes 76208 | tf_op jit(solution)/shard_map/ppermute | solution.py:23
  4.7 8.2 %collective-permute-start.1 = (f32[127,1,50]{0,2,1:T(8,128)S(1)}, f32[127,1,50]{0,2,1:T(8,128)S(1)}, u32[]{:S(2)}, u32[]{:S(2)}) collective-permute-start(f32[127,1,50]{0,2,1:T(8,128)S(1)} %get-tuple-element.37), channel_id=1, source_target_pairs={{16,0},{32,16},{48,32},{64,48},{80,64},{96,80},{112,96},{128,112},... | collective-permute-start | bytes 76208 | tf_op jit(solution)/shard_map/ppermute | solution.py:25
  8.6 0.7 copy-start.8
  9.4 0.7 copy-start.6
  11.1 0.7 copy-start.7
  11.8 0.9 copy-start.5
  17.3 3.7 %copy-start.1 = (f32[127,1,128]{2,1,0:T(1,128)S(1)}, f32[127,1,128]{2,1,0:T(1,128)}, u32[]{:S(2)}) copy-start(f32[127,1,128]{2,1,0:T(1,128)} %param.12) | copy-start | bytes 195076
  17.3 10.3 %all-to-all-start = ((f32[254,1,128]{0,1,2:T(1,128)}), f32[254,1,128]{0,1,2:T(1,128)S(1)}, u32[]{:S(2)}, u32[]{:S(2)}) async-start(f32[254,1,128]{0,1,2:T(1,128)} %copy.69), calls=%async_computation | async-start | bytes 262144 | tf_op jit(solution)/shard_map/all_to_all | solution.py:112
  21.0 0.8 copy-start.3
  31.8 3.6 %copy-start.2 = (f32[127,101]{0,1:T(8,128)S(1)}, f32[127,101]{0,1:T(8,128)}, u32[]{:S(2)}) copy-start(f32[127,101]{0,1:T(8,128)} %fusion.1) | copy-start | bytes 153928
  31.8 10.1 %all-to-all-start.1 = ((f32[128,16,8]{0,2,1:T(8,128)}), f32[128,16,8]{0,2,1:T(8,128)S(1)}, u32[]{:S(2)}, u32[]{:S(2)}) async-start(f32[128,16,8]{0,2,1:T(8,128)} %pad_maximum_fusion.1), calls=%async_computation.1 | async-start | bytes 131072 | tf_op jit(solution)/shard_map/all_to_all | solution.py:116
  42.9 30.7 %all-to-all-start.2 = ((f32[32,1,2]{2,1,0:T(1,128)}), f32[32,1,2]{2,1,0:T(1,128)S(1)}, u32[]{:S(2)}, u32[]{:S(2)}) async-start(f32[32,1,2]{2,1,0:T(1,128)} %broadcast_in_dim.18), calls=%async_computation.2 | async-start | bytes 32768 | tf_op jit(solution)/shard_map/all_to_all | solution.py:133
  61.8 13.7 %collective-permute-start.2 = (f32[127,1,50]{0,2,1:T(8,128)S(1)}, f32[127,1,50]{0,2,1:T(8,128)S(1)}, u32[]{:S(2)}, u32[]{:S(2)}) collective-permute-start(f32[127,1,50]{0,2,1:T(8,128)S(1)} %get-tuple-element.34), channel_id=1, source_target_pairs={{0,16},{16,32},{32,48},{48,64},{64,80},{80,96},{96,112},{112,128},... | collective-permute-start | bytes 76208 | tf_op jit(solution)/shard_map/ppermute | solution.py:23
  63.4 12.1 %collective-permute-start.3 = (f32[127,1,50]{0,2,1:T(8,128)S(1)}, f32[127,1,50]{0,2,1:T(8,128)S(1)}, u32[]{:S(2)}, u32[]{:S(2)}) collective-permute-start(f32[127,1,50]{0,2,1:T(8,128)S(1)} %get-tuple-element.35), channel_id=1, source_target_pairs={{16,0},{32,16},{48,32},{64,48},{80,64},{96,80},{112,96},{128,112},... | collective-permute-start | bytes 76208 | tf_op jit(solution)/shard_map/ppermute | solution.py:25
  79.7 17.7 %copy-start.4 = (f32[127,1,128]{2,1,0:T(1,128)S(1)}, f32[127,1,128]{2,1,0:T(1,128)}, u32[]{:S(2)}) copy-start(f32[127,1,128]{2,1,0:T(1,128)} %param.10) | copy-start | bytes 195076
  91.6 17.6 %all-to-all-start.4 = ((f32[32,1,1]{2,1,0:T(1,128)}), f32[32,1,1]{2,1,0:T(1,128)S(1)}, u32[]{:S(2)}, u32[]{:S(2)}) async-start(f32[32,1,1]{2,1,0:T(1,128)} %broadcast_in_dim.20), calls=%async_computation.4 | async-start | bytes 32768 | tf_op jit(solution)/shard_map/all_to_all | solution.py:133

commit v13 on v9

--- a/solution.py
+++ b/solution.py
@@ -2,6 +2,7 @@
 import jax.numpy as jnp
 from jax import lax
 from jax.experimental import pallas as pl
+from jax.experimental.pallas import tpu as pltpu
 from jax.sharding import PartitionSpec as P
 
 LEV = 127
@@ -136,6 +137,11 @@
     return tuple(v[i] for i in range(len(vals)))
 
 
+def update_kernel(scales_ref, iterate_ref, residual_ref, direction_ref, iterate_out, direction_out):
+    iterate_out[...] = iterate_ref[...] + scales_ref[0, 0] * direction_ref[...]
+    direction_out[...] = residual_ref[...] + scales_ref[0, 1] * direction_ref[...]
+
+
 def local(iterate, residual, direction, obs_weight, vertical, lon_taps, lat_taps, band_sizes):
     bounds = jnp.cumsum(band_sizes)
     levels = jnp.arange(LEV, dtype=jnp.int32)
@@ -162,8 +168,15 @@
     step_length = norm_old / curvature
     residual_next = residual - step_length * applied
     (norm_new,) = total((jnp.sum(residual_next * residual_next),))
-    iterate_next = iterate + step_length * direction
-    direction_next = residual_next + norm_new / norm_old * direction
+    scales = jnp.stack([step_length, norm_new / norm_old]).reshape(1, 2)
+    iterate_next, direction_next = pl.pallas_call(
+        update_kernel,
+        out_shape=(
+            jax.ShapeDtypeStruct(iterate.shape, iterate.dtype),
+            jax.ShapeDtypeStruct(direction.shape, direction.dtype),
+        ),
+        in_specs=[pl.BlockSpec(memory_space=pltpu.SMEM)] + [pl.BlockSpec()] * 3,
+    )(scales, iterate, residual_next, direction)
     return (iterate_next, residual_next, direction_next)
 
 

time: 113 us -> 114 us (level)
  blocking collectives: 9.35 us -> 26.2 us
  waiting for transfers between devices: 30.5 us -> 20.1 us
  starting transfers between devices: 40.4 us -> 34.6 us
  local copies, waits for them, and re-layouts: 10.2 us -> 8.16 us
  Pallas kernels: 4.14 us -> 5.83 us
    all_to_all x1 -> x2, blocking collectives: 9.35 us -> 26.2 us  [total(): lax.all_to_all(jnp.broadcast_to(v[None], (n,) + v.shape), axis, 0, 0, til...]
    all_to_all x2 -> x1, waiting for transfers between devices: 20.5 us -> 10.1 us  [total(): lax.all_to_all(jnp.broadcast_to(v[None], (n,) + v.shape), axis, 0, 0, til...]
    all_to_all x2 -> x1, starting transfers between devices: 24.7 us -> 18.9 us  [total(): lax.all_to_all(jnp.broadcast_to(v[None], (n,) + v.shape), axis, 0, 0, til...]
    pallas_call x0 -> x1, Pallas kernels: none -> 1.69 us  [local(): pl.pallas_call(update_kernel, out_shape=(jax.ShapeDtypeStruct(iterate.sha...]
    unnamed x22 -> x18, local copies, waits for them, and re-layouts: 4.91 us -> 3.52 us
  transfers between devices with their start and end apart: 8 -> 7, of which waited for: 4 -> 3; matrix products, arithmetic and copies ran while one was open for 7% -> 6% of each run, Pallas kernels for 0% -> 0%
where the time goes in v13:
time: 114 us; the launch traced here: 113 us
  starting transfers between devices  34.6 us (30%)
  blocking collectives  26.2 us (23%)
  waiting for transfers between devices  20.1 us (18%)
  other arithmetic  9.98 us (9%)
  local copies, waits for them, and re-layouts  8.16 us (7%)
  Pallas kernels  5.83 us (5%)
  between operations  4.77 us (4%)
  matrix products  3.17 us (3%)
    all_to_all x2, blocking collectives, total(): lax.all_to_all(jnp.broadcast_to(v[None], (n,) + v.shape), axis, 0, 0, til...  26.2 us
    all_to_all x1, starting transfers between devices, total(): lax.all_to_all(jnp.broadcast_to(v[None], (n,) + v.shape), axis, 0, 0, til...  18.9 us
    all_to_all x1, waiting for transfers between devices, total(): lax.all_to_all(jnp.broadcast_to(v[None], (n,) + v.shape), axis, 0, 0, til...  10.1 us
    all_to_all x1, waiting for transfers between devices, to_columns(): return lax.all_to_all(grid_field, 'lat', 2, 1, tiled=True)  5.05 us
    all_to_all x1, waiting for transfers between devices, to_rows(): return lax.all_to_all(grid_field, 'lat', 1, 2, tiled=True)  4.92 us
    ppermute x2, starting transfers between devices, with_halo(): lax.ppermute(tail, axis, [(i, (i + 1) % count) for i in range(count)])  4.68 us
    ppermute x2, starting transfers between devices, with_halo(): lax.ppermute(head, axis, [((i + 1) % count, i) for i in range(count)])  3.88 us
    all_to_all x1, starting transfers between devices, to_columns(): return lax.all_to_all(grid_field, 'lat', 2, 1, tiled=True)  3.64 us
  transfers between devices with their start and end apart: 7, of which 3 were waited for; matrix products, arithmetic and copies ran while one was open for 6% of the time, Pallas kernels for 0%

profile of v13, /device:TPU:1, one launch (start us, length us, event | category | flops | bytes accessed | tf_op | source)
XLA Modules:
  0.0 112.8 jit_solution(6371411163781536243)
XLA Ops:
  0.6 1.0 copy.49
  1.6 3.0 %collective-permute-start = (f32[127,1,50]{0,2,1:T(8,128)S(1)}, f32[127,1,50]{0,2,1:T(8,128)S(1)}, u32[]{:S(2)}, u32[]{:S(2)}) collective-permute-start(f32[127,1,50]{0,2,1:T(8,128)S(1)} %get-tuple-element.25), channel_id=1, source_target_pairs={{0,16},{16,32},{32,48},{48,64},{64,80},{80,96},{96,112},{112,128},... | collective-permute-start | bytes 76208 | tf_op jit(solution)/shard_map/ppermute | solution.py:24
  4.7 3.9 %collective-permute-start.1 = (f32[127,1,50]{0,2,1:T(8,128)S(1)}, f32[127,1,50]{0,2,1:T(8,128)S(1)}, u32[]{:S(2)}, u32[]{:S(2)}) collective-permute-start(f32[127,1,50]{0,2,1:T(8,128)S(1)} %get-tuple-element.26), channel_id=1, source_target_pairs={{16,0},{32,16},{48,32},{64,48},{80,64},{96,80},{112,96},{128,112},... | collective-permute-start | bytes 76208 | tf_op jit(solution)/shard_map/ppermute | solution.py:26
  10.4 0.7 gather_fusion
  11.8 0.9 convolution_bitcast_fusion.3.taps_ref
  12.9 0.7 maximum_bitcast_fusion.extended_ref
  13.5 2.1 %shard_map.103 = f32[128,127]{1,0:T(8,128)} custom-call(f32[101,127]{1,0:T(8,128)} %convolution_bitcast_fusion.3.taps_ref, f32[228,127]{1,0:T(8,128)} %maximum_bitcast_fusion.extended_ref), custom_call_target="tpu_custom_call" | custom-call | tf_op jit(solution)/shard_map/pallas_call | solution.py:107
  15.6 0.9 pad_maximum_fusion
  16.5 0.8 copy.53
  17.3 3.6 %all-to-all-start = ((f32[254,1,128]{0,1,2:T(1,128)}), f32[254,1,128]{0,1,2:T(1,128)S(1)}, u32[]{:S(2)}, u32[]{:S(2)}) async-start(f32[254,1,128]{0,1,2:T(1,128)} %copy.53), calls=%async_computation | async-start | bytes 262144 | tf_op jit(solution)/shard_map/all_to_all | solution.py:114
  21.0 0.7 multiply_reduce_fusion.4
  21.8 0.7 multiply_reduce_fusion.5
  22.5 5.0 %all-to-all-done = f32[254,1,128]{0,1,2:T(1,128)S(1)} async-done(((f32[254,1,128]{0,1,2:T(1,128)}), f32[254,1,128]{0,1,2:T(1,128)S(1)}, u32[]{:S(2)}, u32[]{:S(2)}) %all-to-all-start) | async-done | bytes 130080 | tf_op jit(solution)/shard_map/all_to_all | solution.py:114
  27.9 0.9 multiply_reduce_fusion.2
  30.4 0.7 fusion.9
  31.2 0.7 pad_maximum_fusion.1
  31.9 3.5 %all-to-all-start.1 = ((f32[128,16,8]{0,2,1:T(8,128)}), f32[128,16,8]{0,2,1:T(8,128)S(1)}, u32[]{:S(2)}, u32[]{:S(2)}) async-start(f32[128,16,8]{0,2,1:T(8,128)} %pad_maximum_fusion.1), calls=%async_computation.1 | async-start | bytes 131072 | tf_op jit(solution)/shard_map/all_to_all | solution.py:118
  35.4 0.9 convolution_bitcast_fusion.2.taps_ref
  37.0 4.9 %all-to-all-done.1 = f32[128,16,8]{0,2,1:T(8,128)S(1)} async-done(((f32[128,16,8]{0,2,1:T(8,128)}), f32[128,16,8]{0,2,1:T(8,128)S(1)}, u32[]{:S(2)}, u32[]{:S(2)}) %all-to-all-start.1) | async-done | bytes 65568 | tf_op jit(solution)/shard_map/all_to_all | solution.py:118
  42.8 18.9 %all-to-all-start.2 = ((f32[32,1,2]{2,1,0:T(1,128)}), f32[32,1,2]{2,1,0:T(1,128)S(1)}, u32[]{:S(2)}, u32[]{:S(2)}) async-start(f32[32,1,2]{2,1,0:T(1,128)} %broadcast_in_dim.18), calls=%async_computation.2 | async-start | bytes 32768 | tf_op jit(solution)/shard_map/all_to_all | solution.py:135
  61.7 1.6 %collective-permute-start.2 = (f32[127,1,50]{0,2,1:T(8,128)S(1)}, f32[127,1,50]{0,2,1:T(8,128)S(1)}, u32[]{:S(2)}, u32[]{:S(2)}) collective-permute-start(f32[127,1,50]{0,2,1:T(8,128)S(1)} %get-tuple-element.23), channel_id=1, source_target_pairs={{0,16},{16,32},{32,48},{48,64},{64,80},{80,96},{96,112},{112,128},... | collective-permute-start | bytes 76208 | tf_op jit(solution)/shard_map/ppermute | solution.py:24
  63.4 10.1 %all-to-all-done.2 = f32[32,1,2]{2,1,0:T(1,128)S(1)} async-done(((f32[32,1,2]{2,1,0:T(1,128)}), f32[32,1,2]{2,1,0:T(1,128)S(1)}, u32[]{:S(2)}, u32[]{:S(2)}) %all-to-all-start.2) | async-done | bytes 288 | tf_op jit(solution)/shard_map/all_to_all | solution.py:135
  75.5 0.7 maximum_bitcast_fusion.1.extended_ref
  76.1 2.1 %shard_map.104 = f32[127,128]{1,0:T(8,128)} custom-call(f32[101,127]{1,0:T(8,128)} %convolution_bitcast_fusion.2.taps_ref, f32[228,127]{1,0:T(8,128)} %maximum_bitcast_fusion.1.extended_ref, f32[127,128]{1,0:T(8,128)} %bitcast.58), custom_call_target="tpu_custom_call" | custom-call | tf_op jit(solution)/shard_map/pallas_call | solution.py:95
  78.2 0.8 broadcast_multiply_fusion
  79.0 1.3 %multiply_reduce_fusion.3 = (f32[]{:T(128)}, f32[127,1,128]{2,1,0:T(1,128)}) fusion(f32[127,1,128]{2,1,0:T(1,128)S(1)} %copy-done.2, f32[127,128]{1,0:T(8,128)S(1)} %broadcast_multiply_fusion), kind=kLoop, calls=%fused_computation.18 | loop fusion | flops 48767 | bytes 195076 | tf_op jit(solution)/shard_map/reduce_sum | solution.py:170
  80.3 0.6 broadcast_in_dim.19
  81.0 9.4 %all_to_all.36 = f32[16,1,1]{2,1,0:T(1,128)S(1)} all-to-all(f32[16,1,1]{2,1,0:T(1,128)S(1)} %broadcast_in_dim.19), channel_id=1, replica_groups=mesh['lon'=32,'lat'=16] {'lat'}, dimensions={0} | all-to-all | bytes 128 | tf_op jit(solution)/shard_map/all_to_all | solution.py:135
  91.0 0.7 broadcast_in_dim.20
  91.6 16.8 %all_to_all.37 = f32[32,1,1]{2,1,0:T(1,128)S(1)} all-to-all(f32[32,1,1]{2,1,0:T(1,128)S(1)} %broadcast_in_dim.20), channel_id=1, replica_groups=mesh['lon'=32,'lat'=16] {'lon'}, dimensions={0} | all-to-all | bytes 256 | tf_op jit(solution)/shard_map/all_to_all | solution.py:135
  110.4 0.7 maximum_bitcast_fusion.2.scales_ref
  111.1 1.7 %shard_map.105 = (f32[127,1,128]{2,1,0:T(1,128)}, f32[127,1,128]{2,1,0:T(1,128)}) custom-call(f32[1,2]{1,0:T(1,128)} %maximum_bitcast_fusion.2.scales_ref, f32[127,1,128]{2,1,0:T(1,128)} %iterate_ref.1, f32[127,1,128]{2,1,0:T(1,128)} %get-tuple-element.20.residual_ref, f32[127,1,128]{2,1,0:T(1,128)} %direction_ref.1), custom_call_target="tpu_custom_call" | custom-call | tf_op jit(solution)/shard_map/pallas_call | solution.py:172
  (48 shorter events, 6.9 us)
Async XLA Ops:
  0.6 27.3 %copy-start = (f32[127,127]{1,0:T(8,128)S(1)}, f32[127,127]{1,0:T(8,128)}, u32[]{:S(2)}) copy-start(f32[127,127]{1,0:T(8,128)} %param.14) | copy-start | bytes 193552
  1.6 11.2 %collective-permute-start = (f32[127,1,50]{0,2,1:T(8,128)S(1)}, f32[127,1,50]{0,2,1:T(8,128)S(1)}, u32[]{:S(2)}, u32[]{:S(2)}) collective-permute-start(f32[127,1,50]{0,2,1:T(8,128)S(1)} %get-tuple-element.25), channel_id=1, source_target_pairs={{0,16},{16,32},{32,48},{48,64},{64,80},{80,96},{96,112},{112,128},... | collective-permute-start | bytes 76208 | tf_op jit(solution)/shard_map/ppermute | solution.py:24
  4.7 8.2 %collective-permute-start.1 = (f32[127,1,50]{0,2,1:T(8,128)S(1)}, f32[127,1,50]{0,2,1:T(8,128)S(1)}, u32[]{:S(2)}, u32[]{:S(2)}) collective-permute-start(f32[127,1,50]{0,2,1:T(8,128)S(1)} %get-tuple-element.26), channel_id=1, source_target_pairs={{16,0},{32,16},{48,32},{64,48},{80,64},{96,80},{112,96},{128,112},... | collective-permute-start | bytes 76208 | tf_op jit(solution)/shard_map/ppermute | solution.py:26
  8.6 0.7 copy-start.6
  9.4 0.7 copy-start.5
  11.1 0.7 copy-start.3
  11.8 0.9 copy-start.4
  17.3 3.7 %copy-start.1 = (f32[127,1,128]{2,1,0:T(1,128)S(1)}, f32[127,1,128]{2,1,0:T(1,128)}, u32[]{:S(2)}) copy-start(f32[127,1,128]{2,1,0:T(1,128)} %direction_ref.1) | copy-start | bytes 195076
  17.3 10.3 %all-to-all-start = ((f32[254,1,128]{0,1,2:T(1,128)}), f32[254,1,128]{0,1,2:T(1,128)S(1)}, u32[]{:S(2)}, u32[]{:S(2)}) async-start(f32[254,1,128]{0,1,2:T(1,128)} %copy.53), calls=%async_computation | async-start | bytes 262144 | tf_op jit(solution)/shard_map/all_to_all | solution.py:114
  21.0 0.8 copy-start.2
  31.9 10.0 %all-to-all-start.1 = ((f32[128,16,8]{0,2,1:T(8,128)}), f32[128,16,8]{0,2,1:T(8,128)S(1)}, u32[]{:S(2)}, u32[]{:S(2)}) async-start(f32[128,16,8]{0,2,1:T(8,128)} %pad_maximum_fusion.1), calls=%async_computation.1 | async-start | bytes 131072 | tf_op jit(solution)/shard_map/all_to_all | solution.py:118
  42.8 30.7 %all-to-all-start.2 = ((f32[32,1,2]{2,1,0:T(1,128)}), f32[32,1,2]{2,1,0:T(1,128)S(1)}, u32[]{:S(2)}, u32[]{:S(2)}) async-start(f32[32,1,2]{2,1,0:T(1,128)} %broadcast_in_dim.18), calls=%async_computation.2 | async-start | bytes 32768 | tf_op jit(solution)/shard_map/all_to_all | solution.py:135
  61.7 13.7 %collective-permute-start.2 = (f32[127,1,50]{0,2,1:T(8,128)S(1)}, f32[127,1,50]{0,2,1:T(8,128)S(1)}, u32[]{:S(2)}, u32[]{:S(2)}) collective-permute-start(f32[127,1,50]{0,2,1:T(8,128)S(1)} %get-tuple-element.23), channel_id=1, source_target_pairs={{0,16},{16,32},{32,48},{48,64},{64,80},{80,96},{96,112},{112,128},... | collective-permute-start | bytes 76208 | tf_op jit(solution)/shard_map/ppermute | solution.py:24
  63.4 12.1 %collective-permute-start.3 = (f32[127,1,50]{0,2,1:T(8,128)S(1)}, f32[127,1,50]{0,2,1:T(8,128)S(1)}, u32[]{:S(2)}, u32[]{:S(2)}) collective-permute-start(f32[127,1,50]{0,2,1:T(8,128)S(1)} %get-tuple-element.24), channel_id=1, source_target_pairs={{16,0},{32,16},{48,32},{64,48},{80,64},{96,80},{112,96},{128,112},... | collective-permute-start | bytes 76208 | tf_op jit(solution)/shard_map/ppermute | solution.py:26
